TPU v7x, 768 devices: a whole 4x8x12 slice. The times are simulated.
768 devices in a mesh: tm: 8 (over x, core), height: 96 (over z, y).
Axes of the slice: x: 4, y: 8, z: 12, core: 2. Of those that a mesh axis runs over, the one named last changes fastest.
Arguments:
- clip: bfloat16 [16, 384, 64, 256], P('tm', 'height'), may hold values from -6 to 6
- cotangent: bfloat16 [16, 384, 64, 256], P('tm', 'height'), may hold values from -6 to 6
- spatial_weight: bfloat16 [3, 3, 256, 256], replicated, may hold values from -0.125 to 0.125
- temporal_weight: bfloat16 [3, 256, 256], replicated, may hold values from -0.21875 to 0.21875
Outputs:
- output: bfloat16 [16, 384, 64, 256], P('tm', 'height')
- grad_clip: bfloat16 [16, 384, 64, 256], P('tm', 'height')
- grad_spatial: float32 [589824], P(('tm', 'height'))
- grad_temporal: float32 [196608], P(('tm', 'height'))
All inputs are finite; a program needn't handle non-finite values.
Results may differ from a plain program's by a relative error of at most 0.0049.
Values may be sent and summed in bfloat16 or wider, within the bound.
No kernel may reach another device: no remote copies, remote signals or barrier semaphores. Data moves between devices by JAX's collectives and lax.ppermute only.
A program may use at most 32 MiB of HBM per device.

v0:
```python
import math

import jax
import jax.numpy as jnp
from jax import lax
from jax.sharding import PartitionSpec as P

EPSILON = 1e-06


def extended(cells, sides, width):
    for axis, dim in sides:
        count = lax.axis_size(axis)
        ends = count - 1
        head = lax.slice_in_dim(cells, 0, width, axis=dim)
        tail = lax.slice_in_dim(cells, cells.shape[dim] - width, cells.shape[dim], axis=dim)
        cells = jnp.concatenate(
            [
                lax.ppermute(tail, axis, [(i, (i + 1) % count) for i in range(ends)]),
                cells,
                lax.ppermute(head, axis, [((i + 1) % count, i) for i in range(ends)]),
            ],
            axis=dim,
        )
    return cells


def shifted(block, axis, distance):
    devices = range(lax.axis_size(axis))
    route = [(i - distance, i) for i in devices if i - distance in devices]
    return lax.ppermute(block, axis, route)


def activate(values):
    scale_inv = lax.rsqrt(jnp.mean(values * values, axis=-1, keepdims=True) + EPSILON)
    return jax.nn.silu(values * scale_inv)


def flat_dot(left, weight):
    keep_shape = left.shape[:-1]
    result = jnp.dot(left.reshape(-1, left.shape[-1]), weight, preferred_element_type=jnp.float32)
    return result.reshape(keep_shape + (weight.shape[-1],))


def outer_sum(left, right):
    channels = left.shape[-1]
    return lax.dot_general(
        left.reshape(-1, channels),
        right.reshape(-1, channels),
        (((0,), (0,)), ((), ())),
        preferred_element_type=jnp.float32,
    )


def shards(clip, cotangent, spatial_weight, temporal_weight):
    frame_count, row_count, col_count, channels = clip.shape
    clip_wide = clip.astype(jnp.float32)
    activated = activate(clip_wide).astype(jnp.bfloat16)
    act_ext = extended(activated, (("height", 1),), 1)
    padded = jnp.pad(act_ext, ((0, 0), (0, 0), (1, 1), (0, 0)))
    spatial = jnp.zeros(clip.shape, jnp.float32)
    for tap_row in range(3):
        for tap_col in range(3):
            spatial = spatial + flat_dot(
                padded[:, tap_row : tap_row + row_count, tap_col : tap_col + col_count],
                spatial_weight[tap_row, tap_col],
            )
    middle = spatial.astype(jnp.bfloat16)
    earlier = shifted(middle, "tm", 1)
    history = jnp.concatenate([earlier, middle], axis=0)
    temporal = jnp.zeros(clip.shape, jnp.float32)
    for time_lag in range(3):
        temporal = temporal + flat_dot(
            history[2 - time_lag : 2 - time_lag + frame_count], temporal_weight[time_lag]
        )
    output = (clip_wide + temporal).astype(jnp.bfloat16)
    later = shifted(cotangent, "tm", -1)
    future = jnp.concatenate([cotangent, later], axis=0)
    grad_wide = jnp.zeros(clip.shape, jnp.float32)
    for time_lag in range(3):
        grad_wide = grad_wide + flat_dot(
            future[time_lag : time_lag + frame_count], temporal_weight[time_lag].T
        )
    grad_mid = grad_wide.astype(jnp.bfloat16)
    grad_temporal = jnp.stack(
        [
            outer_sum(history[2 - time_lag : 2 - time_lag + frame_count], cotangent)
            for time_lag in range(3)
        ]
    )
    grad_ext = extended(grad_mid, (("height", 1),), 1)
    grad_pad = jnp.pad(grad_ext, ((0, 0), (0, 0), (1, 1), (0, 0)))
    terms = []
    for tap_row in range(3):
        for tap_col in range(3):
            terms.append(
                outer_sum(
                    padded[:, tap_row : tap_row + row_count, tap_col : tap_col + col_count],
                    grad_mid,
                )
            )
    grad_spatial = jnp.stack(terms)
    grad_act = jnp.zeros(clip.shape, jnp.float32)
    for tap_row in range(3):
        for tap_col in range(3):
            grad_act = grad_act + flat_dot(
                grad_pad[
                    :, 2 - tap_row : 2 - tap_row + row_count, 2 - tap_col : 2 - tap_col + col_count
                ],
                spatial_weight[tap_row, tap_col].T,
            )
    unused, pullback = jax.vjp(activate, clip_wide)
    grad_clip = (cotangent.astype(jnp.float32) + pullback(grad_act)[0]).astype(jnp.bfloat16)
    time_shards = lax.axis_size("tm")
    row_shards = lax.axis_size("height")
    grad_scale = 1.0 / math.sqrt(frame_count * time_shards * row_count * row_shards * col_count)
    flat_spatial = (grad_spatial * grad_scale).reshape(-1)
    flat_temporal = (grad_temporal * grad_scale).reshape(-1)
    spatial_part, temporal_part = (
        lax.psum_scatter(flat_spatial, ("tm", "height"), scatter_dimension=0, tiled=True),
        lax.psum_scatter(flat_temporal, ("tm", "height"), scatter_dimension=0, tiled=True),
    )
    return (output, grad_clip, spatial_part, temporal_part)


def solution(mesh):
    return jax.shard_map(
        shards,
        mesh=mesh,
        in_specs=(P("tm", "height", None, None), P("tm", "height", None, None), P(), P()),
        out_specs=(
            P("tm", "height", None, None),
            P("tm", "height", None, None),
            P(("tm", "height")),
            P(("tm", "height")),
        ),
        check_vma=False,
    )
```

profile of v0, /device:TPU:6, one launch (start us, length us, event | category | flops | bytes accessed | tf_op | source)
XLA Modules:
  0.0 556.8 jit_solution(17456396553843592235)
XLA Ops:
  7.2 2.3 collective-permute-start.3
  9.6 1.1 fusion.29
  10.6 1.2 fusion.87
  11.9 1.8 collective-permute-done.3
  14.3 1.4 collective-permute-start.5
  15.7 4.5 collective-permute-start.4
  20.3 0.3 collective-permute-done.5
  20.6 1.6 collective-permute-done.4
  24.5 0.4 copy-done.2
  24.9 0.5 fusion.30
  25.4 1.0 fusion.28
  26.5 1.3 collective-permute-start.1
  27.8 4.9 collective-permute-start
  32.7 0.3 collective-permute-done.1
  33.0 1.6 collective-permute-done
  37.1 1.9 collective-permute-start.2
  40.1 0.3 fusion.12
  41.5 2.6 copy.32
  44.4 0.4 collective-permute-done.2
  45.4 1.3 copy.33
  47.2 0.9 fusion.5
  48.1 499.2 %all-reduce.7.cloned.1.call-done = (f32[589824]{0:T(1024)}, f32[196608]{0:T(1024)}) async-done(((f32[589824]{0:T(1024)}, f32[196608]{0:T(1024)}), (f32[589824]{0:T(1024)}, f32[196608]{0:T(1024)})) %all-reduce.7.cloned.1.call-update) | async-done | bytes 3145744
  547.3 1.4 dynamic-slice
  548.6 1.3 dynamic-slice.1
  (49 shorter events, 8.7 us)
Async XLA Ops:
  7.2 6.8 %copy-start.1 = (bf16[2,4,64,256]{3,2,1,0:T(8,128)(2,1)S(1)}, bf16[2,4,64,256]{3,2,1,0:T(8,128)(2,1)}, u32[]{:S(2)}) copy-start(bf16[2,4,64,256]{3,2,1,0:T(8,128)(2,1)} %param.5) | copy-start | bytes 786436
  7.2 6.6 %copy-start.3 = (bf16[3,256,256]{2,1,0:T(8,128)(2,1)S(1)}, bf16[3,256,256]{2,1,0:T(8,128)(2,1)}, u32[]{:S(2)}) copy-start(bf16[3,256,256]{2,1,0:T(8,128)(2,1)} %param.7) | copy-start | bytes 1179652
  7.2 540.1 %all-reduce.7.cloned.1.call-start = ((), (), s32[]{:S(2)}) async-start(), calls=%async_computation | async-start | bytes 6291456
  7.2 6.5 %collective-permute-start.3 = (bf16[2,4,64,256]{3,2,1,0:T(8,128)(2,1)}, bf16[2,4,64,256]{3,2,1,0:T(8,128)(2,1)S(1)}, u32[]{:S(2)}, u32[]{:S(2)}) collective-permute-start(bf16[2,4,64,256]{3,2,1,0:T(8,128)(2,1)} %param.5), channel_id=1, source_target_pairs={{96,0},{192,96},{288,192},{384,288},{480,384},{576,480},{672,576},... | collective-permute-start | bytes 786440 | tf_op jit(solution)/shard_map/ppermute | solution.py:31
  14.0 8.3 %copy-start = (bf16[3,3,256,256]{3,2,1,0:T(8,128)(2,1)S(1)}, bf16[3,3,256,256]{3,2,1,0:T(8,128)(2,1)}, u32[]{:S(2)}) copy-start(bf16[3,3,256,256]{3,2,1,0:T(8,128)(2,1)} %param.6) | copy-start | bytes 3538948
  14.3 6.3 %collective-permute-start.5 = (bf16[2,1,64,256]{3,2,1,0:T(8,128)(2,1)S(1)}, bf16[2,1,64,256]{3,2,1,0:T(8,128)(2,1)S(1)}, u32[]{:S(2)}, u32[]{:S(2)}) collective-permute-start(bf16[2,1,64,256]{3,2,1,0:T(8,128)(2,1)S(1)} %get-tuple-element.9), channel_id=1, source_target_pairs={{1,0},{2,1},{3,2},{4,3},{5,4},{6,5},{7,6},{8,7},{9,8},{10,9},{11,1... | collective-permute-start | bytes 196616 | tf_op jit(solution)/shard_map/ppermute | solution.py:21
  15.7 6.4 %collective-permute-start.4 = (bf16[2,1,64,256]{3,2,1,0:T(8,128)(2,1)S(1)}, bf16[2,1,64,256]{3,2,1,0:T(8,128)(2,1)S(1)}, u32[]{:S(2)}, u32[]{:S(2)}) collective-permute-start(bf16[2,1,64,256]{3,2,1,0:T(8,128)(2,1)S(1)} %get-tuple-element.8), channel_id=1, source_target_pairs={{0,1},{1,2},{2,3},{3,4},{4,5},{5,6},{6,7},{7,8},{8,9},{9,10},{10,1... | collective-permute-start | bytes 196616 | tf_op jit(solution)/shard_map/ppermute | solution.py:19
  23.9 1.0 copy-start.2
  26.5 6.5 %collective-permute-start.1 = (bf16[2,1,64,256]{3,2,1,0:T(8,128)(2,1)S(1)}, bf16[2,1,64,256]{3,2,1,0:T(8,128)(2,1)S(1)}, u32[]{:S(2)}, u32[]{:S(2)}) collective-permute-start(bf16[2,1,64,256]{3,2,1,0:T(8,128)(2,1)S(1)} %get-tuple-element.11), channel_id=1, source_target_pairs={{1,0},{2,1},{3,2},{4,3},{5,4},{6,5},{7,6},{8,7},{9,8},{10,9},{11,1... | collective-permute-start | bytes 196616 | tf_op jit(solution)/shard_map/ppermute | solution.py:21
  27.8 6.8 %collective-permute-start = (bf16[2,1,64,256]{3,2,1,0:T(8,128)(2,1)S(1)}, bf16[2,1,64,256]{3,2,1,0:T(8,128)(2,1)S(1)}, u32[]{:S(2)}, u32[]{:S(2)}) collective-permute-start(bf16[2,1,64,256]{3,2,1,0:T(8,128)(2,1)S(1)} %get-tuple-element.10), channel_id=1, source_target_pairs={{0,1},{1,2},{2,3},{3,4},{4,5},{5,6},{6,7},{7,8},{8,9},{9,10},{10,1... | collective-permute-start | bytes 196616 | tf_op jit(solution)/shard_map/ppermute | solution.py:19
  37.1 7.7 %collective-permute-start.2 = (bf16[2,4,64,256]{3,2,1,0:T(8,128)(2,1)S(1)}, bf16[2,4,64,256]{3,2,1,0:T(8,128)(2,1)S(1)}, u32[]{:S(2)}, u32[]{:S(2)}) collective-permute-start(bf16[2,4,64,256]{3,2,1,0:T(8,128)(2,1)S(1)} %fusion.6), channel_id=1, source_target_pairs={{0,96},{96,192},{192,288},{288,384},{384,480},{480,576},{576,672},... | collective-permute-start | bytes 786440 | tf_op jit(solution)/shard_map/ppermute | solution.py:31
Sparse Core Ops, SparseCore 0:
  46.8 500.4 all-reduce.6
where the time goes:
time: 557 us
  waiting for transfers between devices  505 us (91%)
  starting transfers between devices  16.4 us (3%)
  between operations  14.4 us (3%)
  matrix products  11.1 us (2%)
  local copies, waits for them, and re-layouts  7.02 us (1%)
    unnamed x2, waiting for transfers between devices  499 us
  transfers between devices with their start and end apart: 7, of which 7 were waited for; matrix products, arithmetic and copies ran while one was open for 2% of the time, Pallas kernels for 0%

commit v1 on v0

--- a/solution.py
+++ b/solution.py
@@ -50,6 +50,31 @@
         (((0,), (0,)), ((), ())),
         preferred_element_type=jnp.float32,
     )
+
+
+def halving_scatter(block, axis):
+    count = lax.axis_size(axis)
+    index = lax.axis_index(axis)
+    step = 1
+    while count // step % 2 == 0:
+        rest = block.shape[1:]
+        pairs = block.reshape((block.shape[0] // 2, 2) + rest)
+        mine = index // step % 2
+        keep = lax.dynamic_index_in_dim(pairs, mine, axis=1, keepdims=False)
+        send = lax.dynamic_index_in_dim(pairs, 1 - mine, axis=1, keepdims=False)
+        route = [(i, i ^ step) for i in range(count)]
+        block = keep + lax.ppermute(send, axis, route)
+        step *= 2
+    ways = count // step
+    if ways > 1:
+        group = index // step
+        total = lax.dynamic_index_in_dim(block, group, axis=0, keepdims=True)
+        for shift in range(1, ways):
+            route = [(i, (i + shift * step) % count) for i in range(count)]
+            row = lax.dynamic_index_in_dim(block, (group + shift) % ways, axis=0, keepdims=True)
+            total = total + lax.ppermute(row, axis, route)
+        block = total
+    return block
 
 
 def shards(clip, cotangent, spatial_weight, temporal_weight):
@@ -114,12 +139,16 @@
     time_shards = lax.axis_size("tm")
     row_shards = lax.axis_size("height")
     grad_scale = 1.0 / math.sqrt(frame_count * time_shards * row_count * row_shards * col_count)
-    flat_spatial = (grad_spatial * grad_scale).reshape(-1)
-    flat_temporal = (grad_temporal * grad_scale).reshape(-1)
-    spatial_part, temporal_part = (
-        lax.psum_scatter(flat_spatial, ("tm", "height"), scatter_dimension=0, tiled=True),
-        lax.psum_scatter(flat_temporal, ("tm", "height"), scatter_dimension=0, tiled=True),
-    )
+    devices = time_shards * row_shards
+    spatial_rows = grad_spatial.reshape(devices, -1)
+    temporal_rows = grad_temporal.reshape(devices, -1)
+    packed = jnp.concatenate([spatial_rows, temporal_rows], axis=1)
+    packed = packed.reshape(time_shards, row_shards, packed.shape[-1])
+    packed = halving_scatter(packed, "tm")[0]
+    packed = halving_scatter(packed, "height")[0]
+    packed = packed * grad_scale
+    spatial_part = packed[: spatial_rows.shape[1]]
+    temporal_part = packed[spatial_rows.shape[1] :]
     return (output, grad_clip, spatial_part, temporal_part)
 
 

time: 557 us -> 173 us (0.31)
  waiting for transfers between devices: 505 us -> 56.6 us
  starting transfers between devices: 16.4 us -> 78.6 us
  between operations: 14.4 us -> 1.64 us
  matrix products: 11.1 us -> 19.2 us
    unnamed x2 -> x0, waiting for transfers between devices: 499 us -> none
    ppermute x0 -> x10, starting transfers between devices: none -> 62.3 us  [the longest x8 42.9 us: halving_scatter(): block = keep + lax.ppermute(send, axis, route)]
    ppermute x0 -> x10, waiting for transfers between devices: none -> 51 us  [the longest x8 44.5 us: halving_scatter(): block = keep + lax.ppermute(send, axis, route)]
    dot_general x12, matrix products: 3.26 us -> 9.52 us  [outer_sum(): lax.dot_general(left.reshape(-1, channels), right.reshape(-1, channels),...]
  transfers between devices with their start and end apart: 7 -> 16, of which waited for: 7 -> 14; matrix products, arithmetic and copies ran while one was open for 2% -> 8% of each run, Pallas kernels for 0% -> 0%
where the time goes in v1:
time: 173 us; the launch traced here: 170 us
  starting transfers between devices  78.6 us (45%)
  waiting for transfers between devices  56.6 us (33%)
  matrix products  19.2 us (11%)
  local copies, waits for them, and re-layouts  7.1 us (4%)
  other arithmetic  6.85 us (4%)
    ppermute x8, waiting for transfers between devices, halving_scatter(): block = keep + lax.ppermute(send, axis, route)  44.5 us
    ppermute x8, starting transfers between devices, halving_scatter(): block = keep + lax.ppermute(send, axis, route)  42.9 us
    ppermute x2, starting transfers between devices, halving_scatter(): total = total + lax.ppermute(row, axis, route)  19.4 us
    dot_general x24, matrix products, flat_dot(): jnp.dot(left.reshape(-1, left.shape[-1]), weight, preferred_element_type=...  9.71 us
    dot_general x12, matrix products, outer_sum(): lax.dot_general(left.reshape(-1, channels), right.reshape(-1, channels),...  9.52 us
    ppermute x2, starting transfers between devices, extended(): lax.ppermute(tail, axis, [(i, (i + 1) % count) for i in range(ends)])  9.44 us
    ppermute x2, waiting for transfers between devices, halving_scatter(): total = total + lax.ppermute(row, axis, route)  6.52 us
    ppermute x2, starting transfers between devices, shifted(): return lax.ppermute(block, axis, route)  4.23 us
  transfers between devices with their start and end apart: 16, of which 14 were waited for; matrix products, arithmetic and copies ran while one was open for 8% of the time, Pallas kernels for 0%

profile of v1, /device:TPU:6, one launch (start us, length us, event | category | flops | bytes accessed | tf_op | source)
XLA Modules:
  0.0 170.0 jit_solution(12408526681733728623)
XLA Ops:
  0.6 2.3 %collective-permute-start.3 = (bf16[2,4,64,256]{3,2,1,0:T(8,128)(2,1)}, bf16[2,4,64,256]{3,2,1,0:T(8,128)(2,1)S(1)}, u32[]{:S(2)}, u32[]{:S(2)}) collective-permute-start(bf16[2,4,64,256]{3,2,1,0:T(8,128)(2,1)} %param.5), channel_id=1, source_target_pairs={{96,0},{192,96},{288,192},{384,288},{480,384},{576,480},{672,576},... | collective-permute-start | bytes 786440 | tf_op jit(solution)/shard_map/ppermute | solution.py:31
  5.3 1.8 %collective-permute-done.3 = bf16[2,4,64,256]{3,2,1,0:T(8,128)(2,1)S(1)} collective-permute-done((bf16[2,4,64,256]{3,2,1,0:T(8,128)(2,1)}, bf16[2,4,64,256]{3,2,1,0:T(8,128)(2,1)S(1)}, u32[]{:S(2)}, u32[]{:S(2)}) %collective-permute-start.3) | collective-permute-done | bytes 262176 | tf_op jit(solution)/shard_map/ppermute | solution.py:31
  10.9 4.5 %collective-permute-start.4 = (bf16[2,1,64,256]{3,2,1,0:T(8,128)(2,1)S(1)}, bf16[2,1,64,256]{3,2,1,0:T(8,128)(2,1)S(1)}, u32[]{:S(2)}, u32[]{:S(2)}) collective-permute-start(bf16[2,1,64,256]{3,2,1,0:T(8,128)(2,1)S(1)} %get-tuple-element.8), channel_id=1, source_target_pairs={{0,1},{1,2},{2,3},{3,4},{4,5},{5,6},{6,7},{7,8},{8,9},{9,10},{10,1... | collective-permute-start | bytes 196616 | tf_op jit(solution)/shard_map/ppermute | solution.py:19
  22.9 4.9 %collective-permute-start = (bf16[2,1,64,256]{3,2,1,0:T(8,128)(2,1)S(1)}, bf16[2,1,64,256]{3,2,1,0:T(8,128)(2,1)S(1)}, u32[]{:S(2)}, u32[]{:S(2)}) collective-permute-start(bf16[2,1,64,256]{3,2,1,0:T(8,128)(2,1)S(1)} %get-tuple-element.10), channel_id=1, source_target_pairs={{0,1},{1,2},{2,3},{3,4},{4,5},{5,6},{6,7},{7,8},{8,9},{9,10},{10,1... | collective-permute-start | bytes 196616 | tf_op jit(solution)/shard_map/ppermute | solution.py:19
  32.9 1.9 %collective-permute-start.2 = (bf16[2,4,64,256]{3,2,1,0:T(8,128)(2,1)S(1)}, bf16[2,4,64,256]{3,2,1,0:T(8,128)(2,1)S(1)}, u32[]{:S(2)}, u32[]{:S(2)}) collective-permute-start(bf16[2,4,64,256]{3,2,1,0:T(8,128)(2,1)S(1)} %fusion.11), channel_id=1, source_target_pairs={{0,96},{96,192},{192,288},{288,384},{384,480},{480,576},{576,672},... | collective-permute-start | bytes 786440 | tf_op jit(solution)/shard_map/ppermute | solution.py:31
  42.6 2.6 %concatenate.40 = f32[4,2,96,768]{3,2,1,0:T(8,128)S(1)} reshape(f32[9,256,256]{2,1,0:T(8,128)} %fusion.15) | data formatting | bytes 4718592 | tf_op jit(solution)/shard_map/concatenate | solution.py:145
  47.9 1.9 %collective-permute-start.6 = (f32[4,96,1024]{2,1,0:T(8,128)}, f32[4,96,1024]{2,1,0:T(8,128)}, u32[]{:S(2)}, u32[]{:S(2)}) collective-permute-start(f32[4,96,1024]{2,1,0:T(8,128)} %fusion.1), channel_id=1, source_target_pairs={{0,96},{96,0},{192,288},{288,192},{384,480},{480,384},{576,672},{6... | collective-permute-start | bytes 4718600 | tf_op jit(solution)/shard_map/ppermute | solution.py:66
  49.9 3.7 %collective-permute-done.6 = f32[4,96,1024]{2,1,0:T(8,128)} collective-permute-done((f32[4,96,1024]{2,1,0:T(8,128)}, f32[4,96,1024]{2,1,0:T(8,128)}, u32[]{:S(2)}, u32[]{:S(2)}) %collective-permute-start.6) | collective-permute-done | bytes 1572896 | tf_op jit(solution)/shard_map/ppermute | solution.py:66
  56.4 3.7 %collective-permute-start.7 = (f32[2,96,1024]{2,1,0:T(8,128)S(1)}, f32[2,96,1024]{2,1,0:T(8,128)S(1)}, u32[]{:S(2)}, u32[]{:S(2)}) collective-permute-start(f32[2,96,1024]{2,1,0:T(8,128)S(1)} %dynamic-slice_bitcast_fusion), channel_id=1, source_target_pairs={{0,192},{96,288},{192,0},{288,96},{384,576},{480,672},{576,384},{6... | collective-permute-start | bytes 2359304 | tf_op jit(solution)/shard_map/ppermute | solution.py:66
  60.1 18.0 %collective-permute-done.7 = f32[2,96,1024]{2,1,0:T(8,128)S(1)} collective-permute-done((f32[2,96,1024]{2,1,0:T(8,128)S(1)}, f32[2,96,1024]{2,1,0:T(8,128)S(1)}, u32[]{:S(2)}, u32[]{:S(2)}) %collective-permute-start.7) | collective-permute-done | bytes 786464 | tf_op jit(solution)/shard_map/ppermute | solution.py:66
  79.4 8.1 %collective-permute-start.8 = (f32[1,96,1024]{2,1,0:T(8,128)S(1)}, f32[1,96,1024]{2,1,0:T(8,128)S(1)}, u32[]{:S(2)}, u32[]{:S(2)}) collective-permute-start(f32[1,96,1024]{2,1,0:T(8,128)S(1)} %constant_dynamic-slice_fusion.13), channel_id=1, source_target_pairs={{0,384},{96,480},{192,576},{288,672},{384,0},{480,96},{576,192},{6... | collective-permute-start | bytes 1179656 | tf_op jit(solution)/shard_map/ppermute | solution.py:66
  87.6 8.8 %collective-permute-done.8 = f32[1,96,1024]{2,1,0:T(8,128)S(1)} collective-permute-done((f32[1,96,1024]{2,1,0:T(8,128)S(1)}, f32[1,96,1024]{2,1,0:T(8,128)S(1)}, u32[]{:S(2)}, u32[]{:S(2)}) %collective-permute-start.8) | collective-permute-done | bytes 393248 | tf_op jit(solution)/shard_map/ppermute | solution.py:66
  97.1 4.4 %collective-permute-start.9 = (f32[48,1024]{1,0:T(8,128)S(1)}, f32[48,1024]{1,0:T(8,128)S(1)}, u32[]{:S(2)}, u32[]{:S(2)}) collective-permute-start(f32[48,1024]{1,0:T(8,128)S(1)} %bitcast.263), channel_id=1, source_target_pairs={{0,1},{1,0},{2,3},{3,2},{4,5},{5,4},{6,7},{7,6},{8,9},{9,8},{10,11... | collective-permute-start | bytes 589832 | tf_op jit(solution)/shard_map/ppermute | solution.py:66
  101.6 4.0 %collective-permute-done.9 = f32[48,1024]{1,0:T(8,128)S(1)} collective-permute-done((f32[48,1024]{1,0:T(8,128)S(1)}, f32[48,1024]{1,0:T(8,128)S(1)}, u32[]{:S(2)}, u32[]{:S(2)}) %collective-permute-start.9) | collective-permute-done | bytes 196640 | tf_op jit(solution)/shard_map/ppermute | solution.py:66
  106.0 5.1 %collective-permute-start.10 = (f32[24,1024]{1,0:T(8,128)S(1)}, f32[24,1024]{1,0:T(8,128)S(1)}, u32[]{:S(2)}, u32[]{:S(2)}) collective-permute-start(f32[24,1024]{1,0:T(8,128)S(1)} %bitcast.264), channel_id=1, source_target_pairs={{0,2},{1,3},{2,0},{3,1},{4,6},{5,7},{6,4},{7,5},{8,10},{9,11},{10,... | collective-permute-start | bytes 294920 | tf_op jit(solution)/shard_map/ppermute | solution.py:66
  111.2 3.6 %collective-permute-done.10 = f32[24,1024]{1,0:T(8,128)S(1)} collective-permute-done((f32[24,1024]{1,0:T(8,128)S(1)}, f32[24,1024]{1,0:T(8,128)S(1)}, u32[]{:S(2)}, u32[]{:S(2)}) %collective-permute-start.10) | collective-permute-done | bytes 98336 | tf_op jit(solution)/shard_map/ppermute | solution.py:66
  115.0 6.8 %collective-permute-start.11 = (f32[12,1024]{1,0:T(8,128)S(1)}, f32[12,1024]{1,0:T(8,128)S(1)}, u32[]{:S(2)}, u32[]{:S(2)}) collective-permute-start(f32[12,1024]{1,0:T(8,128)S(1)} %bitcast.265), channel_id=1, source_target_pairs={{0,4},{1,5},{2,6},{3,7},{4,0},{5,1},{6,2},{7,3},{8,12},{9,13},{10,... | collective-permute-start | bytes 147464 | tf_op jit(solution)/shard_map/ppermute | solution.py:66
  122.0 3.2 %collective-permute-done.11 = f32[12,1024]{1,0:T(8,128)S(1)} collective-permute-done((f32[12,1024]{1,0:T(8,128)S(1)}, f32[12,1024]{1,0:T(8,128)S(1)}, u32[]{:S(2)}, u32[]{:S(2)}) %collective-permute-start.11) | collective-permute-done | bytes 49184 | tf_op jit(solution)/shard_map/ppermute | solution.py:66
  125.3 6.8 %collective-permute-start.12 = (f32[6,1024]{1,0:T(8,128)S(1)}, f32[6,1024]{1,0:T(8,128)S(1)}, u32[]{:S(2)}, u32[]{:S(2)}) collective-permute-start(f32[6,1024]{1,0:T(8,128)S(1)} %bitcast.266), channel_id=1, source_target_pairs={{0,8},{1,9},{2,10},{3,11},{4,12},{5,13},{6,14},{7,15},{8,0},{9,1},... | collective-permute-start | bytes 73736 | tf_op jit(solution)/shard_map/ppermute | solution.py:66
  132.3 1.6 collective-permute-done.12
  134.0 6.1 %collective-permute-start.13 = (f32[3,1024]{1,0:T(4,128)S(1)}, f32[3,1024]{1,0:T(4,128)S(1)}, u32[]{:S(2)}, u32[]{:S(2)}) collective-permute-start(f32[3,1024]{1,0:T(4,128)S(1)} %bitcast.267), channel_id=1, source_target_pairs={{0,16},{1,17},{2,18},{3,19},{4,20},{5,21},{6,22},{7,23},{8,24},{9,... | collective-permute-start | bytes 36872 | tf_op jit(solution)/shard_map/ppermute | solution.py:66
  141.8 17.5 %collective-permute-start.15 = (f32[1,1024]{1,0:T(1,128)S(1)}, f32[1,1024]{1,0:T(1,128)S(1)}, u32[]{:S(2)}, u32[]{:S(2)}) collective-permute-start(f32[1,1024]{1,0:T(1,128)S(1)} %get-tuple-element.21), channel_id=1, source_target_pairs={{0,64},{1,65},{2,66},{3,67},{4,68},{5,69},{6,70},{7,71},{8,72},{9,... | collective-permute-start | bytes 12296 | tf_op jit(solution)/shard_map/ppermute | solution.py:75
  159.4 1.9 %collective-permute-start.14 = (f32[1,1024]{1,0:T(1,128)S(1)}, f32[1,1024]{1,0:T(1,128)S(1)}, u32[]{:S(2)}, u32[]{:S(2)}) collective-permute-start(f32[1,1024]{1,0:T(1,128)S(1)} %get-tuple-element.20), channel_id=1, source_target_pairs={{0,32},{1,33},{2,34},{3,35},{4,36},{5,37},{6,38},{7,39},{8,40},{9,... | collective-permute-start | bytes 12296 | tf_op jit(solution)/shard_map/ppermute | solution.py:75
  162.3 6.5 %collective-permute-done.14 = f32[1,1024]{1,0:T(1,128)S(1)} collective-permute-done((f32[1,1024]{1,0:T(1,128)S(1)}, f32[1,1024]{1,0:T(1,128)S(1)}, u32[]{:S(2)}, u32[]{:S(2)}) %collective-permute-start.14) | collective-permute-done | bytes 4128 | tf_op jit(solution)/shard_map/ppermute | solution.py:75
  (100 shorter events, 38.4 us)
Async XLA Ops:
  0.6 7.7 %copy-start.2 = (bf16[2,4,64,256]{3,2,1,0:T(8,128)(2,1)S(1)}, bf16[2,4,64,256]{3,2,1,0:T(8,128)(2,1)}, u32[]{:S(2)}) copy-start(bf16[2,4,64,256]{3,2,1,0:T(8,128)(2,1)} %param.5) | copy-start | bytes 786436
  0.6 6.5 %collective-permute-start.3 = (bf16[2,4,64,256]{3,2,1,0:T(8,128)(2,1)}, bf16[2,4,64,256]{3,2,1,0:T(8,128)(2,1)S(1)}, u32[]{:S(2)}, u32[]{:S(2)}) collective-permute-start(bf16[2,4,64,256]{3,2,1,0:T(8,128)(2,1)} %param.5), channel_id=1, source_target_pairs={{96,0},{192,96},{288,192},{384,288},{480,384},{576,480},{672,576},... | collective-permute-start | bytes 786440 | tf_op jit(solution)/shard_map/ppermute | solution.py:31
  8.3 9.2 %copy-start.1 = (bf16[3,3,256,256]{3,2,1,0:T(8,128)(2,1)S(1)}, bf16[3,3,256,256]{3,2,1,0:T(8,128)(2,1)}, u32[]{:S(2)}) copy-start(bf16[3,3,256,256]{3,2,1,0:T(8,128)(2,1)} %param.6) | copy-start | bytes 3538948
  9.6 6.2 %collective-permute-start.5 = (bf16[2,1,64,256]{3,2,1,0:T(8,128)(2,1)S(1)}, bf16[2,1,64,256]{3,2,1,0:T(8,128)(2,1)S(1)}, u32[]{:S(2)}, u32[]{:S(2)}) collective-permute-start(bf16[2,1,64,256]{3,2,1,0:T(8,128)(2,1)S(1)} %get-tuple-element.9), channel_id=1, source_target_pairs={{1,0},{2,1},{3,2},{4,3},{5,4},{6,5},{7,6},{8,7},{9,8},{10,9},{11,1... | collective-permute-start | bytes 196616 | tf_op jit(solution)/shard_map/ppermute | solution.py:21
  10.9 6.4 %collective-permute-start.4 = (bf16[2,1,64,256]{3,2,1,0:T(8,128)(2,1)S(1)}, bf16[2,1,64,256]{3,2,1,0:T(8,128)(2,1)S(1)}, u32[]{:S(2)}, u32[]{:S(2)}) collective-permute-start(bf16[2,1,64,256]{3,2,1,0:T(8,128)(2,1)S(1)} %get-tuple-element.8), channel_id=1, source_target_pairs={{0,1},{1,2},{2,3},{3,4},{4,5},{5,6},{6,7},{7,8},{8,9},{9,10},{10,1... | collective-permute-start | bytes 196616 | tf_op jit(solution)/shard_map/ppermute | solution.py:19
  19.1 1.0 copy-start.3
  21.6 6.5 %collective-permute-start.1 = (bf16[2,1,64,256]{3,2,1,0:T(8,128)(2,1)S(1)}, bf16[2,1,64,256]{3,2,1,0:T(8,128)(2,1)S(1)}, u32[]{:S(2)}, u32[]{:S(2)}) collective-permute-start(bf16[2,1,64,256]{3,2,1,0:T(8,128)(2,1)S(1)} %get-tuple-element.11), channel_id=1, source_target_pairs={{1,0},{2,1},{3,2},{4,3},{5,4},{6,5},{7,6},{8,7},{9,8},{10,9},{11,1... | collective-permute-start | bytes 196616 | tf_op jit(solution)/shard_map/ppermute | solution.py:21
  22.9 6.8 %collective-permute-start = (bf16[2,1,64,256]{3,2,1,0:T(8,128)(2,1)S(1)}, bf16[2,1,64,256]{3,2,1,0:T(8,128)(2,1)S(1)}, u32[]{:S(2)}, u32[]{:S(2)}) collective-permute-start(bf16[2,1,64,256]{3,2,1,0:T(8,128)(2,1)S(1)} %get-tuple-element.10), channel_id=1, source_target_pairs={{0,1},{1,2},{2,3},{3,4},{4,5},{5,6},{6,7},{7,8},{8,9},{9,10},{10,1... | collective-permute-start | bytes 196616 | tf_op jit(solution)/shard_map/ppermute | solution.py:19
  32.9 12.5 %collective-permute-start.2 = (bf16[2,4,64,256]{3,2,1,0:T(8,128)(2,1)S(1)}, bf16[2,4,64,256]{3,2,1,0:T(8,128)(2,1)S(1)}, u32[]{:S(2)}, u32[]{:S(2)}) collective-permute-start(bf16[2,4,64,256]{3,2,1,0:T(8,128)(2,1)S(1)} %fusion.11), channel_id=1, source_target_pairs={{0,96},{96,192},{192,288},{288,384},{384,480},{480,576},{576,672},... | collective-permute-start | bytes 786440 | tf_op jit(solution)/shard_map/ppermute | solution.py:31
  45.5 0.7 copy-start.6
  47.9 5.6 %collective-permute-start.6 = (f32[4,96,1024]{2,1,0:T(8,128)}, f32[4,96,1024]{2,1,0:T(8,128)}, u32[]{:S(2)}, u32[]{:S(2)}) collective-permute-start(f32[4,96,1024]{2,1,0:T(8,128)} %fusion.1), channel_id=1, source_target_pairs={{0,96},{96,0},{192,288},{288,192},{384,480},{480,384},{576,672},{6... | collective-permute-start | bytes 4718600 | tf_op jit(solution)/shard_map/ppermute | solution.py:66
  55.2 1.2 copy-start
  56.4 21.7 %collective-permute-start.7 = (f32[2,96,1024]{2,1,0:T(8,128)S(1)}, f32[2,96,1024]{2,1,0:T(8,128)S(1)}, u32[]{:S(2)}, u32[]{:S(2)}) collective-permute-start(f32[2,96,1024]{2,1,0:T(8,128)S(1)} %dynamic-slice_bitcast_fusion), channel_id=1, source_target_pairs={{0,192},{96,288},{192,0},{288,96},{384,576},{480,672},{576,384},{6... | collective-permute-start | bytes 2359304 | tf_op jit(solution)/shard_map/ppermute | solution.py:66
  79.4 17.0 %collective-permute-start.8 = (f32[1,96,1024]{2,1,0:T(8,128)S(1)}, f32[1,96,1024]{2,1,0:T(8,128)S(1)}, u32[]{:S(2)}, u32[]{:S(2)}) collective-permute-start(f32[1,96,1024]{2,1,0:T(8,128)S(1)} %constant_dynamic-slice_fusion.13), channel_id=1, source_target_pairs={{0,384},{96,480},{192,576},{288,672},{384,0},{480,96},{576,192},{6... | collective-permute-start | bytes 1179656 | tf_op jit(solution)/shard_map/ppermute | solution.py:66
  97.1 34.9 %copy-start.5 = (bf16[3,256,256]{2,1,0:T(8,128)(2,1)S(1)}, bf16[3,256,256]{2,1,0:T(8,128)(2,1)}, u32[]{:S(2)}) copy-start(bf16[3,256,256]{2,1,0:T(8,128)(2,1)} %param.7) | copy-start | bytes 1179652
  97.1 8.5 %collective-permute-start.9 = (f32[48,1024]{1,0:T(8,128)S(1)}, f32[48,1024]{1,0:T(8,128)S(1)}, u32[]{:S(2)}, u32[]{:S(2)}) collective-permute-start(f32[48,1024]{1,0:T(8,128)S(1)} %bitcast.263), channel_id=1, source_target_pairs={{0,1},{1,0},{2,3},{3,2},{4,5},{5,4},{6,7},{7,6},{8,9},{9,8},{10,11... | collective-permute-start | bytes 589832 | tf_op jit(solution)/shard_map/ppermute | solution.py:66
  105.8 34.3 %copy-start.7 = (bf16[2,4,64,256]{3,2,1,0:T(8,128)(2,1)S(1)}, bf16[2,4,64,256]{3,2,1,0:T(8,128)(2,1)}, u32[]{:S(2)}) copy-start(bf16[2,4,64,256]{3,2,1,0:T(8,128)(2,1)} %copy-done.6) | copy-start | bytes 786436
  106.0 8.8 %collective-permute-start.10 = (f32[24,1024]{1,0:T(8,128)S(1)}, f32[24,1024]{1,0:T(8,128)S(1)}, u32[]{:S(2)}, u32[]{:S(2)}) collective-permute-start(f32[24,1024]{1,0:T(8,128)S(1)} %bitcast.264), channel_id=1, source_target_pairs={{0,2},{1,3},{2,0},{3,1},{4,6},{5,7},{6,4},{7,5},{8,10},{9,11},{10,... | collective-permute-start | bytes 294920 | tf_op jit(solution)/shard_map/ppermute | solution.py:66
  114.9 46.4 %copy-start.4 = (bf16[2,4,64,256]{3,2,1,0:T(8,128)(2,1)S(1)}, bf16[2,4,64,256]{3,2,1,0:T(8,128)(2,1)}, u32[]{:S(2)}) copy-start(bf16[2,4,64,256]{3,2,1,0:T(8,128)(2,1)} %param.4) | copy-start | bytes 786436
  115.0 10.2 %collective-permute-start.11 = (f32[12,1024]{1,0:T(8,128)S(1)}, f32[12,1024]{1,0:T(8,128)S(1)}, u32[]{:S(2)}, u32[]{:S(2)}) collective-permute-start(f32[12,1024]{1,0:T(8,128)S(1)} %bitcast.265), channel_id=1, source_target_pairs={{0,4},{1,5},{2,6},{3,7},{4,0},{5,1},{6,2},{7,3},{8,12},{9,13},{10,... | collective-permute-start | bytes 147464 | tf_op jit(solution)/shard_map/ppermute | solution.py:66
  125.3 8.6 %collective-permute-start.12 = (f32[6,1024]{1,0:T(8,128)S(1)}, f32[6,1024]{1,0:T(8,128)S(1)}, u32[]{:S(2)}, u32[]{:S(2)}) collective-permute-start(f32[6,1024]{1,0:T(8,128)S(1)} %bitcast.266), channel_id=1, source_target_pairs={{0,8},{1,9},{2,10},{3,11},{4,12},{5,13},{6,14},{7,15},{8,0},{9,1},... | collective-permute-start | bytes 73736 | tf_op jit(solution)/shard_map/ppermute | solution.py:66
  134.0 7.8 %collective-permute-start.13 = (f32[3,1024]{1,0:T(4,128)S(1)}, f32[3,1024]{1,0:T(4,128)S(1)}, u32[]{:S(2)}, u32[]{:S(2)}) collective-permute-start(f32[3,1024]{1,0:T(4,128)S(1)} %bitcast.267), channel_id=1, source_target_pairs={{0,16},{1,17},{2,18},{3,19},{4,20},{5,21},{6,22},{7,23},{8,24},{9,... | collective-permute-start | bytes 36872 | tf_op jit(solution)/shard_map/ppermute | solution.py:66
  141.8 20.4 %collective-permute-start.15 = (f32[1,1024]{1,0:T(1,128)S(1)}, f32[1,1024]{1,0:T(1,128)S(1)}, u32[]{:S(2)}, u32[]{:S(2)}) collective-permute-start(f32[1,1024]{1,0:T(1,128)S(1)} %get-tuple-element.21), channel_id=1, source_target_pairs={{0,64},{1,65},{2,66},{3,67},{4,68},{5,69},{6,70},{7,71},{8,72},{9,... | collective-permute-start | bytes 12296 | tf_op jit(solution)/shard_map/ppermute | solution.py:75
  159.4 9.4 %collective-permute-start.14 = (f32[1,1024]{1,0:T(1,128)S(1)}, f32[1,1024]{1,0:T(1,128)S(1)}, u32[]{:S(2)}, u32[]{:S(2)}) collective-permute-start(f32[1,1024]{1,0:T(1,128)S(1)} %get-tuple-element.20), channel_id=1, source_target_pairs={{0,32},{1,33},{2,34},{3,35},{4,36},{5,37},{6,38},{7,39},{8,40},{9,... | collective-permute-start | bytes 12296 | tf_op jit(solution)/shard_map/ppermute | solution.py:75

commit v2 on v1

--- a/solution.py
+++ b/solution.py
@@ -145,7 +145,8 @@
     packed = jnp.concatenate([spatial_rows, temporal_rows], axis=1)
     packed = packed.reshape(time_shards, row_shards, packed.shape[-1])
     packed = halving_scatter(packed, "tm")[0]
-    packed = halving_scatter(packed, "height")[0]
+    packed = lax.all_to_all(packed, "height", 0, 0, tiled=True)
+    packed = jnp.sum(packed, axis=0)
     packed = packed * grad_scale
     spatial_part = packed[: spatial_rows.shape[1]]
     temporal_part = packed[spatial_rows.shape[1] :]

time: 173 us -> 148 us (0.86)
  starting transfers between devices: 78.6 us -> 54.2 us
    ppermute x8 -> x3, starting transfers between devices: 42.9 us -> 13.8 us  [halving_scatter(): block = keep + lax.ppermute(send, axis, route)]
    all_to_all x0 -> x1, starting transfers between devices: none -> 24.1 us  [shards(): packed = lax.all_to_all(packed, 'height', 0, 0, tiled=True)]
    all_to_all x0 -> x1, waiting for transfers between devices: none -> 21.3 us  [shards(): packed = lax.all_to_all(packed, 'height', 0, 0, tiled=True)]
    ppermute x2 -> x0, starting transfers between devices: 19.4 us -> none  [halving_scatter(): total = total + lax.ppermute(row, axis, route)]
    ppermute x8 -> x3, waiting for transfers between devices: 44.5 us -> 30.6 us  [halving_scatter(): block = keep + lax.ppermute(send, axis, route)]
    ppermute x2 -> x0, waiting for transfers between devices: 6.52 us -> none  [halving_scatter(): total = total + lax.ppermute(row, axis, route)]
  transfers between devices with their start and end apart: 16 -> 10, of which waited for: 14 -> 9; matrix products, arithmetic and copies ran while one was open for 8% -> 10% of each run, Pallas kernels for 0% -> 0%
where the time goes in v2:
time: 148 us; the launch traced here: 146 us
  waiting for transfers between devices  57.4 us (39%)
  starting transfers between devices  54.2 us (37%)
  matrix products  19.3 us (13%)
  other arithmetic  7.01 us (5%)
  local copies, waits for them, and re-layouts  6.44 us (4%)
    ppermute x3, waiting for transfers between devices, halving_scatter(): block = keep + lax.ppermute(send, axis, route)  30.6 us
    all_to_all x1, starting transfers between devices, shards(): packed = lax.all_to_all(packed, 'height', 0, 0, tiled=True)  24.1 us
    all_to_all x1, waiting for transfers between devices, shards(): packed = lax.all_to_all(packed, 'height', 0, 0, tiled=True)  21.3 us
    ppermute x3, starting transfers between devices, halving_scatter(): block = keep + lax.ppermute(send, axis, route)  13.8 us
    dot_general x24, matrix products, flat_dot(): jnp.dot(left.reshape(-1, left.shape[-1]), weight, preferred_element_type=...  9.72 us
    dot_general x12, matrix products, outer_sum(): lax.dot_general(left.reshape(-1, channels), right.reshape(-1, channels),...  9.62 us
    ppermute x2, starting transfers between devices, extended(): lax.ppermute(tail, axis, [(i, (i + 1) % count) for i in range(ends)])  9.44 us
    ppermute x2, starting transfers between devices, shifted(): return lax.ppermute(block, axis, route)  4.23 us
  transfers between devices with their start and end apart: 10, of which 9 were waited for; matrix products, arithmetic and copies ran while one was open for 10% of the time, Pallas kernels for 0%

profile of v2, /device:TPU:6, one launch (start us, length us, event | category | flops | bytes accessed | tf_op | source)
XLA Modules:
  0.0 145.6 jit_solution(10932739347671720128)
XLA Ops:
  0.6 2.3 %collective-permute-start.3 = (bf16[2,4,64,256]{3,2,1,0:T(8,128)(2,1)}, bf16[2,4,64,256]{3,2,1,0:T(8,128)(2,1)S(1)}, u32[]{:S(2)}, u32[]{:S(2)}) collective-permute-start(bf16[2,4,64,256]{3,2,1,0:T(8,128)(2,1)} %param.5), channel_id=1, source_target_pairs={{96,0},{192,96},{288,192},{384,288},{480,384},{576,480},{672,576},... | collective-permute-start | bytes 786440 | tf_op jit(solution)/shard_map/ppermute | solution.py:31
  4.1 1.2 fusion.92
  5.3 1.8 %collective-permute-done.3 = bf16[2,4,64,256]{3,2,1,0:T(8,128)(2,1)S(1)} collective-permute-done((bf16[2,4,64,256]{3,2,1,0:T(8,128)(2,1)}, bf16[2,4,64,256]{3,2,1,0:T(8,128)(2,1)S(1)}, u32[]{:S(2)}, u32[]{:S(2)}) %collective-permute-start.3) | collective-permute-done | bytes 262176 | tf_op jit(solution)/shard_map/ppermute | solution.py:31
  8.3 1.3 fusion.12
  9.6 1.3 collective-permute-start.5
  10.9 4.5 %collective-permute-start.4 = (bf16[2,1,64,256]{3,2,1,0:T(8,128)(2,1)S(1)}, bf16[2,1,64,256]{3,2,1,0:T(8,128)(2,1)S(1)}, u32[]{:S(2)}, u32[]{:S(2)}) collective-permute-start(bf16[2,1,64,256]{3,2,1,0:T(8,128)(2,1)S(1)} %get-tuple-element.6), channel_id=1, source_target_pairs={{0,1},{1,2},{2,3},{3,4},{4,5},{5,6},{6,7},{7,8},{8,9},{9,10},{10,1... | collective-permute-start | bytes 196616 | tf_op jit(solution)/shard_map/ppermute | solution.py:19
  15.8 1.6 %collective-permute-done.4 = bf16[2,1,64,256]{3,2,1,0:T(8,128)(2,1)S(1)} collective-permute-done((bf16[2,1,64,256]{3,2,1,0:T(8,128)(2,1)S(1)}, bf16[2,1,64,256]{3,2,1,0:T(8,128)(2,1)S(1)}, u32[]{:S(2)}, u32[]{:S(2)}) %collective-permute-start.4) | collective-permute-done | bytes 65568 | tf_op jit(solution)/shard_map/ppermute | solution.py:19
  21.6 1.3 collective-permute-start.1
  22.9 4.9 %collective-permute-start = (bf16[2,1,64,256]{3,2,1,0:T(8,128)(2,1)S(1)}, bf16[2,1,64,256]{3,2,1,0:T(8,128)(2,1)S(1)}, u32[]{:S(2)}, u32[]{:S(2)}) collective-permute-start(bf16[2,1,64,256]{3,2,1,0:T(8,128)(2,1)S(1)} %get-tuple-element.8), channel_id=1, source_target_pairs={{0,1},{1,2},{2,3},{3,4},{4,5},{5,6},{6,7},{7,8},{8,9},{9,10},{10,1... | collective-permute-start | bytes 196616 | tf_op jit(solution)/shard_map/ppermute | solution.py:19
  28.2 1.6 %collective-permute-done = bf16[2,1,64,256]{3,2,1,0:T(8,128)(2,1)S(1)} collective-permute-done((bf16[2,1,64,256]{3,2,1,0:T(8,128)(2,1)S(1)}, bf16[2,1,64,256]{3,2,1,0:T(8,128)(2,1)S(1)}, u32[]{:S(2)}, u32[]{:S(2)}) %collective-permute-start) | collective-permute-done | bytes 65568 | tf_op jit(solution)/shard_map/ppermute | solution.py:19
  33.0 1.9 %collective-permute-start.2 = (bf16[2,4,64,256]{3,2,1,0:T(8,128)(2,1)S(1)}, bf16[2,4,64,256]{3,2,1,0:T(8,128)(2,1)S(1)}, u32[]{:S(2)}, u32[]{:S(2)}) collective-permute-start(bf16[2,4,64,256]{3,2,1,0:T(8,128)(2,1)S(1)} %fusion.11), channel_id=1, source_target_pairs={{0,96},{96,192},{192,288},{288,384},{384,480},{480,576},{576,672},... | collective-permute-start | bytes 786440 | tf_op jit(solution)/shard_map/ppermute | solution.py:31
  42.7 2.6 %concatenate.40 = f32[4,2,96,768]{3,2,1,0:T(8,128)S(1)} reshape(f32[9,256,256]{2,1,0:T(8,128)} %fusion.15) | data formatting | bytes 4718592 | tf_op jit(solution)/shard_map/concatenate | solution.py:145
  46.6 1.4 fusion.1
  48.0 1.9 %collective-permute-start.6 = (f32[4,96,1024]{2,1,0:T(8,128)}, f32[4,96,1024]{2,1,0:T(8,128)}, u32[]{:S(2)}, u32[]{:S(2)}) collective-permute-start(f32[4,96,1024]{2,1,0:T(8,128)} %fusion.1), channel_id=1, source_target_pairs={{0,96},{96,0},{192,288},{288,192},{384,480},{480,384},{576,672},{6... | collective-permute-start | bytes 4718600 | tf_op jit(solution)/shard_map/ppermute | solution.py:66
  50.0 3.7 %collective-permute-done.6 = f32[4,96,1024]{2,1,0:T(8,128)} collective-permute-done((f32[4,96,1024]{2,1,0:T(8,128)}, f32[4,96,1024]{2,1,0:T(8,128)}, u32[]{:S(2)}, u32[]{:S(2)}) %collective-permute-start.6) | collective-permute-done | bytes 1572896 | tf_op jit(solution)/shard_map/ppermute | solution.py:66
  53.7 1.6 %fusion.4 = f32[4,96,1024]{2,1,0:T(8,128)S(1)} fusion(f32[4,96,1024]{2,1,0:T(8,128)} %collective-permute-done.6, s32[]{:T(128)S(6)} %select_n.45, f32[4,2,96,768]{3,2,1,0:T(8,128)S(1)} %concatenate.40, f32[4,2,96,256]{3,2,1,0:T(8,128)S(1)} %bitcast.237), kind=kLoop, calls=%fused_computation.8 | loop fusion | flops 786432 | bytes 6291460 | tf_op jit(solution)/shard_map/add | solution.py:66
  55.3 1.2 copy-done
  56.5 3.7 %collective-permute-start.7 = (f32[2,96,1024]{2,1,0:T(8,128)S(1)}, f32[2,96,1024]{2,1,0:T(8,128)S(1)}, u32[]{:S(2)}, u32[]{:S(2)}) collective-permute-start(f32[2,96,1024]{2,1,0:T(8,128)S(1)} %dynamic-slice_bitcast_fusion), channel_id=1, source_target_pairs={{0,192},{96,288},{192,0},{288,96},{384,576},{480,672},{576,384},{6... | collective-permute-start | bytes 2359304 | tf_op jit(solution)/shard_map/ppermute | solution.py:66
  60.2 18.0 %collective-permute-done.7 = f32[2,96,1024]{2,1,0:T(8,128)S(1)} collective-permute-done((f32[2,96,1024]{2,1,0:T(8,128)S(1)}, f32[2,96,1024]{2,1,0:T(8,128)S(1)}, u32[]{:S(2)}, u32[]{:S(2)}) %collective-permute-start.7) | collective-permute-done | bytes 786464 | tf_op jit(solution)/shard_map/ppermute | solution.py:66
  78.2 1.2 bitcast_add_fusion
  79.5 8.3 %collective-permute-start.8 = (f32[1,96,1024]{2,1,0:T(8,128)S(1)}, f32[1,96,1024]{2,1,0:T(8,128)S(1)}, u32[]{:S(2)}, u32[]{:S(2)}) collective-permute-start(f32[1,96,1024]{2,1,0:T(8,128)S(1)} %constant_dynamic-slice_fusion), channel_id=1, source_target_pairs={{0,384},{96,480},{192,576},{288,672},{384,0},{480,96},{576,192},{6... | collective-permute-start | bytes 1179656 | tf_op jit(solution)/shard_map/ppermute | solution.py:66
  87.8 8.9 %collective-permute-done.8 = f32[1,96,1024]{2,1,0:T(8,128)S(1)} collective-permute-done((f32[1,96,1024]{2,1,0:T(8,128)S(1)}, f32[1,96,1024]{2,1,0:T(8,128)S(1)}, u32[]{:S(2)}, u32[]{:S(2)}) %collective-permute-start.8) | collective-permute-done | bytes 393248 | tf_op jit(solution)/shard_map/ppermute | solution.py:66
  97.9 24.1 %all-to-all-start = ((f32[96,1,1024]{2,1,0:T(1,128)}), f32[96,1,1024]{2,1,0:T(1,128)S(1)}, u32[]{:S(2)}, u32[]{:S(2)}) async-start(f32[96,1,1024]{2,1,0:T(1,128)} %copy.8), calls=%async_computation | async-start | bytes 786432 | tf_op jit(solution)/shard_map/all_to_all | solution.py:148
  123.5 21.3 %all-to-all-done = f32[96,1,1024]{2,1,0:T(1,128)S(1)} async-done(((f32[96,1,1024]{2,1,0:T(1,128)}), f32[96,1,1024]{2,1,0:T(1,128)S(1)}, u32[]{:S(2)}, u32[]{:S(2)}) %all-to-all-start) | async-done | bytes 393248 | tf_op jit(solution)/shard_map/all_to_all | solution.py:148
  (70 shorter events, 22.9 us)
Async XLA Ops:
  0.6 7.7 %copy-start.2 = (bf16[2,4,64,256]{3,2,1,0:T(8,128)(2,1)S(1)}, bf16[2,4,64,256]{3,2,1,0:T(8,128)(2,1)}, u32[]{:S(2)}) copy-start(bf16[2,4,64,256]{3,2,1,0:T(8,128)(2,1)} %param.5) | copy-start | bytes 786436
  0.6 6.5 %collective-permute-start.3 = (bf16[2,4,64,256]{3,2,1,0:T(8,128)(2,1)}, bf16[2,4,64,256]{3,2,1,0:T(8,128)(2,1)S(1)}, u32[]{:S(2)}, u32[]{:S(2)}) collective-permute-start(bf16[2,4,64,256]{3,2,1,0:T(8,128)(2,1)} %param.5), channel_id=1, source_target_pairs={{96,0},{192,96},{288,192},{384,288},{480,384},{576,480},{672,576},... | collective-permute-start | bytes 786440 | tf_op jit(solution)/shard_map/ppermute | solution.py:31
  8.3 9.2 %copy-start.1 = (bf16[3,3,256,256]{3,2,1,0:T(8,128)(2,1)S(1)}, bf16[3,3,256,256]{3,2,1,0:T(8,128)(2,1)}, u32[]{:S(2)}) copy-start(bf16[3,3,256,256]{3,2,1,0:T(8,128)(2,1)} %param.6) | copy-start | bytes 3538948
  9.6 6.2 %collective-permute-start.5 = (bf16[2,1,64,256]{3,2,1,0:T(8,128)(2,1)S(1)}, bf16[2,1,64,256]{3,2,1,0:T(8,128)(2,1)S(1)}, u32[]{:S(2)}, u32[]{:S(2)}) collective-permute-start(bf16[2,1,64,256]{3,2,1,0:T(8,128)(2,1)S(1)} %get-tuple-element.7), channel_id=1, source_target_pairs={{1,0},{2,1},{3,2},{4,3},{5,4},{6,5},{7,6},{8,7},{9,8},{10,9},{11,1... | collective-permute-start | bytes 196616 | tf_op jit(solution)/shard_map/ppermute | solution.py:21
  10.9 6.4 %collective-permute-start.4 = (bf16[2,1,64,256]{3,2,1,0:T(8,128)(2,1)S(1)}, bf16[2,1,64,256]{3,2,1,0:T(8,128)(2,1)S(1)}, u32[]{:S(2)}, u32[]{:S(2)}) collective-permute-start(bf16[2,1,64,256]{3,2,1,0:T(8,128)(2,1)S(1)} %get-tuple-element.6), channel_id=1, source_target_pairs={{0,1},{1,2},{2,3},{3,4},{4,5},{5,6},{6,7},{7,8},{8,9},{9,10},{10,1... | collective-permute-start | bytes 196616 | tf_op jit(solution)/shard_map/ppermute | solution.py:19
  19.1 1.0 copy-start.3
  21.6 6.5 %collective-permute-start.1 = (bf16[2,1,64,256]{3,2,1,0:T(8,128)(2,1)S(1)}, bf16[2,1,64,256]{3,2,1,0:T(8,128)(2,1)S(1)}, u32[]{:S(2)}, u32[]{:S(2)}) collective-permute-start(bf16[2,1,64,256]{3,2,1,0:T(8,128)(2,1)S(1)} %get-tuple-element.9), channel_id=1, source_target_pairs={{1,0},{2,1},{3,2},{4,3},{5,4},{6,5},{7,6},{8,7},{9,8},{10,9},{11,1... | collective-permute-start | bytes 196616 | tf_op jit(solution)/shard_map/ppermute | solution.py:21
  22.9 6.8 %collective-permute-start = (bf16[2,1,64,256]{3,2,1,0:T(8,128)(2,1)S(1)}, bf16[2,1,64,256]{3,2,1,0:T(8,128)(2,1)S(1)}, u32[]{:S(2)}, u32[]{:S(2)}) collective-permute-start(bf16[2,1,64,256]{3,2,1,0:T(8,128)(2,1)S(1)} %get-tuple-element.8), channel_id=1, source_target_pairs={{0,1},{1,2},{2,3},{3,4},{4,5},{5,6},{6,7},{7,8},{8,9},{9,10},{10,1... | collective-permute-start | bytes 196616 | tf_op jit(solution)/shard_map/ppermute | solution.py:19
  33.0 12.6 %collective-permute-start.2 = (bf16[2,4,64,256]{3,2,1,0:T(8,128)(2,1)S(1)}, bf16[2,4,64,256]{3,2,1,0:T(8,128)(2,1)S(1)}, u32[]{:S(2)}, u32[]{:S(2)}) collective-permute-start(bf16[2,4,64,256]{3,2,1,0:T(8,128)(2,1)S(1)} %fusion.11), channel_id=1, source_target_pairs={{0,96},{96,192},{192,288},{288,384},{384,480},{480,576},{576,672},... | collective-permute-start | bytes 786440 | tf_op jit(solution)/shard_map/ppermute | solution.py:31
  45.6 0.7 copy-start.6
  48.0 5.6 %collective-permute-start.6 = (f32[4,96,1024]{2,1,0:T(8,128)}, f32[4,96,1024]{2,1,0:T(8,128)}, u32[]{:S(2)}, u32[]{:S(2)}) collective-permute-start(f32[4,96,1024]{2,1,0:T(8,128)} %fusion.1), channel_id=1, source_target_pairs={{0,96},{96,0},{192,288},{288,192},{384,480},{480,384},{576,672},{6... | collective-permute-start | bytes 4718600 | tf_op jit(solution)/shard_map/ppermute | solution.py:66
  55.3 1.2 copy-start
  56.5 21.7 %collective-permute-start.7 = (f32[2,96,1024]{2,1,0:T(8,128)S(1)}, f32[2,96,1024]{2,1,0:T(8,128)S(1)}, u32[]{:S(2)}, u32[]{:S(2)}) collective-permute-start(f32[2,96,1024]{2,1,0:T(8,128)S(1)} %dynamic-slice_bitcast_fusion), channel_id=1, source_target_pairs={{0,192},{96,288},{192,0},{288,96},{384,576},{480,672},{576,384},{6... | collective-permute-start | bytes 2359304 | tf_op jit(solution)/shard_map/ppermute | solution.py:66
  79.5 42.5 %copy-start.5 = (bf16[3,256,256]{2,1,0:T(8,128)(2,1)S(1)}, bf16[3,256,256]{2,1,0:T(8,128)(2,1)}, u32[]{:S(2)}) copy-start(bf16[3,256,256]{2,1,0:T(8,128)(2,1)} %param.7) | copy-start | bytes 1179652
  79.5 17.2 %collective-permute-start.8 = (f32[1,96,1024]{2,1,0:T(8,128)S(1)}, f32[1,96,1024]{2,1,0:T(8,128)S(1)}, u32[]{:S(2)}, u32[]{:S(2)}) collective-permute-start(f32[1,96,1024]{2,1,0:T(8,128)S(1)} %constant_dynamic-slice_fusion), channel_id=1, source_target_pairs={{0,384},{96,480},{192,576},{288,672},{384,0},{480,96},{576,192},{6... | collective-permute-start | bytes 1179656 | tf_op jit(solution)/shard_map/ppermute | solution.py:66
  87.8 34.5 %copy-start.7 = (bf16[2,4,64,256]{3,2,1,0:T(8,128)(2,1)S(1)}, bf16[2,4,64,256]{3,2,1,0:T(8,128)(2,1)}, u32[]{:S(2)}) copy-start(bf16[2,4,64,256]{3,2,1,0:T(8,128)(2,1)} %copy-done.6) | copy-start | bytes 786436
  96.7 25.8 %copy-start.4 = (bf16[2,4,64,256]{3,2,1,0:T(8,128)(2,1)S(1)}, bf16[2,4,64,256]{3,2,1,0:T(8,128)(2,1)}, u32[]{:S(2)}) copy-start(bf16[2,4,64,256]{3,2,1,0:T(8,128)(2,1)} %param.4) | copy-start | bytes 786436
  97.9 46.8 %all-to-all-start = ((f32[96,1,1024]{2,1,0:T(1,128)}), f32[96,1,1024]{2,1,0:T(1,128)S(1)}, u32[]{:S(2)}, u32[]{:S(2)}) async-start(f32[96,1,1024]{2,1,0:T(1,128)} %copy.8), calls=%async_computation | async-start | bytes 786432 | tf_op jit(solution)/shard_map/all_to_all | solution.py:148
  145.0 0.6 copy-start.8

commit v3 on v2

--- a/solution.py
+++ b/solution.py
@@ -113,7 +113,8 @@
             for time_lag in range(3)
         ]
     )
-    grad_ext = extended(grad_mid, (("height", 1),), 1)
+    grad_mid_late, unused_history = lax.optimization_barrier((grad_mid, earlier))
+    grad_ext = extended(grad_mid_late, (("height", 1),), 1)
     grad_pad = jnp.pad(grad_ext, ((0, 0), (0, 0), (1, 1), (0, 0)))
     terms = []
     for tap_row in range(3):

time: 148 us -> 135 us (0.912); the launches traced: 146 us -> 135 us
  waiting for transfers between devices: 57.4 us -> 42.3 us
  matrix products: 19.3 us -> 25.4 us
    ppermute x3, waiting for transfers between devices: 30.6 us -> 24.9 us  [halving_scatter(): block = keep + lax.ppermute(send, axis, route)]
    dot_general x24, matrix products: 9.72 us -> 15.2 us  [flat_dot(): jnp.dot(left.reshape(-1, left.shape[-1]), weight, preferred_element_type=...]
    all_to_all x1, starting transfers between devices: 24.1 us -> 20 us  [shards(): packed = lax.all_to_all(packed, 'height', 0, 0, tiled=True)]
    all_to_all x1, waiting for transfers between devices: 21.3 us -> 17.4 us  [shards(): packed = lax.all_to_all(packed, 'height', 0, 0, tiled=True)]
    ppermute x2, waiting for transfers between devices: 3.16 us -> 0.01 us  [extended(): lax.ppermute(tail, axis, [(i, (i + 1) % count) for i in range(ends)])]
    ppermute x3, starting transfers between devices: 13.8 us -> 16.6 us  [halving_scatter(): block = keep + lax.ppermute(send, axis, route)]
    ppermute x2, waiting for transfers between devices: 1.84 us -> 0.01 us  [shifted(): return lax.ppermute(block, axis, route)]
  transfers between devices with their start and end apart: 10 -> 10, of which waited for: 9 -> 3; matrix products, arithmetic and copies ran while one was open for 10% -> 23% of each run, Pallas kernels for 0% -> 0%
where the time goes in v3:
time: 135 us
  starting transfers between devices  53 us (39%)
  waiting for transfers between devices  42.3 us (31%)
  matrix products  25.4 us (19%)
  other arithmetic  7.05 us (5%)
  local copies, waits for them, and re-layouts  5.67 us (4%)
    ppermute x3, waiting for transfers between devices, halving_scatter(): block = keep + lax.ppermute(send, axis, route)  24.9 us
    all_to_all x1, starting transfers between devices, shards(): packed = lax.all_to_all(packed, 'height', 0, 0, tiled=True)  20 us
    all_to_all x1, waiting for transfers between devices, shards(): packed = lax.all_to_all(packed, 'height', 0, 0, tiled=True)  17.4 us
    ppermute x3, starting transfers between devices, halving_scatter(): block = keep + lax.ppermute(send, axis, route)  16.6 us
    dot_general x24, matrix products, flat_dot(): jnp.dot(left.reshape(-1, left.shape[-1]), weight, preferred_element_type=...  15.2 us
    dot_general x12, matrix products, outer_sum(): lax.dot_general(left.reshape(-1, channels), right.reshape(-1, channels),...  10.2 us
    ppermute x2, starting transfers between devices, extended(): lax.ppermute(tail, axis, [(i, (i + 1) % count) for i in range(ends)])  9.23 us
    ppermute x2, starting transfers between devices, shifted(): return lax.ppermute(block, axis, route)  4.47 us
  transfers between devices with their start and end apart: 10, of which 3 were waited for; matrix products, arithmetic and copies ran while one was open for 23% of the time, Pallas kernels for 0%

profile of v3, /device:TPU:6, one launch (start us, length us, event | category | flops | bytes accessed | tf_op | source)
XLA Modules:
  0.0 134.6 jit_solution(1707453499437258845)
XLA Ops:
  0.6 1.2 fusion.35
  1.8 1.2 fusion.30
  3.0 1.3 collective-permute-start.1
  4.3 4.5 %collective-permute-start = (bf16[2,1,64,256]{3,2,1,0:T(8,128)(2,1)S(1)}, bf16[2,1,64,256]{3,2,1,0:T(8,128)(2,1)S(1)}, u32[]{:S(2)}, u32[]{:S(2)}) collective-permute-start(bf16[2,1,64,256]{3,2,1,0:T(8,128)(2,1)S(1)} %get-tuple-element.8), channel_id=1, source_target_pairs={{0,1},{1,2},{2,3},{3,4},{4,5},{5,6},{6,7},{7,8},{8,9},{9,10},{10,1... | collective-permute-start | bytes 196616 | tf_op jit(solution)/shard_map/ppermute | solution.py:19
  8.9 1.9 %collective-permute-start.3 = (bf16[2,4,64,256]{3,2,1,0:T(8,128)(2,1)}, bf16[2,4,64,256]{3,2,1,0:T(8,128)(2,1)S(1)}, u32[]{:S(2)}, u32[]{:S(2)}) collective-permute-start(bf16[2,4,64,256]{3,2,1,0:T(8,128)(2,1)} %param.5), channel_id=1, source_target_pairs={{96,0},{192,96},{288,192},{384,288},{480,384},{576,480},{672,576},... | collective-permute-start | bytes 786440 | tf_op jit(solution)/shard_map/ppermute | solution.py:31
  10.8 2.0 %fusion.94 = f32[2,4,64,256]{3,2,1,0:T(8,128)} fusion(bf16[2,4,64,256]{3,2,1,0:T(8,128)(2,1)} %param.5, bf16[3,256,256]{2,1,0:T(8,128)(2,1)} %param.7), kind=kOutput, calls=%fused_computation.144 | convolution fusion | flops 67108864 | bytes 917504 | tf_op jit(solution)/shard_map/dot_general | solution.py:41
  15.2 2.5 %collective-permute-start.2 = (bf16[2,4,64,256]{3,2,1,0:T(8,128)(2,1)S(1)}, bf16[2,4,64,256]{3,2,1,0:T(8,128)(2,1)S(1)}, u32[]{:S(2)}, u32[]{:S(2)}) collective-permute-start(bf16[2,4,64,256]{3,2,1,0:T(8,128)(2,1)S(1)} %fusion.12), channel_id=1, source_target_pairs={{0,96},{96,192},{192,288},{288,384},{384,480},{480,576},{576,672},... | collective-permute-start | bytes 786440 | tf_op jit(solution)/shard_map/ppermute | solution.py:31
  29.6 2.6 %concatenate.40 = f32[4,2,96,768]{3,2,1,0:T(8,128)S(1)} reshape(f32[9,256,256]{2,1,0:T(8,128)} %fusion.16) | data formatting | bytes 4718592 | tf_op jit(solution)/shard_map/concatenate | solution.py:146
  33.3 1.4 %fusion.1 = f32[4,96,1024]{2,1,0:T(8,128)} fusion(s32[]{:T(128)S(6)} %select_n.46, f32[4,2,96,768]{3,2,1,0:T(8,128)S(1)} %concatenate.40, f32[4,2,96,256]{3,2,1,0:T(8,128)S(1)} %bitcast.236), kind=kLoop, calls=%fused_computation.5 | loop fusion | flops 393216 | bytes 4718596 | tf_op jit(solution)/shard_map/jit(dynamic_index_in_dim)/squeeze | solution.py:64
  34.7 1.9 %collective-permute-start.6 = (f32[4,96,1024]{2,1,0:T(8,128)}, f32[4,96,1024]{2,1,0:T(8,128)}, u32[]{:S(2)}, u32[]{:S(2)}) collective-permute-start(f32[4,96,1024]{2,1,0:T(8,128)} %fusion.1), channel_id=1, source_target_pairs={{0,96},{96,0},{192,288},{288,192},{384,480},{480,384},{576,672},{6... | collective-permute-start | bytes 4718600 | tf_op jit(solution)/shard_map/ppermute | solution.py:66
  36.7 1.3 fusion.96
  38.0 1.3 collective-permute-start.5
  39.3 4.7 %collective-permute-start.4 = (bf16[2,1,64,256]{3,2,1,0:T(8,128)(2,1)S(1)}, bf16[2,1,64,256]{3,2,1,0:T(8,128)(2,1)S(1)}, u32[]{:S(2)}, u32[]{:S(2)}) collective-permute-start(bf16[2,1,64,256]{3,2,1,0:T(8,128)(2,1)S(1)} %get-tuple-element.6), channel_id=1, source_target_pairs={{0,1},{1,2},{2,3},{3,4},{4,5},{5,6},{6,7},{7,8},{8,9},{9,10},{10,1... | collective-permute-start | bytes 196616 | tf_op jit(solution)/shard_map/ppermute | solution.py:19
  44.0 1.2 fusion.90
  45.3 1.8 %fusion.11 = bf16[2,4,64,256]{3,2,1,0:T(8,128)(2,1)} fusion(f32[2,4,64,256]{3,2,1,0:T(8,128)S(1)} %fusion.90, f32[2,4,64,256]{3,2,1,0:T(8,128)S(1)} %fusion.96, bf16[2,4,64,256]{3,2,1,0:T(8,128)(2,1)S(1)} %copy-done.2, bf16[2,4,64,256]{3,2,1,0:T(8,128)(2,1)S(1)} %copy-done.7, bf16[2,4,64,256]{3,2,1,0:T(8,128)(2,1)S(1)} %copy-done.11, ...), kind=kOutput, calls=%fused_computation.32 | convolution fusion | flops 68812800 | bytes 2228224 | tf_op jit(solution)/shard_map/dot_general | solution.py:41
  47.4 1.6 %fusion.4 = f32[4,96,1024]{2,1,0:T(8,128)S(1)} fusion(f32[4,96,1024]{2,1,0:T(8,128)} %collective-permute-done.6, s32[]{:T(128)S(6)} %select_n.45, f32[4,2,96,768]{3,2,1,0:T(8,128)S(1)} %concatenate.40, f32[4,2,96,256]{3,2,1,0:T(8,128)S(1)} %bitcast.237), kind=kLoop, calls=%fused_computation.8 | loop fusion | flops 786432 | bytes 6291460 | tf_op jit(solution)/shard_map/add | solution.py:66
  49.1 3.6 %collective-permute-start.7 = (f32[2,96,1024]{2,1,0:T(8,128)S(1)}, f32[2,96,1024]{2,1,0:T(8,128)S(1)}, u32[]{:S(2)}, u32[]{:S(2)}) collective-permute-start(f32[2,96,1024]{2,1,0:T(8,128)S(1)} %dynamic-slice_bitcast_fusion), channel_id=1, source_target_pairs={{0,192},{96,288},{192,0},{288,96},{384,576},{480,672},{576,384},{6... | collective-permute-start | bytes 2359304 | tf_op jit(solution)/shard_map/ppermute | solution.py:66
  53.6 16.8 %collective-permute-done.7 = f32[2,96,1024]{2,1,0:T(8,128)S(1)} collective-permute-done((f32[2,96,1024]{2,1,0:T(8,128)S(1)}, f32[2,96,1024]{2,1,0:T(8,128)S(1)}, u32[]{:S(2)}, u32[]{:S(2)}) %collective-permute-start.7) | collective-permute-done | bytes 786464 | tf_op jit(solution)/shard_map/ppermute | solution.py:66
  70.5 11.1 %collective-permute-start.8 = (f32[1,96,1024]{2,1,0:T(8,128)S(1)}, f32[1,96,1024]{2,1,0:T(8,128)S(1)}, u32[]{:S(2)}, u32[]{:S(2)}) collective-permute-start(f32[1,96,1024]{2,1,0:T(8,128)S(1)} %constant_dynamic-slice_fusion), channel_id=1, source_target_pairs={{0,384},{96,480},{192,576},{288,672},{384,0},{480,96},{576,192},{6... | collective-permute-start | bytes 1179656 | tf_op jit(solution)/shard_map/ppermute | solution.py:66
  82.2 8.1 %collective-permute-done.8 = f32[1,96,1024]{2,1,0:T(8,128)S(1)} collective-permute-done((f32[1,96,1024]{2,1,0:T(8,128)S(1)}, f32[1,96,1024]{2,1,0:T(8,128)S(1)}, u32[]{:S(2)}, u32[]{:S(2)}) %collective-permute-start.8) | collective-permute-done | bytes 393248 | tf_op jit(solution)/shard_map/ppermute | solution.py:66
  91.6 20.0 %all-to-all-start = ((f32[96,1,1024]{2,1,0:T(1,128)}), f32[96,1,1024]{2,1,0:T(1,128)S(1)}, u32[]{:S(2)}, u32[]{:S(2)}) async-start(f32[96,1,1024]{2,1,0:T(1,128)} %copy.8), calls=%async_computation | async-start | bytes 786432 | tf_op jit(solution)/shard_map/all_to_all | solution.py:149
  112.8 1.2 convolution_add_fusion.4
  114.0 1.4 %fusion.36 = (f32[2,4,64]{2,1,0:T(4,128)S(1)}, f32[2,4,64,256]{3,2,1,0:T(8,128)S(1)}) fusion(bf16[2,4,64,256]{3,2,1,0:T(8,128)(2,1)S(1)} %copy-done.3, f32[2,4,64]{2,1,0:T(4,128)S(1)} %fusion.122, f32[2,4,64,256]{3,2,1,0:T(8,128)S(1)} %fusion.48, f32[2,4,64,256]{3,2,1,0:T(8,128)S(1)} %convolution_add_fusion.4, bf16[3,3,256,256]{3,2,1,0:T(8,128)(2,1)} %param.6, ...), kind=kOutput, calls=%fused_computation.78 | convolution fusion | flops 69729792 | bytes 2297856 | tf_op jit(solution)/shard_map/dot_general | solution.py:41
  116.4 17.4 %all-to-all-done = f32[96,1,1024]{2,1,0:T(1,128)S(1)} async-done(((f32[96,1,1024]{2,1,0:T(1,128)}), f32[96,1,1024]{2,1,0:T(1,128)S(1)}, u32[]{:S(2)}, u32[]{:S(2)}) %all-to-all-start) | async-done | bytes 393248 | tf_op jit(solution)/shard_map/all_to_all | solution.py:149
  (83 shorter events, 21.2 us)
Async XLA Ops:
  0.6 12.4 %copy-start = (bf16[3,3,256,256]{3,2,1,0:T(8,128)(2,1)S(1)}, bf16[3,3,256,256]{3,2,1,0:T(8,128)(2,1)}, u32[]{:S(2)}) copy-start(bf16[3,3,256,256]{3,2,1,0:T(8,128)(2,1)} %param.6) | copy-start | bytes 3538948
  3.0 9.8 %collective-permute-start.1 = (bf16[2,1,64,256]{3,2,1,0:T(8,128)(2,1)S(1)}, bf16[2,1,64,256]{3,2,1,0:T(8,128)(2,1)S(1)}, u32[]{:S(2)}, u32[]{:S(2)}) collective-permute-start(bf16[2,1,64,256]{3,2,1,0:T(8,128)(2,1)S(1)} %get-tuple-element.9), channel_id=1, source_target_pairs={{1,0},{2,1},{3,2},{4,3},{5,4},{6,5},{7,6},{8,7},{9,8},{10,9},{11,1... | collective-permute-start | bytes 196616 | tf_op jit(solution)/shard_map/ppermute | solution.py:21
  4.3 8.5 %collective-permute-start = (bf16[2,1,64,256]{3,2,1,0:T(8,128)(2,1)S(1)}, bf16[2,1,64,256]{3,2,1,0:T(8,128)(2,1)S(1)}, u32[]{:S(2)}, u32[]{:S(2)}) collective-permute-start(bf16[2,1,64,256]{3,2,1,0:T(8,128)(2,1)S(1)} %get-tuple-element.8), channel_id=1, source_target_pairs={{0,1},{1,2},{2,3},{3,4},{4,5},{5,6},{6,7},{7,8},{8,9},{9,10},{10,1... | collective-permute-start | bytes 196616 | tf_op jit(solution)/shard_map/ppermute | solution.py:19
  8.9 9.8 %collective-permute-start.3 = (bf16[2,4,64,256]{3,2,1,0:T(8,128)(2,1)}, bf16[2,4,64,256]{3,2,1,0:T(8,128)(2,1)S(1)}, u32[]{:S(2)}, u32[]{:S(2)}) collective-permute-start(bf16[2,4,64,256]{3,2,1,0:T(8,128)(2,1)} %param.5), channel_id=1, source_target_pairs={{96,0},{192,96},{288,192},{384,288},{480,384},{576,480},{672,576},... | collective-permute-start | bytes 786440 | tf_op jit(solution)/shard_map/ppermute | solution.py:31
  14.7 3.1 %copy-start.4 = (bf16[2,4,64,256]{3,2,1,0:T(8,128)(2,1)S(1)}, bf16[2,4,64,256]{3,2,1,0:T(8,128)(2,1)}, u32[]{:S(2)}) copy-start(bf16[2,4,64,256]{3,2,1,0:T(8,128)(2,1)} %param.5) | copy-start | bytes 786436
  14.9 4.5 %copy-start.9 = (bf16[3,256,256]{2,1,0:T(8,128)(2,1)S(1)}, bf16[3,256,256]{2,1,0:T(8,128)(2,1)}, u32[]{:S(2)}) copy-start(bf16[3,256,256]{2,1,0:T(8,128)(2,1)} %param.7) | copy-start | bytes 1179652
  14.9 4.8 %copy-start.8 = (f32[2,4,64,256]{3,2,1,0:T(8,128)S(1)}, f32[2,4,64,256]{3,2,1,0:T(8,128)}, u32[]{:S(2)}) copy-start(f32[2,4,64,256]{3,2,1,0:T(8,128)} %fusion.94) | copy-start | bytes 1572868
  15.2 17.3 %copy-start.6 = (bf16[2,4,64,256]{3,2,1,0:T(8,128)(2,1)}, bf16[2,4,64,256]{3,2,1,0:T(8,128)(2,1)S(1)}, u32[]{:S(2)}) copy-start(bf16[2,4,64,256]{3,2,1,0:T(8,128)(2,1)S(1)} %fusion.12) | copy-start | bytes 786436
  15.2 17.0 %collective-permute-start.2 = (bf16[2,4,64,256]{3,2,1,0:T(8,128)(2,1)S(1)}, bf16[2,4,64,256]{3,2,1,0:T(8,128)(2,1)S(1)}, u32[]{:S(2)}, u32[]{:S(2)}) collective-permute-start(bf16[2,4,64,256]{3,2,1,0:T(8,128)(2,1)S(1)} %fusion.12), channel_id=1, source_target_pairs={{0,96},{96,192},{192,288},{288,384},{384,480},{480,576},{576,672},... | collective-permute-start | bytes 786440 | tf_op jit(solution)/shard_map/ppermute | solution.py:31
  18.7 0.7 copy-start.12
  32.2 1.0 copy-start.13
  32.2 0.7 copy-start.10
  34.7 12.7 %collective-permute-start.6 = (f32[4,96,1024]{2,1,0:T(8,128)}, f32[4,96,1024]{2,1,0:T(8,128)}, u32[]{:S(2)}, u32[]{:S(2)}) collective-permute-start(f32[4,96,1024]{2,1,0:T(8,128)} %fusion.1), channel_id=1, source_target_pairs={{0,96},{96,0},{192,288},{288,192},{384,480},{480,384},{576,672},{6... | collective-permute-start | bytes 4718600 | tf_op jit(solution)/shard_map/ppermute | solution.py:66
  36.7 8.5 %copy-start.2 = (bf16[2,4,64,256]{3,2,1,0:T(8,128)(2,1)S(1)}, bf16[2,4,64,256]{3,2,1,0:T(8,128)(2,1)}, u32[]{:S(2)}) copy-start(bf16[2,4,64,256]{3,2,1,0:T(8,128)(2,1)} %param.4) | copy-start | bytes 786436
  36.7 8.5 %copy-start.7 = (bf16[2,4,64,256]{3,2,1,0:T(8,128)(2,1)S(1)}, bf16[2,4,64,256]{3,2,1,0:T(8,128)(2,1)}, u32[]{:S(2)}) copy-start(bf16[2,4,64,256]{3,2,1,0:T(8,128)(2,1)} %copy-done.6) | copy-start | bytes 786436
  36.7 8.5 %copy-start.11 = (bf16[2,4,64,256]{3,2,1,0:T(8,128)(2,1)S(1)}, bf16[2,4,64,256]{3,2,1,0:T(8,128)(2,1)}, u32[]{:S(2)}) copy-start(bf16[2,4,64,256]{3,2,1,0:T(8,128)(2,1)} %copy-done.10) | copy-start | bytes 786436
  38.0 9.1 %collective-permute-start.5 = (bf16[2,1,64,256]{3,2,1,0:T(8,128)(2,1)S(1)}, bf16[2,1,64,256]{3,2,1,0:T(8,128)(2,1)S(1)}, u32[]{:S(2)}, u32[]{:S(2)}) collective-permute-start(bf16[2,1,64,256]{3,2,1,0:T(8,128)(2,1)S(1)} %get-tuple-element.7), channel_id=1, source_target_pairs={{1,0},{2,1},{3,2},{4,3},{5,4},{6,5},{7,6},{8,7},{9,8},{10,9},{11,1... | collective-permute-start | bytes 196616 | tf_op jit(solution)/shard_map/ppermute | solution.py:21
  39.3 7.8 %copy-start.1 = (bf16[3,3,256,256]{3,2,1,0:T(8,128)(2,1)S(1)}, bf16[3,3,256,256]{3,2,1,0:T(8,128)(2,1)}, u32[]{:S(2)}) copy-start(bf16[3,3,256,256]{3,2,1,0:T(8,128)(2,1)} %param.6) | copy-start | bytes 3538948
  39.3 13.3 %collective-permute-start.4 = (bf16[2,1,64,256]{3,2,1,0:T(8,128)(2,1)S(1)}, bf16[2,1,64,256]{3,2,1,0:T(8,128)(2,1)S(1)}, u32[]{:S(2)}, u32[]{:S(2)}) collective-permute-start(bf16[2,1,64,256]{3,2,1,0:T(8,128)(2,1)S(1)} %get-tuple-element.6), channel_id=1, source_target_pairs={{0,1},{1,2},{2,3},{3,4},{4,5},{5,6},{6,7},{7,8},{8,9},{9,10},{10,1... | collective-permute-start | bytes 196616 | tf_op jit(solution)/shard_map/ppermute | solution.py:19
  49.1 21.3 %collective-permute-start.7 = (f32[2,96,1024]{2,1,0:T(8,128)S(1)}, f32[2,96,1024]{2,1,0:T(8,128)S(1)}, u32[]{:S(2)}, u32[]{:S(2)}) collective-permute-start(f32[2,96,1024]{2,1,0:T(8,128)S(1)} %dynamic-slice_bitcast_fusion), channel_id=1, source_target_pairs={{0,192},{96,288},{192,0},{288,96},{384,576},{480,672},{576,384},{6... | collective-permute-start | bytes 2359304 | tf_op jit(solution)/shard_map/ppermute | solution.py:66
  70.5 19.8 %collective-permute-start.8 = (f32[1,96,1024]{2,1,0:T(8,128)S(1)}, f32[1,96,1024]{2,1,0:T(8,128)S(1)}, u32[]{:S(2)}, u32[]{:S(2)}) collective-permute-start(f32[1,96,1024]{2,1,0:T(8,128)S(1)} %constant_dynamic-slice_fusion), channel_id=1, source_target_pairs={{0,384},{96,480},{192,576},{288,672},{384,0},{480,96},{576,192},{6... | collective-permute-start | bytes 1179656 | tf_op jit(solution)/shard_map/ppermute | solution.py:66
  91.6 22.4 %copy-start.3 = (bf16[2,4,64,256]{3,2,1,0:T(8,128)(2,1)S(1)}, bf16[2,4,64,256]{3,2,1,0:T(8,128)(2,1)}, u32[]{:S(2)}) copy-start(bf16[2,4,64,256]{3,2,1,0:T(8,128)(2,1)} %param.4) | copy-start | bytes 786436
  91.6 42.2 %all-to-all-start = ((f32[96,1,1024]{2,1,0:T(1,128)}), f32[96,1,1024]{2,1,0:T(1,128)S(1)}, u32[]{:S(2)}, u32[]{:S(2)}) async-start(f32[96,1,1024]{2,1,0:T(1,128)} %copy.8), calls=%async_computation | async-start | bytes 786432 | tf_op jit(solution)/shard_map/all_to_all | solution.py:149
  114.0 1.5 %copy-start.5 = (bf16[2,4,64,256]{3,2,1,0:T(8,128)(2,1)S(1)}, bf16[2,4,64,256]{3,2,1,0:T(8,128)(2,1)}, u32[]{:S(2)}) copy-start(bf16[2,4,64,256]{3,2,1,0:T(8,128)(2,1)} %param.5) | copy-start | bytes 786436
  (1 other events, 0.6 us)

commit v4 on v2

--- a/solution.py
+++ b/solution.py
@@ -52,7 +52,7 @@
     )
 
 
-def halving_scatter(block, axis):
+def halving_scatter(block, axis, tie=None, tie_after=0):
     count = lax.axis_size(axis)
     index = lax.axis_index(axis)
     step = 1
@@ -64,6 +64,8 @@
         send = lax.dynamic_index_in_dim(pairs, 1 - mine, axis=1, keepdims=False)
         route = [(i, i ^ step) for i in range(count)]
         block = keep + lax.ppermute(send, axis, route)
+        if tie is not None and step == 1 << tie_after:
+            block, tie = lax.optimization_barrier((block, tie))
         step *= 2
     ways = count // step
     if ways > 1:
@@ -74,7 +76,7 @@
             row = lax.dynamic_index_in_dim(block, (group + shift) % ways, axis=0, keepdims=True)
             total = total + lax.ppermute(row, axis, route)
         block = total
-    return block
+    return block, tie
 
 
 def shards(clip, cotangent, spatial_weight, temporal_weight):
@@ -113,8 +115,6 @@
             for time_lag in range(3)
         ]
     )
-    grad_ext = extended(grad_mid, (("height", 1),), 1)
-    grad_pad = jnp.pad(grad_ext, ((0, 0), (0, 0), (1, 1), (0, 0)))
     terms = []
     for tap_row in range(3):
         for tap_col in range(3):
@@ -125,6 +125,19 @@
                 )
             )
     grad_spatial = jnp.stack(terms)
+    grad_mid_late, unused_history = lax.optimization_barrier((grad_mid, earlier))
+    time_shards = lax.axis_size("tm")
+    row_shards = lax.axis_size("height")
+    grad_scale = 1.0 / math.sqrt(frame_count * time_shards * row_count * row_shards * col_count)
+    devices = time_shards * row_shards
+    spatial_rows = grad_spatial.reshape(devices, -1)
+    temporal_rows = grad_temporal.reshape(devices, -1)
+    packed = jnp.concatenate([spatial_rows, temporal_rows], axis=1)
+    packed = packed.reshape(time_shards, row_shards, packed.shape[-1])
+    packed, grad_mid_late = halving_scatter(packed, "tm", grad_mid_late, 1)
+    packed = packed[0]
+    grad_ext = extended(grad_mid_late, (("height", 1),), 1)
+    grad_pad = jnp.pad(grad_ext, ((0, 0), (0, 0), (1, 1), (0, 0)))
     grad_act = jnp.zeros(clip.shape, jnp.float32)
     for tap_row in range(3):
         for tap_col in range(3):
@@ -136,15 +149,6 @@
             )
     unused, pullback = jax.vjp(activate, clip_wide)
     grad_clip = (cotangent.astype(jnp.float32) + pullback(grad_act)[0]).astype(jnp.bfloat16)
-    time_shards = lax.axis_size("tm")
-    row_shards = lax.axis_size("height")
-    grad_scale = 1.0 / math.sqrt(frame_count * time_shards * row_count * row_shards * col_count)
-    devices = time_shards * row_shards
-    spatial_rows = grad_spatial.reshape(devices, -1)
-    temporal_rows = grad_temporal.reshape(devices, -1)
-    packed = jnp.concatenate([spatial_rows, temporal_rows], axis=1)
-    packed = packed.reshape(time_shards, row_shards, packed.shape[-1])
-    packed = halving_scatter(packed, "tm")[0]
     packed = lax.all_to_all(packed, "height", 0, 0, tiled=True)
     packed = jnp.sum(packed, axis=0)
     packed = packed * grad_scale

time: 148 us -> 134 us (0.905)
  waiting for transfers between devices: 57.4 us -> 46.6 us
  starting transfers between devices: 54.2 us -> 49.7 us
    ppermute x3, waiting for transfers between devices: 30.6 us -> 26.3 us  [halving_scatter(): block = keep + lax.ppermute(send, axis, route)]
    ppermute x2, waiting for transfers between devices: 3.16 us -> 0.01 us  [extended(): lax.ppermute(tail, axis, [(i, (i + 1) % count) for i in range(ends)])]
    all_to_all x1, starting transfers between devices: 24.1 us -> 21.1 us  [shards(): packed = lax.all_to_all(packed, 'height', 0, 0, tiled=True)]
    ppermute x2, starting transfers between devices: 9.44 us -> 7.4 us  [extended(): lax.ppermute(tail, axis, [(i, (i + 1) % count) for i in range(ends)])]
    all_to_all x1, waiting for transfers between devices: 21.3 us -> 19.4 us  [shards(): packed = lax.all_to_all(packed, 'height', 0, 0, tiled=True)]
    ppermute x2, waiting for transfers between devices: 1.84 us -> 0.01 us  [shifted(): return lax.ppermute(block, axis, route)]
  transfers between devices with their start and end apart: 10 -> 10, of which waited for: 9 -> 5; matrix products, arithmetic and copies ran while one was open for 10% -> 18% of each run, Pallas kernels for 0% -> 0%
where the time goes in v4:
time: 134 us; the launch traced here: 132 us
  starting transfers between devices  49.7 us (37%)
  waiting for transfers between devices  46.6 us (35%)
  matrix products  20.5 us (15%)
  local copies, waits for them, and re-layouts  7.2 us (5%)
  other arithmetic  7.01 us (5%)
    ppermute x3, waiting for transfers between devices, halving_scatter(): block = keep + lax.ppermute(send, axis, route)  26.3 us
    all_to_all x1, starting transfers between devices, shards(): packed = lax.all_to_all(packed, 'height', 0, 0, tiled=True)  21.1 us
    all_to_all x1, waiting for transfers between devices, shards(): packed = lax.all_to_all(packed, 'height', 0, 0, tiled=True)  19.4 us
    ppermute x3, starting transfers between devices, halving_scatter(): block = keep + lax.ppermute(send, axis, route)  14.7 us
    dot_general x24, matrix products, flat_dot(): jnp.dot(left.reshape(-1, left.shape[-1]), weight, preferred_element_type=...  10.3 us
    dot_general x12, matrix products, outer_sum(): lax.dot_general(left.reshape(-1, channels), right.reshape(-1, channels),...  10.2 us
    ppermute x2, starting transfers between devices, extended(): lax.ppermute(tail, axis, [(i, (i + 1) % count) for i in range(ends)])  7.4 us
    ppermute x2, starting transfers between devices, shifted(): return lax.ppermute(block, axis, route)  3.97 us
  transfers between devices with their start and end apart: 10, of which 5 were waited for; matrix products, arithmetic and copies ran while one was open for 18% of the time, Pallas kernels for 0%

profile of v4, /device:TPU:6, one launch (start us, length us, event | category | flops | bytes accessed | tf_op | source)
XLA Modules:
  0.0 132.2 jit_solution(17869632757828139151)
XLA Ops:
  0.6 1.2 fusion.34
  1.8 1.2 fusion.29
  3.0 3.5 %collective-permute-start = (bf16[2,1,64,256]{3,2,1,0:T(8,128)(2,1)S(1)}, bf16[2,1,64,256]{3,2,1,0:T(8,128)(2,1)S(1)}, u32[]{:S(2)}, u32[]{:S(2)}) collective-permute-start(bf16[2,1,64,256]{3,2,1,0:T(8,128)(2,1)S(1)} %get-tuple-element.12), channel_id=1, source_target_pairs={{0,1},{1,2},{2,3},{3,4},{4,5},{5,6},{6,7},{7,8},{8,9},{9,10},{10,1... | collective-permute-start | bytes 196616 | tf_op jit(solution)/shard_map/ppermute | solution.py:19
  6.5 1.3 collective-permute-start.1
  7.8 1.9 %collective-permute-start.3 = (bf16[2,4,64,256]{3,2,1,0:T(8,128)(2,1)}, bf16[2,4,64,256]{3,2,1,0:T(8,128)(2,1)S(1)}, u32[]{:S(2)}, u32[]{:S(2)}) collective-permute-start(bf16[2,4,64,256]{3,2,1,0:T(8,128)(2,1)} %param.5), channel_id=1, source_target_pairs={{96,0},{192,96},{288,192},{384,288},{480,384},{576,480},{672,576},... | collective-permute-start | bytes 786440 | tf_op jit(solution)/shard_map/ppermute | solution.py:31
  9.8 2.0 %fusion.92 = f32[2,4,64,256]{3,2,1,0:T(8,128)} fusion(bf16[2,4,64,256]{3,2,1,0:T(8,128)(2,1)} %param.5, bf16[3,256,256]{2,1,0:T(8,128)(2,1)} %param.7), kind=kOutput, calls=%fused_computation.143 | convolution fusion | flops 67108864 | bytes 917504 | tf_op jit(solution)/shard_map/dot_general | solution.py:41
  15.0 2.1 %collective-permute-start.2 = (bf16[2,4,64,256]{3,2,1,0:T(8,128)(2,1)S(1)}, bf16[2,4,64,256]{3,2,1,0:T(8,128)(2,1)S(1)}, u32[]{:S(2)}, u32[]{:S(2)}) collective-permute-start(bf16[2,4,64,256]{3,2,1,0:T(8,128)(2,1)S(1)} %fusion.11), channel_id=1, source_target_pairs={{0,96},{96,192},{192,288},{288,384},{384,480},{480,576},{576,672},... | collective-permute-start | bytes 786440 | tf_op jit(solution)/shard_map/ppermute | solution.py:31
  19.0 1.2 fusion.12
  28.9 2.6 %concatenate.37 = f32[4,2,96,768]{3,2,1,0:T(8,128)S(1)} reshape(f32[9,256,256]{2,1,0:T(8,128)} %fusion.15) | data formatting | bytes 4718592 | tf_op jit(solution)/shard_map/concatenate | solution.py:135
  32.5 1.4 %fusion.1 = f32[4,96,1024]{2,1,0:T(8,128)} fusion(s32[]{:T(128)S(6)} %select_n.46, f32[4,2,96,768]{3,2,1,0:T(8,128)S(1)} %concatenate.37, f32[4,2,96,256]{3,2,1,0:T(8,128)S(1)} %bitcast.236), kind=kLoop, calls=%fused_computation.5 | loop fusion | flops 393216 | bytes 4718596 | tf_op jit(solution)/shard_map/jit(dynamic_index_in_dim)/squeeze | solution.py:64
  33.9 1.9 %collective-permute-start.4 = (f32[4,96,1024]{2,1,0:T(8,128)}, f32[4,96,1024]{2,1,0:T(8,128)}, u32[]{:S(2)}, u32[]{:S(2)}) collective-permute-start(f32[4,96,1024]{2,1,0:T(8,128)} %fusion.1), channel_id=1, source_target_pairs={{0,96},{96,0},{192,288},{288,192},{384,480},{480,384},{576,672},{6... | collective-permute-start | bytes 4718600 | tf_op jit(solution)/shard_map/ppermute | solution.py:66
  35.9 3.7 %collective-permute-done.4 = f32[4,96,1024]{2,1,0:T(8,128)} collective-permute-done((f32[4,96,1024]{2,1,0:T(8,128)}, f32[4,96,1024]{2,1,0:T(8,128)}, u32[]{:S(2)}, u32[]{:S(2)}) %collective-permute-start.4) | collective-permute-done | bytes 1572896 | tf_op jit(solution)/shard_map/ppermute | solution.py:66
  39.6 1.6 %fusion.4 = f32[4,96,1024]{2,1,0:T(8,128)S(1)} fusion(f32[4,96,1024]{2,1,0:T(8,128)} %collective-permute-done.4, s32[]{:T(128)S(6)} %select_n.45, f32[4,2,96,768]{3,2,1,0:T(8,128)S(1)} %concatenate.37, f32[4,2,96,256]{3,2,1,0:T(8,128)S(1)} %bitcast.237), kind=kLoop, calls=%fused_computation.8 | loop fusion | flops 786432 | bytes 6291460 | tf_op jit(solution)/shard_map/add | solution.py:66
  41.2 1.1 copy-done
  42.4 3.8 %collective-permute-start.5 = (f32[2,96,1024]{2,1,0:T(8,128)S(1)}, f32[2,96,1024]{2,1,0:T(8,128)S(1)}, u32[]{:S(2)}, u32[]{:S(2)}) collective-permute-start(f32[2,96,1024]{2,1,0:T(8,128)S(1)} %dynamic-slice_bitcast_fusion), channel_id=1, source_target_pairs={{0,192},{96,288},{192,0},{288,96},{384,576},{480,672},{576,384},{6... | collective-permute-start | bytes 2359304 | tf_op jit(solution)/shard_map/ppermute | solution.py:66
  47.7 16.6 %collective-permute-done.5 = f32[2,96,1024]{2,1,0:T(8,128)S(1)} collective-permute-done((f32[2,96,1024]{2,1,0:T(8,128)S(1)}, f32[2,96,1024]{2,1,0:T(8,128)S(1)}, u32[]{:S(2)}, u32[]{:S(2)}) %collective-permute-start.5) | collective-permute-done | bytes 786464 | tf_op jit(solution)/shard_map/ppermute | solution.py:66
  64.4 3.9 %collective-permute-start.6 = (bf16[2,1,64,256]{3,2,1,0:T(8,128)(2,1)S(1)}, bf16[2,1,64,256]{3,2,1,0:T(8,128)(2,1)S(1)}, u32[]{:S(2)}, u32[]{:S(2)}) collective-permute-start(bf16[2,1,64,256]{3,2,1,0:T(8,128)(2,1)S(1)} %get-tuple-element.10), channel_id=1, source_target_pairs={{0,1},{1,2},{2,3},{3,4},{4,5},{5,6},{6,7},{7,8},{8,9},{9,10},{10,1... | collective-permute-start | bytes 196616 | tf_op jit(solution)/shard_map/ppermute | solution.py:19
  68.3 1.3 collective-permute-start.7
  69.7 8.9 %collective-permute-start.8 = (f32[1,96,1024]{2,1,0:T(8,128)S(1)}, f32[1,96,1024]{2,1,0:T(8,128)S(1)}, u32[]{:S(2)}, u32[]{:S(2)}) collective-permute-start(f32[1,96,1024]{2,1,0:T(8,128)S(1)} %constant_dynamic-slice_fusion), channel_id=1, source_target_pairs={{0,384},{96,480},{192,576},{288,672},{384,0},{480,96},{576,192},{6... | collective-permute-start | bytes 1179656 | tf_op jit(solution)/shard_map/ppermute | solution.py:66
  80.1 1.1 convolution_add_fusion.5
  81.2 6.0 %collective-permute-done.8 = f32[1,96,1024]{2,1,0:T(8,128)S(1)} collective-permute-done((f32[1,96,1024]{2,1,0:T(8,128)S(1)}, f32[1,96,1024]{2,1,0:T(8,128)S(1)}, u32[]{:S(2)}, u32[]{:S(2)}) %collective-permute-start.8) | collective-permute-done | bytes 393248 | tf_op jit(solution)/shard_map/ppermute | solution.py:66
  87.3 1.2 copy.8
  88.5 21.1 %all-to-all-start = ((f32[96,1,1024]{2,1,0:T(1,128)}), f32[96,1,1024]{2,1,0:T(1,128)S(1)}, u32[]{:S(2)}, u32[]{:S(2)}) async-start(f32[96,1,1024]{2,1,0:T(1,128)} %copy.8), calls=%async_computation | async-start | bytes 786432 | tf_op jit(solution)/shard_map/all_to_all | solution.py:152
  112.0 19.4 %all-to-all-done = f32[96,1,1024]{2,1,0:T(1,128)S(1)} async-done(((f32[96,1,1024]{2,1,0:T(1,128)}), f32[96,1,1024]{2,1,0:T(1,128)S(1)}, u32[]{:S(2)}, u32[]{:S(2)}) %all-to-all-start) | async-done | bytes 393248 | tf_op jit(solution)/shard_map/all_to_all | solution.py:152
  (89 shorter events, 21.1 us)
Async XLA Ops:
  0.6 12.2 %copy-start.2 = (bf16[3,3,256,256]{3,2,1,0:T(8,128)(2,1)S(1)}, bf16[3,3,256,256]{3,2,1,0:T(8,128)(2,1)}, u32[]{:S(2)}) copy-start(bf16[3,3,256,256]{3,2,1,0:T(8,128)(2,1)} %param.6) | copy-start | bytes 3538948
  3.0 8.8 %collective-permute-start = (bf16[2,1,64,256]{3,2,1,0:T(8,128)(2,1)S(1)}, bf16[2,1,64,256]{3,2,1,0:T(8,128)(2,1)S(1)}, u32[]{:S(2)}, u32[]{:S(2)}) collective-permute-start(bf16[2,1,64,256]{3,2,1,0:T(8,128)(2,1)S(1)} %get-tuple-element.12), channel_id=1, source_target_pairs={{0,1},{1,2},{2,3},{3,4},{4,5},{5,6},{6,7},{7,8},{8,9},{9,10},{10,1... | collective-permute-start | bytes 196616 | tf_op jit(solution)/shard_map/ppermute | solution.py:19
  6.5 6.2 %collective-permute-start.1 = (bf16[2,1,64,256]{3,2,1,0:T(8,128)(2,1)S(1)}, bf16[2,1,64,256]{3,2,1,0:T(8,128)(2,1)S(1)}, u32[]{:S(2)}, u32[]{:S(2)}) collective-permute-start(bf16[2,1,64,256]{3,2,1,0:T(8,128)(2,1)S(1)} %get-tuple-element.13), channel_id=1, source_target_pairs={{1,0},{2,1},{3,2},{4,3},{5,4},{6,5},{7,6},{8,7},{9,8},{10,9},{11,1... | collective-permute-start | bytes 196616 | tf_op jit(solution)/shard_map/ppermute | solution.py:21
  7.8 10.2 %collective-permute-start.3 = (bf16[2,4,64,256]{3,2,1,0:T(8,128)(2,1)}, bf16[2,4,64,256]{3,2,1,0:T(8,128)(2,1)S(1)}, u32[]{:S(2)}, u32[]{:S(2)}) collective-permute-start(bf16[2,4,64,256]{3,2,1,0:T(8,128)(2,1)} %param.5), channel_id=1, source_target_pairs={{96,0},{192,96},{288,192},{384,288},{480,384},{576,480},{672,576},... | collective-permute-start | bytes 786440 | tf_op jit(solution)/shard_map/ppermute | solution.py:31
  14.5 2.6 %copy-start.5 = (bf16[2,4,64,256]{3,2,1,0:T(8,128)(2,1)S(1)}, bf16[2,4,64,256]{3,2,1,0:T(8,128)(2,1)}, u32[]{:S(2)}) copy-start(bf16[2,4,64,256]{3,2,1,0:T(8,128)(2,1)} %param.5) | copy-start | bytes 786436
  14.7 4.0 %copy-start.11 = (bf16[3,256,256]{2,1,0:T(8,128)(2,1)S(1)}, bf16[3,256,256]{2,1,0:T(8,128)(2,1)}, u32[]{:S(2)}) copy-start(bf16[3,256,256]{2,1,0:T(8,128)(2,1)} %param.7) | copy-start | bytes 1179652
  14.7 4.3 %copy-start.9 = (f32[2,4,64,256]{3,2,1,0:T(8,128)S(1)}, f32[2,4,64,256]{3,2,1,0:T(8,128)}, u32[]{:S(2)}) copy-start(f32[2,4,64,256]{3,2,1,0:T(8,128)} %fusion.92) | copy-start | bytes 1572868
  15.0 16.8 %copy-start.7 = (bf16[2,4,64,256]{3,2,1,0:T(8,128)(2,1)}, bf16[2,4,64,256]{3,2,1,0:T(8,128)(2,1)S(1)}, u32[]{:S(2)}) copy-start(bf16[2,4,64,256]{3,2,1,0:T(8,128)(2,1)S(1)} %fusion.11) | copy-start | bytes 786436
  15.0 16.5 %collective-permute-start.2 = (bf16[2,4,64,256]{3,2,1,0:T(8,128)(2,1)S(1)}, bf16[2,4,64,256]{3,2,1,0:T(8,128)(2,1)S(1)}, u32[]{:S(2)}, u32[]{:S(2)}) collective-permute-start(bf16[2,4,64,256]{3,2,1,0:T(8,128)(2,1)S(1)} %fusion.11), channel_id=1, source_target_pairs={{0,96},{96,192},{192,288},{288,384},{384,480},{480,576},{576,672},... | collective-permute-start | bytes 786440 | tf_op jit(solution)/shard_map/ppermute | solution.py:31
  31.4 1.0 copy-start.16
  33.9 5.6 %collective-permute-start.4 = (f32[4,96,1024]{2,1,0:T(8,128)}, f32[4,96,1024]{2,1,0:T(8,128)}, u32[]{:S(2)}, u32[]{:S(2)}) collective-permute-start(f32[4,96,1024]{2,1,0:T(8,128)} %fusion.1), channel_id=1, source_target_pairs={{0,96},{96,0},{192,288},{288,192},{384,480},{480,384},{576,672},{6... | collective-permute-start | bytes 4718600 | tf_op jit(solution)/shard_map/ppermute | solution.py:66
  41.2 1.2 copy-start
  41.2 5.1 %copy-start.8 = (bf16[2,4,64,256]{3,2,1,0:T(8,128)(2,1)S(1)}, bf16[2,4,64,256]{3,2,1,0:T(8,128)(2,1)}, u32[]{:S(2)}) copy-start(bf16[2,4,64,256]{3,2,1,0:T(8,128)(2,1)} %copy-done.7) | copy-start | bytes 786436
  41.2 5.1 %copy-start.12 = (bf16[3,256,256]{2,1,0:T(8,128)(2,1)S(1)}, bf16[3,256,256]{2,1,0:T(8,128)(2,1)}, u32[]{:S(2)}) copy-start(bf16[3,256,256]{2,1,0:T(8,128)(2,1)} %param.7) | copy-start | bytes 1179652
  41.2 5.3 %copy-start.14 = (bf16[2,4,64,256]{3,2,1,0:T(8,128)(2,1)S(1)}, bf16[2,4,64,256]{3,2,1,0:T(8,128)(2,1)}, u32[]{:S(2)}) copy-start(bf16[2,4,64,256]{3,2,1,0:T(8,128)(2,1)} %copy-done.13) | copy-start | bytes 786436
  42.3 4.4 %copy-start.4 = (bf16[2,4,64,256]{3,2,1,0:T(8,128)(2,1)S(1)}, bf16[2,4,64,256]{3,2,1,0:T(8,128)(2,1)}, u32[]{:S(2)}) copy-start(bf16[2,4,64,256]{3,2,1,0:T(8,128)(2,1)} %param.4) | copy-start | bytes 786436
  42.4 21.9 %collective-permute-start.5 = (f32[2,96,1024]{2,1,0:T(8,128)S(1)}, f32[2,96,1024]{2,1,0:T(8,128)S(1)}, u32[]{:S(2)}, u32[]{:S(2)}) collective-permute-start(f32[2,96,1024]{2,1,0:T(8,128)S(1)} %dynamic-slice_bitcast_fusion), channel_id=1, source_target_pairs={{0,192},{96,288},{192,0},{288,96},{384,576},{480,672},{576,384},{6... | collective-permute-start | bytes 2359304 | tf_op jit(solution)/shard_map/ppermute | solution.py:66
  46.5 17.8 %copy-start.1 = (f32[4,96,1024]{2,1,0:T(8,128)S(1)}, f32[4,96,1024]{2,1,0:T(8,128)}, u32[]{:S(2)}) copy-start(f32[4,96,1024]{2,1,0:T(8,128)} %copy-done) | copy-start | bytes 4718596
  47.7 30.9 %copy-start.3 = (bf16[3,3,256,256]{3,2,1,0:T(8,128)(2,1)S(1)}, bf16[3,3,256,256]{3,2,1,0:T(8,128)(2,1)}, u32[]{:S(2)}) copy-start(bf16[3,3,256,256]{3,2,1,0:T(8,128)(2,1)} %param.6) | copy-start | bytes 3538948
  64.4 14.5 %collective-permute-start.6 = (bf16[2,1,64,256]{3,2,1,0:T(8,128)(2,1)S(1)}, bf16[2,1,64,256]{3,2,1,0:T(8,128)(2,1)S(1)}, u32[]{:S(2)}, u32[]{:S(2)}) collective-permute-start(bf16[2,1,64,256]{3,2,1,0:T(8,128)(2,1)S(1)} %get-tuple-element.10), channel_id=1, source_target_pairs={{0,1},{1,2},{2,3},{3,4},{4,5},{5,6},{6,7},{7,8},{8,9},{9,10},{10,1... | collective-permute-start | bytes 196616 | tf_op jit(solution)/shard_map/ppermute | solution.py:19
  68.3 10.3 %collective-permute-start.7 = (bf16[2,1,64,256]{3,2,1,0:T(8,128)(2,1)S(1)}, bf16[2,1,64,256]{3,2,1,0:T(8,128)(2,1)S(1)}, u32[]{:S(2)}, u32[]{:S(2)}) collective-permute-start(bf16[2,1,64,256]{3,2,1,0:T(8,128)(2,1)S(1)} %get-tuple-element.11), channel_id=1, source_target_pairs={{1,0},{2,1},{3,2},{4,3},{5,4},{6,5},{7,6},{8,7},{9,8},{10,9},{11,1... | collective-permute-start | bytes 196616 | tf_op jit(solution)/shard_map/ppermute | solution.py:21
  69.7 17.6 %collective-permute-start.8 = (f32[1,96,1024]{2,1,0:T(8,128)S(1)}, f32[1,96,1024]{2,1,0:T(8,128)S(1)}, u32[]{:S(2)}, u32[]{:S(2)}) collective-permute-start(f32[1,96,1024]{2,1,0:T(8,128)S(1)} %constant_dynamic-slice_fusion), channel_id=1, source_target_pairs={{0,384},{96,480},{192,576},{288,672},{384,0},{480,96},{576,192},{6... | collective-permute-start | bytes 1179656 | tf_op jit(solution)/shard_map/ppermute | solution.py:66
  87.3 22.5 %copy-start.10 = (f32[2,4,64,256]{3,2,1,0:T(8,128)S(1)}, f32[2,4,64,256]{3,2,1,0:T(8,128)}, u32[]{:S(2)}) copy-start(f32[2,4,64,256]{3,2,1,0:T(8,128)} %convolution_add_fusion.5) | copy-start | bytes 1572868
  88.5 42.9 %all-to-all-start = ((f32[96,1,1024]{2,1,0:T(1,128)}), f32[96,1,1024]{2,1,0:T(1,128)S(1)}, u32[]{:S(2)}, u32[]{:S(2)}) async-start(f32[96,1,1024]{2,1,0:T(1,128)} %copy.8), calls=%async_computation | async-start | bytes 786432 | tf_op jit(solution)/shard_map/all_to_all | solution.py:152
  (4 other events, 3.0 us)

commit v5 on v4

--- a/solution.py
+++ b/solution.py
@@ -48,6 +48,17 @@
         left.reshape(-1, channels),
         right.reshape(-1, channels),
         (((0,), (0,)), ((), ())),
+        preferred_element_type=jnp.float32,
+    )
+
+
+def stacked_outer_sum(lefts, right):
+    channels = right.shape[-1]
+    stack = jnp.stack([left.reshape(-1, channels) for left in lefts])
+    return lax.dot_general(
+        stack,
+        right.reshape(-1, channels),
+        (((1,), (0,)), ((), ())),
         preferred_element_type=jnp.float32,
     )
 
@@ -109,22 +120,17 @@
             future[time_lag : time_lag + frame_count], temporal_weight[time_lag].T
         )
     grad_mid = grad_wide.astype(jnp.bfloat16)
-    grad_temporal = jnp.stack(
+    grad_temporal = stacked_outer_sum(
+        [history[2 - time_lag : 2 - time_lag + frame_count] for time_lag in range(3)], cotangent
+    )
+    grad_spatial = stacked_outer_sum(
         [
-            outer_sum(history[2 - time_lag : 2 - time_lag + frame_count], cotangent)
-            for time_lag in range(3)
-        ]
+            padded[:, tap_row : tap_row + row_count, tap_col : tap_col + col_count]
+            for tap_row in range(3)
+            for tap_col in range(3)
+        ],
+        grad_mid,
     )
-    terms = []
-    for tap_row in range(3):
-        for tap_col in range(3):
-            terms.append(
-                outer_sum(
-                    padded[:, tap_row : tap_row + row_count, tap_col : tap_col + col_count],
-                    grad_mid,
-                )
-            )
-    grad_spatial = jnp.stack(terms)
     grad_mid_late, unused_history = lax.optimization_barrier((grad_mid, earlier))
     time_shards = lax.axis_size("tm")
     row_shards = lax.axis_size("height")

time: 134 us -> 144 us (1.075)
  local copies, waits for them, and re-layouts: 7.2 us -> 22.4 us
  matrix products: 20.5 us -> 15.9 us
  waiting for transfers between devices: 46.6 us -> 43.1 us
  other arithmetic: 7.01 us -> 8.67 us
    another operation x0 -> x10, local copies, waits for them, and re-layouts: none -> 6.93 us  [stacked_outer_sum(): stack = jnp.stack([left.reshape(-1, channels) for left in lefts])]
    dot_general x12 -> x2, matrix products: 10.2 us -> 5.44 us  [stacked_outer_sum(): lax.dot_general(stack, right.reshape(-1, channels), (((1,), (0,)), ((), (...]
    unnamed x36 -> x58, local copies, waits for them, and re-layouts: 2.79 us -> 7.53 us
    ppermute x3, waiting for transfers between devices: 26.3 us -> 21.7 us  [halving_scatter(): block = keep + lax.ppermute(send, axis, route)]
    dot_general x0 -> x1, local copies, waits for them, and re-layouts: none -> 2.34 us  [stacked_outer_sum(): lax.dot_general(stack, right.reshape(-1, channels), (((1,), (0,)), ((), (...]
    ppermute x3, starting transfers between devices: 14.7 us -> 12.7 us  [halving_scatter(): block = keep + lax.ppermute(send, axis, route)]
    ppermute x2, waiting for transfers between devices: 0.01 us -> 1.6 us  [extended(): lax.ppermute(tail, axis, [(i, (i + 1) % count) for i in range(ends)])]
  transfers between devices with their start and end apart: 10 -> 10, of which waited for: 5 -> 5; matrix products, arithmetic and copies ran while one was open for 18% -> 22% of each run, Pallas kernels for 0% -> 0%
where the time goes in v5:
time: 144 us; the launch traced here: 142 us
  starting transfers between devices  50.8 us (35%)
  waiting for transfers between devices  43.1 us (30%)
  local copies, waits for them, and re-layouts  22.4 us (16%)
  matrix products  15.9 us (11%)
  other arithmetic  8.67 us (6%)
    all_to_all x1, starting transfers between devices, shards(): packed = lax.all_to_all(packed, 'height', 0, 0, tiled=True)  21.7 us
    ppermute x3, waiting for transfers between devices, halving_scatter(): block = keep + lax.ppermute(send, axis, route)  21.7 us
    all_to_all x1, waiting for transfers between devices, shards(): packed = lax.all_to_all(packed, 'height', 0, 0, tiled=True)  19.7 us
    ppermute x3, starting transfers between devices, halving_scatter(): block = keep + lax.ppermute(send, axis, route)  12.7 us
    dot_general x24, matrix products, flat_dot(): jnp.dot(left.reshape(-1, left.shape[-1]), weight, preferred_element_type=...  10.4 us
    ppermute x2, starting transfers between devices, extended(): lax.ppermute(tail, axis, [(i, (i + 1) % count) for i in range(ends)])  8.66 us
    unnamed x58, local copies, waits for them, and re-layouts  7.53 us
    another operation x10, local copies, waits for them, and re-layouts, stacked_outer_sum(): stack = jnp.stack([left.reshape(-1, channels) for left in lefts])  6.93 us
  transfers between devices with their start and end apart: 10, of which 5 were waited for; matrix products, arithmetic and copies ran while one was open for 22% of the time, Pallas kernels for 0%

profile of v5, /device:TPU:6, one launch (start us, length us, event | category | flops | bytes accessed | tf_op | source)
XLA Modules:
  0.0 142.1 jit_solution(6784146318620973523)
XLA Ops:
  1.7 1.2 fusion.20
  2.9 3.5 %collective-permute-start = (bf16[2,1,64,256]{3,2,1,0:T(8,128)(2,1)S(1)}, bf16[2,1,64,256]{3,2,1,0:T(8,128)(2,1)S(1)}, u32[]{:S(2)}, u32[]{:S(2)}) collective-permute-start(bf16[2,1,64,256]{3,2,1,0:T(8,128)(2,1)S(1)} %get-tuple-element.20), channel_id=1, source_target_pairs={{0,1},{1,2},{2,3},{3,4},{4,5},{5,6},{6,7},{7,8},{8,9},{9,10},{10,1... | collective-permute-start | bytes 196616 | tf_op jit(solution)/shard_map/ppermute | solution.py:19
  6.4 1.3 collective-permute-start.1
  7.7 1.9 %collective-permute-start.3 = (bf16[2,4,64,256]{3,2,1,0:T(8,128)(2,1)}, bf16[2,4,64,256]{3,2,1,0:T(8,128)(2,1)}, u32[]{:S(2)}, u32[]{:S(2)}) collective-permute-start(bf16[2,4,64,256]{3,2,1,0:T(8,128)(2,1)} %param.5), channel_id=1, source_target_pairs={{96,0},{192,96},{288,192},{384,288},{480,384},{576,480},{672,576},... | collective-permute-start | bytes 786440 | tf_op jit(solution)/shard_map/ppermute | solution.py:31
  9.7 2.1 %fusion.80 = f32[2,4,64,256]{3,2,1,0:T(8,128)} fusion(bf16[2,4,64,256]{3,2,1,0:T(8,128)(2,1)} %param.5, bf16[3,256,256]{2,1,0:T(8,128)(2,1)} %param.7), kind=kOutput, calls=%fused_computation.119 | convolution fusion | flops 67108864 | bytes 917504 | tf_op jit(solution)/shard_map/dot_general | solution.py:41
  21.8 3.2 %collective-permute-start.2 = (bf16[2,4,64,256]{3,2,1,0:T(8,128)(2,1)S(1)}, bf16[2,4,64,256]{3,2,1,0:T(8,128)(2,1)S(1)}, u32[]{:S(2)}, u32[]{:S(2)}) collective-permute-start(bf16[2,4,64,256]{3,2,1,0:T(8,128)(2,1)S(1)} %fusion.11), channel_id=1, source_target_pairs={{0,96},{96,192},{192,288},{288,384},{384,480},{480,576},{576,672},... | collective-permute-start | bytes 786440 | tf_op jit(solution)/shard_map/ppermute | solution.py:31
  31.1 1.2 fusion.74
  32.3 1.2 fusion.12
  33.5 3.9 %fusion.124 = f32[9,256,256]{2,1,0:T(8,128)} fusion(bf16[9,512,256]{1,2,0:T(8,128)(2,1)} %constant_dynamic-update-slice_fusion, bf16[512,256,1]{1,0,2:T(8,128)(2,1)S(1)} %bitcast.158), kind=kOutput, calls=%fused_computation.176 | convolution fusion | flops 603979776 | bytes 4980736 | tf_op jit(solution)/shard_map/dot_general | solution.py:58
  37.4 2.6 %concatenate.35 = f32[4,2,96,768]{3,2,1,0:T(8,128)S(1)} reshape(f32[9,256,256]{2,1,0:T(8,128)} %fusion.124) | data formatting | bytes 4718592 | tf_op jit(solution)/shard_map/concatenate | solution.py:141
  41.0 2.3 %copy.47 = bf16[3,256,512]{2,1,0:T(8,128)(2,1)} copy(bf16[3,256,512]{1,2,0:T(8,128)(2,1)} %maximum_bitcast_fusion) | data formatting | bytes 1572864 | tf_op jit(solution)/shard_map/dot_general | solution.py:58
  43.4 1.5 %fusion.125 = f32[4,2,96,256]{3,2,1,0:T(8,128)S(1)} fusion(bf16[4,2,96,512]{3,2,1,0:T(8,128)(2,1)} %bitcast.164, bf16[512,256,1,1]{1,0,3,2:T(8,128)(2,1)} %bitcast.162), kind=kOutput, calls=%fused_computation.177 | convolution fusion | flops 201326592 | bytes 1835008 | tf_op jit(solution)/shard_map/dot_general | solution.py:58
  44.9 1.4 %fusion.1 = f32[4,96,1024]{2,1,0:T(8,128)} fusion(s32[]{:T(128)S(6)} %select_n.46, f32[4,2,96,768]{3,2,1,0:T(8,128)S(1)} %concatenate.35, f32[4,2,96,256]{3,2,1,0:T(8,128)S(1)} %fusion.125), kind=kLoop, calls=%fused_computation.5 | loop fusion | flops 393216 | bytes 4718596 | tf_op jit(solution)/shard_map/jit(dynamic_index_in_dim)/squeeze | solution.py:75
  46.4 1.9 %collective-permute-start.4 = (f32[4,96,1024]{2,1,0:T(8,128)}, f32[4,96,1024]{2,1,0:T(8,128)}, u32[]{:S(2)}, u32[]{:S(2)}) collective-permute-start(f32[4,96,1024]{2,1,0:T(8,128)} %fusion.1), channel_id=1, source_target_pairs={{0,96},{96,0},{192,288},{288,192},{384,480},{480,384},{576,672},{6... | collective-permute-start | bytes 4718600 | tf_op jit(solution)/shard_map/ppermute | solution.py:77
  48.3 3.7 %collective-permute-done.4 = f32[4,96,1024]{2,1,0:T(8,128)} collective-permute-done((f32[4,96,1024]{2,1,0:T(8,128)}, f32[4,96,1024]{2,1,0:T(8,128)}, u32[]{:S(2)}, u32[]{:S(2)}) %collective-permute-start.4) | collective-permute-done | bytes 1572896 | tf_op jit(solution)/shard_map/ppermute | solution.py:77
  52.0 1.6 %fusion.4 = f32[4,96,1024]{2,1,0:T(8,128)S(1)} fusion(f32[4,96,1024]{2,1,0:T(8,128)} %collective-permute-done.4, s32[]{:T(128)S(6)} %select_n.45, f32[4,2,96,768]{3,2,1,0:T(8,128)S(1)} %concatenate.35, f32[4,2,96,256]{3,2,1,0:T(8,128)S(1)} %fusion.125), kind=kLoop, calls=%fused_computation.8 | loop fusion | flops 786432 | bytes 6291460 | tf_op jit(solution)/shard_map/add | solution.py:77
  55.8 2.5 %collective-permute-start.5 = (f32[2,96,1024]{2,1,0:T(8,128)}, f32[2,96,1024]{2,1,0:T(8,128)S(1)}, u32[]{:S(2)}, u32[]{:S(2)}) collective-permute-start(f32[2,96,1024]{2,1,0:T(8,128)} %dynamic-slice_bitcast_fusion), channel_id=1, source_target_pairs={{0,192},{96,288},{192,0},{288,96},{384,576},{480,672},{576,384},{6... | collective-permute-start | bytes 2359304 | tf_op jit(solution)/shard_map/ppermute | solution.py:77
  59.8 17.7 %collective-permute-done.5 = f32[2,96,1024]{2,1,0:T(8,128)S(1)} collective-permute-done((f32[2,96,1024]{2,1,0:T(8,128)}, f32[2,96,1024]{2,1,0:T(8,128)S(1)}, u32[]{:S(2)}, u32[]{:S(2)}) %collective-permute-start.5) | collective-permute-done | bytes 786464 | tf_op jit(solution)/shard_map/ppermute | solution.py:77
  77.6 1.3 collective-permute-start.7
  78.9 8.3 %collective-permute-start.8 = (f32[1,96,1024]{2,1,0:T(8,128)S(1)}, f32[1,96,1024]{2,1,0:T(8,128)S(1)}, u32[]{:S(2)}, u32[]{:S(2)}) collective-permute-start(f32[1,96,1024]{2,1,0:T(8,128)S(1)} %constant_dynamic-slice_fusion), channel_id=1, source_target_pairs={{0,384},{96,480},{192,576},{288,672},{384,0},{480,96},{576,192},{6... | collective-permute-start | bytes 1179656 | tf_op jit(solution)/shard_map/ppermute | solution.py:77
  87.2 5.2 %collective-permute-start.6 = (bf16[2,1,64,256]{3,2,1,0:T(8,128)(2,1)S(1)}, bf16[2,1,64,256]{3,2,1,0:T(8,128)(2,1)S(1)}, u32[]{:S(2)}, u32[]{:S(2)}) collective-permute-start(bf16[2,1,64,256]{3,2,1,0:T(8,128)(2,1)S(1)} %get-tuple-element.16), channel_id=1, source_target_pairs={{0,1},{1,2},{2,3},{3,4},{4,5},{5,6},{6,7},{7,8},{8,9},{9,10},{10,1... | collective-permute-start | bytes 196616 | tf_op jit(solution)/shard_map/ppermute | solution.py:19
  92.7 1.6 %collective-permute-done.6 = bf16[2,1,64,256]{3,2,1,0:T(8,128)(2,1)S(1)} collective-permute-done((bf16[2,1,64,256]{3,2,1,0:T(8,128)(2,1)S(1)}, bf16[2,1,64,256]{3,2,1,0:T(8,128)(2,1)S(1)}, u32[]{:S(2)}, u32[]{:S(2)}) %collective-permute-start.6) | collective-permute-done | bytes 65568 | tf_op jit(solution)/shard_map/ppermute | solution.py:19
  97.3 21.7 %all-to-all-start = ((f32[96,1,1024]{2,1,0:T(1,128)}), f32[96,1,1024]{2,1,0:T(1,128)S(1)}, u32[]{:S(2)}, u32[]{:S(2)}) async-start(f32[96,1,1024]{2,1,0:T(1,128)} %copy.48), calls=%async_computation | async-start | bytes 786432 | tf_op jit(solution)/shard_map/all_to_all | solution.py:158
  121.5 19.7 %all-to-all-done = f32[96,1,1024]{2,1,0:T(1,128)S(1)} async-done(((f32[96,1,1024]{2,1,0:T(1,128)}), f32[96,1,1024]{2,1,0:T(1,128)S(1)}, u32[]{:S(2)}, u32[]{:S(2)}) %all-to-all-start) | async-done | bytes 393248 | tf_op jit(solution)/shard_map/all_to_all | solution.py:158
  (115 shorter events, 28.3 us)
Async XLA Ops:
  2.9 9.6 %collective-permute-start = (bf16[2,1,64,256]{3,2,1,0:T(8,128)(2,1)S(1)}, bf16[2,1,64,256]{3,2,1,0:T(8,128)(2,1)S(1)}, u32[]{:S(2)}, u32[]{:S(2)}) collective-permute-start(bf16[2,1,64,256]{3,2,1,0:T(8,128)(2,1)S(1)} %get-tuple-element.20), channel_id=1, source_target_pairs={{0,1},{1,2},{2,3},{3,4},{4,5},{5,6},{6,7},{7,8},{8,9},{9,10},{10,1... | collective-permute-start | bytes 196616 | tf_op jit(solution)/shard_map/ppermute | solution.py:19
  6.4 6.2 %collective-permute-start.1 = (bf16[2,1,64,256]{3,2,1,0:T(8,128)(2,1)S(1)}, bf16[2,1,64,256]{3,2,1,0:T(8,128)(2,1)S(1)}, u32[]{:S(2)}, u32[]{:S(2)}) collective-permute-start(bf16[2,1,64,256]{3,2,1,0:T(8,128)(2,1)S(1)} %get-tuple-element.21), channel_id=1, source_target_pairs={{1,0},{2,1},{3,2},{4,3},{5,4},{6,5},{7,6},{8,7},{9,8},{10,9},{11,1... | collective-permute-start | bytes 196616 | tf_op jit(solution)/shard_map/ppermute | solution.py:21
  7.7 23.4 %collective-permute-start.3 = (bf16[2,4,64,256]{3,2,1,0:T(8,128)(2,1)}, bf16[2,4,64,256]{3,2,1,0:T(8,128)(2,1)}, u32[]{:S(2)}, u32[]{:S(2)}) collective-permute-start(bf16[2,4,64,256]{3,2,1,0:T(8,128)(2,1)} %param.5), channel_id=1, source_target_pairs={{96,0},{192,96},{288,192},{384,288},{480,384},{576,480},{672,576},... | collective-permute-start | bytes 786440 | tf_op jit(solution)/shard_map/ppermute | solution.py:31
  14.5 5.1 %copy-start.4 = (bf16[3,3,256,256]{3,2,1,0:T(8,128)(2,1)S(1)}, bf16[3,3,256,256]{3,2,1,0:T(8,128)(2,1)}, u32[]{:S(2)}) copy-start(bf16[3,3,256,256]{3,2,1,0:T(8,128)(2,1)} %param.6) | copy-start | bytes 3538948
  21.3 4.5 %copy-start.21 = (bf16[1,512,256]{1,2,0:T(8,128)(2,1)S(1)}, bf16[1,512,256]{1,2,0:T(8,128)(2,1)}, u32[]{:S(2)}) copy-start(bf16[1,512,256]{1,2,0:T(8,128)(2,1)} %copy.40) | copy-start | bytes 786436
  21.5 5.0 %copy-start.19 = (bf16[1,512,256]{1,2,0:T(8,128)(2,1)S(1)}, bf16[1,512,256]{1,2,0:T(8,128)(2,1)}, u32[]{:S(2)}) copy-start(bf16[1,512,256]{1,2,0:T(8,128)(2,1)} %copy.41) | copy-start | bytes 786436
  21.5 5.7 %copy-start.15 = (bf16[1,512,256]{1,2,0:T(8,128)(2,1)S(1)}, bf16[1,512,256]{1,2,0:T(8,128)(2,1)}, u32[]{:S(2)}) copy-start(bf16[1,512,256]{1,2,0:T(8,128)(2,1)} %copy.42) | copy-start | bytes 786436
  21.5 6.5 %copy-start.18 = (bf16[1,512,256]{1,2,0:T(8,128)(2,1)S(1)}, bf16[1,512,256]{1,2,0:T(8,128)(2,1)}, u32[]{:S(2)}) copy-start(bf16[1,512,256]{1,2,0:T(8,128)(2,1)} %copy.43) | copy-start | bytes 786436
  21.8 18.3 %copy-start = (bf16[2,4,64,256]{3,2,1,0:T(8,128)(2,1)}, bf16[2,4,64,256]{3,2,1,0:T(8,128)(2,1)S(1)}, u32[]{:S(2)}) copy-start(bf16[2,4,64,256]{3,2,1,0:T(8,128)(2,1)S(1)} %fusion.11) | copy-start | bytes 786436
  21.8 6.9 %copy-start.17 = (bf16[1,512,256]{1,2,0:T(8,128)(2,1)S(1)}, bf16[1,512,256]{1,2,0:T(8,128)(2,1)}, u32[]{:S(2)}) copy-start(bf16[1,512,256]{1,2,0:T(8,128)(2,1)} %copy.44) | copy-start | bytes 786436
  21.8 7.7 %copy-start.14 = (bf16[2,4,64,256]{3,2,1,0:T(8,128)(2,1)S(1)}, bf16[2,4,64,256]{3,2,1,0:T(8,128)(2,1)}, u32[]{:S(2)}) copy-start(bf16[2,4,64,256]{3,2,1,0:T(8,128)(2,1)} %get-tuple-element.18) | copy-start | bytes 786436
  21.8 18.2 %collective-permute-start.2 = (bf16[2,4,64,256]{3,2,1,0:T(8,128)(2,1)S(1)}, bf16[2,4,64,256]{3,2,1,0:T(8,128)(2,1)S(1)}, u32[]{:S(2)}, u32[]{:S(2)}) collective-permute-start(bf16[2,4,64,256]{3,2,1,0:T(8,128)(2,1)S(1)} %fusion.11), channel_id=1, source_target_pairs={{0,96},{96,192},{192,288},{288,384},{384,480},{480,576},{576,672},... | collective-permute-start | bytes 786440 | tf_op jit(solution)/shard_map/ppermute | solution.py:31
  46.4 5.6 %collective-permute-start.4 = (f32[4,96,1024]{2,1,0:T(8,128)}, f32[4,96,1024]{2,1,0:T(8,128)}, u32[]{:S(2)}, u32[]{:S(2)}) collective-permute-start(f32[4,96,1024]{2,1,0:T(8,128)} %fusion.1), channel_id=1, source_target_pairs={{0,96},{96,0},{192,288},{288,192},{384,480},{480,384},{576,672},{6... | collective-permute-start | bytes 4718600 | tf_op jit(solution)/shard_map/ppermute | solution.py:77
  53.6 4.7 %copy-start.1 = (bf16[2,4,64,256]{3,2,1,0:T(8,128)(2,1)S(1)}, bf16[2,4,64,256]{3,2,1,0:T(8,128)(2,1)}, u32[]{:S(2)}) copy-start(bf16[2,4,64,256]{3,2,1,0:T(8,128)(2,1)} %copy-done) | copy-start | bytes 786436
  53.6 4.7 %copy-start.13 = (bf16[3,256,256]{2,1,0:T(8,128)(2,1)S(1)}, bf16[3,256,256]{2,1,0:T(8,128)(2,1)}, u32[]{:S(2)}) copy-start(bf16[3,256,256]{2,1,0:T(8,128)(2,1)} %param.7) | copy-start | bytes 1179652
  53.6 4.9 %copy-start.10 = (bf16[2,4,64,256]{3,2,1,0:T(8,128)(2,1)S(1)}, bf16[2,4,64,256]{3,2,1,0:T(8,128)(2,1)}, u32[]{:S(2)}) copy-start(bf16[2,4,64,256]{3,2,1,0:T(8,128)(2,1)} %copy-done.9) | copy-start | bytes 786436
  54.8 4.0 %copy-start.8 = (bf16[2,4,64,256]{3,2,1,0:T(8,128)(2,1)S(1)}, bf16[2,4,64,256]{3,2,1,0:T(8,128)(2,1)}, u32[]{:S(2)}) copy-start(bf16[2,4,64,256]{3,2,1,0:T(8,128)(2,1)} %param.4) | copy-start | bytes 786436
  55.8 21.7 %collective-permute-start.5 = (f32[2,96,1024]{2,1,0:T(8,128)}, f32[2,96,1024]{2,1,0:T(8,128)S(1)}, u32[]{:S(2)}, u32[]{:S(2)}) collective-permute-start(f32[2,96,1024]{2,1,0:T(8,128)} %dynamic-slice_bitcast_fusion), channel_id=1, source_target_pairs={{0,192},{96,288},{192,0},{288,96},{384,576},{480,672},{576,384},{6... | collective-permute-start | bytes 2359304 | tf_op jit(solution)/shard_map/ppermute | solution.py:77
  58.6 18.9 %copy-start.3 = (f32[4,96,1024]{2,1,0:T(8,128)S(1)}, f32[4,96,1024]{2,1,0:T(8,128)}, u32[]{:S(2)}) copy-start(f32[4,96,1024]{2,1,0:T(8,128)} %copy-done.2) | copy-start | bytes 4718596
  59.8 32.6 %copy-start.5 = (bf16[3,3,256,256]{3,2,1,0:T(8,128)(2,1)S(1)}, bf16[3,3,256,256]{3,2,1,0:T(8,128)(2,1)}, u32[]{:S(2)}) copy-start(bf16[3,3,256,256]{3,2,1,0:T(8,128)(2,1)} %param.6) | copy-start | bytes 3538948
  77.6 14.8 %collective-permute-start.7 = (bf16[2,1,64,256]{3,2,1,0:T(8,128)(2,1)S(1)}, bf16[2,1,64,256]{3,2,1,0:T(8,128)(2,1)S(1)}, u32[]{:S(2)}, u32[]{:S(2)}) collective-permute-start(bf16[2,1,64,256]{3,2,1,0:T(8,128)(2,1)S(1)} %get-tuple-element.17), channel_id=1, source_target_pairs={{1,0},{2,1},{3,2},{4,3},{5,4},{6,5},{7,6},{8,7},{9,8},{10,9},{11,1... | collective-permute-start | bytes 196616 | tf_op jit(solution)/shard_map/ppermute | solution.py:21
  78.9 17.2 %collective-permute-start.8 = (f32[1,96,1024]{2,1,0:T(8,128)S(1)}, f32[1,96,1024]{2,1,0:T(8,128)S(1)}, u32[]{:S(2)}, u32[]{:S(2)}) collective-permute-start(f32[1,96,1024]{2,1,0:T(8,128)S(1)} %constant_dynamic-slice_fusion), channel_id=1, source_target_pairs={{0,384},{96,480},{192,576},{288,672},{384,0},{480,96},{576,192},{6... | collective-permute-start | bytes 1179656 | tf_op jit(solution)/shard_map/ppermute | solution.py:77
  87.2 7.1 %collective-permute-start.6 = (bf16[2,1,64,256]{3,2,1,0:T(8,128)(2,1)S(1)}, bf16[2,1,64,256]{3,2,1,0:T(8,128)(2,1)S(1)}, u32[]{:S(2)}, u32[]{:S(2)}) collective-permute-start(bf16[2,1,64,256]{3,2,1,0:T(8,128)(2,1)S(1)} %get-tuple-element.16), channel_id=1, source_target_pairs={{0,1},{1,2},{2,3},{3,4},{4,5},{5,6},{6,7},{7,8},{8,9},{9,10},{10,1... | collective-permute-start | bytes 196616 | tf_op jit(solution)/shard_map/ppermute | solution.py:19
  97.3 43.9 %all-to-all-start = ((f32[96,1,1024]{2,1,0:T(1,128)}), f32[96,1,1024]{2,1,0:T(1,128)S(1)}, u32[]{:S(2)}, u32[]{:S(2)}) async-start(f32[96,1,1024]{2,1,0:T(1,128)} %copy.48), calls=%async_computation | async-start | bytes 786432 | tf_op jit(solution)/shard_map/all_to_all | solution.py:158
  (11 other events, 29.6 us)

commit v6 on v4

--- a/solution.py
+++ b/solution.py
@@ -52,7 +52,7 @@
     )
 
 
-def halving_scatter(block, axis, tie=None, tie_after=0):
+def halving_scatter(block, axis, tie=None, tie_after=0, narrow_from=None):
     count = lax.axis_size(axis)
     index = lax.axis_index(axis)
     step = 1
@@ -63,7 +63,11 @@
         keep = lax.dynamic_index_in_dim(pairs, mine, axis=1, keepdims=False)
         send = lax.dynamic_index_in_dim(pairs, 1 - mine, axis=1, keepdims=False)
         route = [(i, i ^ step) for i in range(count)]
-        block = keep + lax.ppermute(send, axis, route)
+        if narrow_from is not None and step >= narrow_from:
+            sent = lax.ppermute(send.astype(jnp.bfloat16), axis, route).astype(block.dtype)
+        else:
+            sent = lax.ppermute(send, axis, route)
+        block = keep + sent
         if tie is not None and step == 1 << tie_after:
             block, tie = lax.optimization_barrier((block, tie))
         step *= 2
@@ -134,7 +138,7 @@
     temporal_rows = grad_temporal.reshape(devices, -1)
     packed = jnp.concatenate([spatial_rows, temporal_rows], axis=1)
     packed = packed.reshape(time_shards, row_shards, packed.shape[-1])
-    packed, grad_mid_late = halving_scatter(packed, "tm", grad_mid_late, 1)
+    packed, grad_mid_late = halving_scatter(packed, "tm", grad_mid_late, 1, narrow_from=2)
     packed = packed[0]
     grad_ext = extended(grad_mid_late, (("height", 1),), 1)
     grad_pad = jnp.pad(grad_ext, ((0, 0), (0, 0), (1, 1), (0, 0)))

time: 134 us -> 120 us (0.90)
  waiting for transfers between devices: 46.6 us -> 33.5 us
    ppermute x3, waiting for transfers between devices: 26.3 us -> 13.4 us  [the longest x2 11 us: halving_scatter(): lax.ppermute(send.astype(jnp.bfloat16), axis, route).astype(block.dtype)]
    unnamed x36 -> x30, local copies, waits for them, and re-layouts: 2.79 us -> 1.67 us
  transfers between devices with their start and end apart: 10 -> 10, of which waited for: 5 -> 5; matrix products, arithmetic and copies ran while one was open for 18% -> 20% of each run, Pallas kernels for 0% -> 0%
where the time goes in v6:
time: 120 us; the launch traced here: 118 us
  starting transfers between devices  49.8 us (42%)
  waiting for transfers between devices  33.5 us (28%)
  matrix products  20.7 us (17%)
  other arithmetic  7.02 us (6%)
  local copies, waits for them, and re-layouts  6.07 us (5%)
  between operations  1.24 us (1%)
    all_to_all x1, starting transfers between devices, shards(): packed = lax.all_to_all(packed, 'height', 0, 0, tiled=True)  21.2 us
    all_to_all x1, waiting for transfers between devices, shards(): packed = lax.all_to_all(packed, 'height', 0, 0, tiled=True)  19.2 us
    ppermute x2, starting transfers between devices, halving_scatter(): lax.ppermute(send.astype(jnp.bfloat16), axis, route).astype(block.dtype)  12.8 us
    ppermute x2, waiting for transfers between devices, halving_scatter(): lax.ppermute(send.astype(jnp.bfloat16), axis, route).astype(block.dtype)  11 us
    dot_general x24, matrix products, flat_dot(): jnp.dot(left.reshape(-1, left.shape[-1]), weight, preferred_element_type=...  10.5 us
    dot_general x12, matrix products, outer_sum(): lax.dot_general(left.reshape(-1, channels), right.reshape(-1, channels),...  10.2 us
    ppermute x2, starting transfers between devices, extended(): lax.ppermute(tail, axis, [(i, (i + 1) % count) for i in range(ends)])  7.39 us
    ppermute x2, starting transfers between devices, shifted(): return lax.ppermute(block, axis, route)  3.97 us
  transfers between devices with their start and end apart: 10, of which 5 were waited for; matrix products, arithmetic and copies ran while one was open for 20% of the time, Pallas kernels for 0%

profile of v6, /device:TPU:6, one launch (start us, length us, event | category | flops | bytes accessed | tf_op | source)
XLA Modules:
  0.0 118.4 jit_solution(14364996619360089238)
XLA Ops:
  0.6 1.2 %fusion.34 = f32[2,4,64]{2,1,0:T(4,128)S(1)} fusion(bf16[2,4,64,256]{3,2,1,0:T(8,128)(2,1)} %param.4), kind=kLoop, calls=%fused_computation.77 | loop fusion | flops 392704 | bytes 264192 | tf_op jit(solution)/shard_map/reduce_sum | solution.py:35
  1.8 1.2 fusion.29
  3.0 3.5 %collective-permute-start = (bf16[2,1,64,256]{3,2,1,0:T(8,128)(2,1)S(1)}, bf16[2,1,64,256]{3,2,1,0:T(8,128)(2,1)S(1)}, u32[]{:S(2)}, u32[]{:S(2)}) collective-permute-start(bf16[2,1,64,256]{3,2,1,0:T(8,128)(2,1)S(1)} %get-tuple-element.12), channel_id=1, source_target_pairs={{0,1},{1,2},{2,3},{3,4},{4,5},{5,6},{6,7},{7,8},{8,9},{9,10},{10,1... | collective-permute-start | bytes 196616 | tf_op jit(solution)/shard_map/ppermute | solution.py:19
  6.5 1.3 %collective-permute-start.1 = (bf16[2,1,64,256]{3,2,1,0:T(8,128)(2,1)S(1)}, bf16[2,1,64,256]{3,2,1,0:T(8,128)(2,1)S(1)}, u32[]{:S(2)}, u32[]{:S(2)}) collective-permute-start(bf16[2,1,64,256]{3,2,1,0:T(8,128)(2,1)S(1)} %get-tuple-element.13), channel_id=1, source_target_pairs={{1,0},{2,1},{3,2},{4,3},{5,4},{6,5},{7,6},{8,7},{9,8},{10,9},{11,1... | collective-permute-start | bytes 196616 | tf_op jit(solution)/shard_map/ppermute | solution.py:21
  7.8 1.9 %collective-permute-start.3 = (bf16[2,4,64,256]{3,2,1,0:T(8,128)(2,1)}, bf16[2,4,64,256]{3,2,1,0:T(8,128)(2,1)S(1)}, u32[]{:S(2)}, u32[]{:S(2)}) collective-permute-start(bf16[2,4,64,256]{3,2,1,0:T(8,128)(2,1)} %param.5), channel_id=1, source_target_pairs={{96,0},{192,96},{288,192},{384,288},{480,384},{576,480},{672,576},... | collective-permute-start | bytes 786440 | tf_op jit(solution)/shard_map/ppermute | solution.py:31
  9.8 2.0 %fusion.93 = f32[2,4,64,256]{3,2,1,0:T(8,128)} fusion(bf16[2,4,64,256]{3,2,1,0:T(8,128)(2,1)} %param.5, bf16[3,256,256]{2,1,0:T(8,128)(2,1)} %param.7), kind=kOutput, calls=%fused_computation.145 | convolution fusion | flops 67108864 | bytes 917504 | tf_op jit(solution)/shard_map/dot_general | solution.py:41
  15.0 2.1 %collective-permute-start.2 = (bf16[2,4,64,256]{3,2,1,0:T(8,128)(2,1)S(1)}, bf16[2,4,64,256]{3,2,1,0:T(8,128)(2,1)S(1)}, u32[]{:S(2)}, u32[]{:S(2)}) collective-permute-start(bf16[2,4,64,256]{3,2,1,0:T(8,128)(2,1)S(1)} %fusion.11), channel_id=1, source_target_pairs={{0,96},{96,192},{192,288},{288,384},{384,480},{480,576},{576,672},... | collective-permute-start | bytes 786440 | tf_op jit(solution)/shard_map/ppermute | solution.py:31
  19.0 1.2 fusion.12
  24.0 1.0 fusion.18
  28.9 2.6 %concatenate.37 = f32[4,2,96,768]{3,2,1,0:T(8,128)S(1)} reshape(f32[9,256,256]{2,1,0:T(8,128)} %fusion.15) | data formatting | bytes 4718592 | tf_op jit(solution)/shard_map/concatenate | solution.py:139
  32.6 1.4 %fusion.1 = f32[4,96,1024]{2,1,0:T(8,128)} fusion(s32[]{:T(128)S(6)} %select_n.46, f32[4,2,96,768]{3,2,1,0:T(8,128)S(1)} %concatenate.37, f32[4,2,96,256]{3,2,1,0:T(8,128)S(1)} %bitcast.236), kind=kLoop, calls=%fused_computation.5 | loop fusion | flops 393216 | bytes 4718596 | tf_op jit(solution)/shard_map/jit(dynamic_index_in_dim)/squeeze | solution.py:64
  34.0 1.9 %collective-permute-start.4 = (f32[4,96,1024]{2,1,0:T(8,128)}, f32[4,96,1024]{2,1,0:T(8,128)}, u32[]{:S(2)}, u32[]{:S(2)}) collective-permute-start(f32[4,96,1024]{2,1,0:T(8,128)} %fusion.1), channel_id=1, source_target_pairs={{0,96},{96,0},{192,288},{288,192},{384,480},{480,384},{576,672},{6... | collective-permute-start | bytes 4718600 | tf_op jit(solution)/shard_map/ppermute | solution.py:69
  36.0 1.2 %fusion.95 = f32[2,4,64,256]{3,2,1,0:T(8,128)S(1)} fusion(bf16[2,4,64,256]{3,2,1,0:T(8,128)(2,1)} %copy-done.5, bf16[3,256,256]{2,1,0:T(8,128)(2,1)} %param.7), kind=kOutput, calls=%fused_computation.147 | convolution fusion | flops 67108864 | bytes 917504 | tf_op jit(solution)/shard_map/dot_general | solution.py:41
  37.2 2.4 %collective-permute-done.4 = f32[4,96,1024]{2,1,0:T(8,128)} collective-permute-done((f32[4,96,1024]{2,1,0:T(8,128)}, f32[4,96,1024]{2,1,0:T(8,128)}, u32[]{:S(2)}, u32[]{:S(2)}) %collective-permute-start.4) | collective-permute-done | bytes 1572896 | tf_op jit(solution)/shard_map/ppermute | solution.py:69
  39.6 1.6 %fusion.4 = f32[4,96,1024]{2,1,0:T(8,128)S(1)} fusion(f32[4,96,1024]{2,1,0:T(8,128)} %collective-permute-done.4, s32[]{:T(128)S(6)} %select_n.45, f32[4,2,96,768]{3,2,1,0:T(8,128)S(1)} %concatenate.37, f32[4,2,96,256]{3,2,1,0:T(8,128)S(1)} %bitcast.237), kind=kLoop, calls=%fused_computation.8 | loop fusion | flops 786432 | bytes 6291460 | tf_op jit(solution)/shard_map/add | solution.py:70
  41.3 3.8 %collective-permute-start.5 = (bf16[2,96,1024]{2,1,0:T(8,128)(2,1)S(1)}, bf16[2,96,1024]{2,1,0:T(8,128)(2,1)S(1)}, u32[]{:S(2)}, u32[]{:S(2)}) collective-permute-start(bf16[2,96,1024]{2,1,0:T(8,128)(2,1)S(1)} %fusion.40), channel_id=1, source_target_pairs={{0,192},{96,288},{192,0},{288,96},{384,576},{480,672},{576,384},{6... | collective-permute-start | bytes 1179656 | tf_op jit(solution)/shard_map/ppermute | solution.py:67
  46.4 8.4 %collective-permute-done.5 = bf16[2,96,1024]{2,1,0:T(8,128)(2,1)S(1)} collective-permute-done((bf16[2,96,1024]{2,1,0:T(8,128)(2,1)S(1)}, bf16[2,96,1024]{2,1,0:T(8,128)(2,1)S(1)}, u32[]{:S(2)}, u32[]{:S(2)}) %collective-permute-start.5) | collective-permute-done | bytes 393248 | tf_op jit(solution)/shard_map/ppermute | solution.py:67
  54.9 3.9 %collective-permute-start.6 = (bf16[2,1,64,256]{3,2,1,0:T(8,128)(2,1)S(1)}, bf16[2,1,64,256]{3,2,1,0:T(8,128)(2,1)S(1)}, u32[]{:S(2)}, u32[]{:S(2)}) collective-permute-start(bf16[2,1,64,256]{3,2,1,0:T(8,128)(2,1)S(1)} %get-tuple-element.10), channel_id=1, source_target_pairs={{0,1},{1,2},{2,3},{3,4},{4,5},{5,6},{6,7},{7,8},{8,9},{9,10},{10,1... | collective-permute-start | bytes 196616 | tf_op jit(solution)/shard_map/ppermute | solution.py:19
  58.8 1.3 %collective-permute-start.7 = (bf16[2,1,64,256]{3,2,1,0:T(8,128)(2,1)S(1)}, bf16[2,1,64,256]{3,2,1,0:T(8,128)(2,1)S(1)}, u32[]{:S(2)}, u32[]{:S(2)}) collective-permute-start(bf16[2,1,64,256]{3,2,1,0:T(8,128)(2,1)S(1)} %get-tuple-element.11), channel_id=1, source_target_pairs={{1,0},{2,1},{3,2},{4,3},{5,4},{6,5},{7,6},{8,7},{9,8},{10,9},{11,1... | collective-permute-start | bytes 196616 | tf_op jit(solution)/shard_map/ppermute | solution.py:21
  60.2 9.0 %collective-permute-start.8 = (bf16[1,96,1024]{2,1,0:T(8,128)(2,1)S(1)}, bf16[1,96,1024]{2,1,0:T(8,128)(2,1)S(1)}, u32[]{:S(2)}, u32[]{:S(2)}) collective-permute-start(bf16[1,96,1024]{2,1,0:T(8,128)(2,1)S(1)} %dynamic-slice_convert_fusion.1), channel_id=1, source_target_pairs={{0,384},{96,480},{192,576},{288,672},{384,0},{480,96},{576,192},{6... | collective-permute-start | bytes 589832 | tf_op jit(solution)/shard_map/ppermute | solution.py:67
  70.9 2.6 %collective-permute-done.8 = bf16[1,96,1024]{2,1,0:T(8,128)(2,1)S(1)} collective-permute-done((bf16[1,96,1024]{2,1,0:T(8,128)(2,1)S(1)}, bf16[1,96,1024]{2,1,0:T(8,128)(2,1)S(1)}, u32[]{:S(2)}, u32[]{:S(2)}) %collective-permute-start.8) | collective-permute-done | bytes 196640 | tf_op jit(solution)/shard_map/ppermute | solution.py:67
  73.6 1.2 copy.8
  74.7 21.2 %all-to-all-start = ((f32[96,1,1024]{2,1,0:T(1,128)}), f32[96,1,1024]{2,1,0:T(1,128)S(1)}, u32[]{:S(2)}, u32[]{:S(2)}) async-start(f32[96,1,1024]{2,1,0:T(1,128)} %copy.8), calls=%async_computation | async-start | bytes 786432 | tf_op jit(solution)/shard_map/all_to_all | solution.py:156
  98.3 19.2 %all-to-all-done = f32[96,1,1024]{2,1,0:T(1,128)S(1)} async-done(((f32[96,1,1024]{2,1,0:T(1,128)}), f32[96,1,1024]{2,1,0:T(1,128)S(1)}, u32[]{:S(2)}, u32[]{:S(2)}) %all-to-all-start) | async-done | bytes 393248 | tf_op jit(solution)/shard_map/all_to_all | solution.py:156
  (83 shorter events, 20.2 us)
Async XLA Ops:
  0.6 12.2 %copy-start = (bf16[3,3,256,256]{3,2,1,0:T(8,128)(2,1)S(1)}, bf16[3,3,256,256]{3,2,1,0:T(8,128)(2,1)}, u32[]{:S(2)}) copy-start(bf16[3,3,256,256]{3,2,1,0:T(8,128)(2,1)} %param.6) | copy-start | bytes 3538948
  3.0 8.8 %collective-permute-start = (bf16[2,1,64,256]{3,2,1,0:T(8,128)(2,1)S(1)}, bf16[2,1,64,256]{3,2,1,0:T(8,128)(2,1)S(1)}, u32[]{:S(2)}, u32[]{:S(2)}) collective-permute-start(bf16[2,1,64,256]{3,2,1,0:T(8,128)(2,1)S(1)} %get-tuple-element.12), channel_id=1, source_target_pairs={{0,1},{1,2},{2,3},{3,4},{4,5},{5,6},{6,7},{7,8},{8,9},{9,10},{10,1... | collective-permute-start | bytes 196616 | tf_op jit(solution)/shard_map/ppermute | solution.py:19
  6.5 6.2 %collective-permute-start.1 = (bf16[2,1,64,256]{3,2,1,0:T(8,128)(2,1)S(1)}, bf16[2,1,64,256]{3,2,1,0:T(8,128)(2,1)S(1)}, u32[]{:S(2)}, u32[]{:S(2)}) collective-permute-start(bf16[2,1,64,256]{3,2,1,0:T(8,128)(2,1)S(1)} %get-tuple-element.13), channel_id=1, source_target_pairs={{1,0},{2,1},{3,2},{4,3},{5,4},{6,5},{7,6},{8,7},{9,8},{10,9},{11,1... | collective-permute-start | bytes 196616 | tf_op jit(solution)/shard_map/ppermute | solution.py:21
  7.8 10.2 %collective-permute-start.3 = (bf16[2,4,64,256]{3,2,1,0:T(8,128)(2,1)}, bf16[2,4,64,256]{3,2,1,0:T(8,128)(2,1)S(1)}, u32[]{:S(2)}, u32[]{:S(2)}) collective-permute-start(bf16[2,4,64,256]{3,2,1,0:T(8,128)(2,1)} %param.5), channel_id=1, source_target_pairs={{96,0},{192,96},{288,192},{384,288},{480,384},{576,480},{672,576},... | collective-permute-start | bytes 786440 | tf_op jit(solution)/shard_map/ppermute | solution.py:31
  14.5 2.6 %copy-start.3 = (bf16[2,4,64,256]{3,2,1,0:T(8,128)(2,1)S(1)}, bf16[2,4,64,256]{3,2,1,0:T(8,128)(2,1)}, u32[]{:S(2)}) copy-start(bf16[2,4,64,256]{3,2,1,0:T(8,128)(2,1)} %param.5) | copy-start | bytes 786436
  14.7 4.0 %copy-start.8 = (bf16[3,256,256]{2,1,0:T(8,128)(2,1)S(1)}, bf16[3,256,256]{2,1,0:T(8,128)(2,1)}, u32[]{:S(2)}) copy-start(bf16[3,256,256]{2,1,0:T(8,128)(2,1)} %param.7) | copy-start | bytes 1179652
  14.7 4.3 %copy-start.7 = (f32[2,4,64,256]{3,2,1,0:T(8,128)S(1)}, f32[2,4,64,256]{3,2,1,0:T(8,128)}, u32[]{:S(2)}) copy-start(f32[2,4,64,256]{3,2,1,0:T(8,128)} %fusion.93) | copy-start | bytes 1572868
  15.0 16.8 %copy-start.5 = (bf16[2,4,64,256]{3,2,1,0:T(8,128)(2,1)}, bf16[2,4,64,256]{3,2,1,0:T(8,128)(2,1)S(1)}, u32[]{:S(2)}) copy-start(bf16[2,4,64,256]{3,2,1,0:T(8,128)(2,1)S(1)} %fusion.11) | copy-start | bytes 786436
  15.0 16.5 %collective-permute-start.2 = (bf16[2,4,64,256]{3,2,1,0:T(8,128)(2,1)S(1)}, bf16[2,4,64,256]{3,2,1,0:T(8,128)(2,1)S(1)}, u32[]{:S(2)}, u32[]{:S(2)}) collective-permute-start(bf16[2,4,64,256]{3,2,1,0:T(8,128)(2,1)S(1)} %fusion.11), channel_id=1, source_target_pairs={{0,96},{96,192},{192,288},{288,384},{384,480},{480,576},{576,672},... | collective-permute-start | bytes 786440 | tf_op jit(solution)/shard_map/ppermute | solution.py:31
  18.0 0.7 copy-start.12
  31.5 1.0 copy-start.13
  31.5 0.7 copy-start.10
  34.0 5.6 %collective-permute-start.4 = (f32[4,96,1024]{2,1,0:T(8,128)}, f32[4,96,1024]{2,1,0:T(8,128)}, u32[]{:S(2)}, u32[]{:S(2)}) collective-permute-start(f32[4,96,1024]{2,1,0:T(8,128)} %fusion.1), channel_id=1, source_target_pairs={{0,96},{96,0},{192,288},{288,192},{384,480},{480,384},{576,672},{6... | collective-permute-start | bytes 4718600 | tf_op jit(solution)/shard_map/ppermute | solution.py:69
  37.2 7.9 %copy-start.9 = (bf16[3,256,256]{2,1,0:T(8,128)(2,1)S(1)}, bf16[3,256,256]{2,1,0:T(8,128)(2,1)}, u32[]{:S(2)}) copy-start(bf16[3,256,256]{2,1,0:T(8,128)(2,1)} %param.7) | copy-start | bytes 1179652
  37.2 7.9 %copy-start.11 = (bf16[2,4,64,256]{3,2,1,0:T(8,128)(2,1)S(1)}, bf16[2,4,64,256]{3,2,1,0:T(8,128)(2,1)}, u32[]{:S(2)}) copy-start(bf16[2,4,64,256]{3,2,1,0:T(8,128)(2,1)} %copy-done.10) | copy-start | bytes 786436
  41.3 4.2 %copy-start.2 = (bf16[2,4,64,256]{3,2,1,0:T(8,128)(2,1)S(1)}, bf16[2,4,64,256]{3,2,1,0:T(8,128)(2,1)}, u32[]{:S(2)}) copy-start(bf16[2,4,64,256]{3,2,1,0:T(8,128)(2,1)} %param.4) | copy-start | bytes 786436
  41.3 4.2 %copy-start.6 = (bf16[2,4,64,256]{3,2,1,0:T(8,128)(2,1)S(1)}, bf16[2,4,64,256]{3,2,1,0:T(8,128)(2,1)}, u32[]{:S(2)}) copy-start(bf16[2,4,64,256]{3,2,1,0:T(8,128)(2,1)} %copy-done.5) | copy-start | bytes 786436
  41.3 13.4 %collective-permute-start.5 = (bf16[2,96,1024]{2,1,0:T(8,128)(2,1)S(1)}, bf16[2,96,1024]{2,1,0:T(8,128)(2,1)S(1)}, u32[]{:S(2)}, u32[]{:S(2)}) collective-permute-start(bf16[2,96,1024]{2,1,0:T(8,128)(2,1)S(1)} %fusion.40), channel_id=1, source_target_pairs={{0,192},{96,288},{192,0},{288,96},{384,576},{480,672},{576,384},{6... | collective-permute-start | bytes 1179656 | tf_op jit(solution)/shard_map/ppermute | solution.py:67
  46.4 22.8 %copy-start.1 = (bf16[3,3,256,256]{3,2,1,0:T(8,128)(2,1)S(1)}, bf16[3,3,256,256]{3,2,1,0:T(8,128)(2,1)}, u32[]{:S(2)}) copy-start(bf16[3,3,256,256]{3,2,1,0:T(8,128)(2,1)} %param.6) | copy-start | bytes 3538948
  54.9 14.5 %collective-permute-start.6 = (bf16[2,1,64,256]{3,2,1,0:T(8,128)(2,1)S(1)}, bf16[2,1,64,256]{3,2,1,0:T(8,128)(2,1)S(1)}, u32[]{:S(2)}, u32[]{:S(2)}) collective-permute-start(bf16[2,1,64,256]{3,2,1,0:T(8,128)(2,1)S(1)} %get-tuple-element.10), channel_id=1, source_target_pairs={{0,1},{1,2},{2,3},{3,4},{4,5},{5,6},{6,7},{7,8},{8,9},{9,10},{10,1... | collective-permute-start | bytes 196616 | tf_op jit(solution)/shard_map/ppermute | solution.py:19
  58.8 10.3 %collective-permute-start.7 = (bf16[2,1,64,256]{3,2,1,0:T(8,128)(2,1)S(1)}, bf16[2,1,64,256]{3,2,1,0:T(8,128)(2,1)S(1)}, u32[]{:S(2)}, u32[]{:S(2)}) collective-permute-start(bf16[2,1,64,256]{3,2,1,0:T(8,128)(2,1)S(1)} %get-tuple-element.11), channel_id=1, source_target_pairs={{1,0},{2,1},{3,2},{4,3},{5,4},{6,5},{7,6},{8,7},{9,8},{10,9},{11,1... | collective-permute-start | bytes 196616 | tf_op jit(solution)/shard_map/ppermute | solution.py:21
  60.2 13.4 %collective-permute-start.8 = (bf16[1,96,1024]{2,1,0:T(8,128)(2,1)S(1)}, bf16[1,96,1024]{2,1,0:T(8,128)(2,1)S(1)}, u32[]{:S(2)}, u32[]{:S(2)}) collective-permute-start(bf16[1,96,1024]{2,1,0:T(8,128)(2,1)S(1)} %dynamic-slice_convert_fusion.1), channel_id=1, source_target_pairs={{0,384},{96,480},{192,576},{288,672},{384,0},{480,96},{576,192},{6... | collective-permute-start | bytes 589832 | tf_op jit(solution)/shard_map/ppermute | solution.py:67
  74.7 42.8 %all-to-all-start = ((f32[96,1,1024]{2,1,0:T(1,128)}), f32[96,1,1024]{2,1,0:T(1,128)S(1)}, u32[]{:S(2)}, u32[]{:S(2)}) async-start(f32[96,1,1024]{2,1,0:T(1,128)} %copy.8), calls=%async_computation | async-start | bytes 786432 | tf_op jit(solution)/shard_map/all_to_all | solution.py:156
  96.5 1.0 copy-start.4
  (1 other events, 0.6 us)

commit v7 on v6

--- a/solution.py
+++ b/solution.py
@@ -138,7 +138,7 @@
     temporal_rows = grad_temporal.reshape(devices, -1)
     packed = jnp.concatenate([spatial_rows, temporal_rows], axis=1)
     packed = packed.reshape(time_shards, row_shards, packed.shape[-1])
-    packed, grad_mid_late = halving_scatter(packed, "tm", grad_mid_late, 1, narrow_from=2)
+    packed, grad_mid_late = halving_scatter(packed, "tm", grad_mid_late, 2, narrow_from=2)
     packed = packed[0]
     grad_ext = extended(grad_mid_late, (("height", 1),), 1)
     grad_pad = jnp.pad(grad_ext, ((0, 0), (0, 0), (1, 1), (0, 0)))

time: 120 us -> 121 us (level)
    all_to_all x1, waiting for transfers between devices: 19.2 us -> 12.9 us  [shards(): packed = lax.all_to_all(packed, 'height', 0, 0, tiled=True)]
    ppermute x2, waiting for transfers between devices: 0.01 us -> 2.07 us  [extended(): lax.ppermute(tail, axis, [(i, (i + 1) % count) for i in range(ends)])]
    ppermute x2, waiting for transfers between devices: 11 us -> 12.7 us  [halving_scatter(): lax.ppermute(send.astype(jnp.bfloat16), axis, route).astype(block.dtype)]
    ppermute x1, waiting for transfers between devices: 2.4 us -> 3.67 us  [halving_scatter(): sent = lax.ppermute(send, axis, route)]
    add x2 -> x3, other arithmetic: 1.71 us -> 2.89 us  [halving_scatter(): block = keep + sent]
    unnamed x30 -> x32, local copies, waits for them, and re-layouts: 1.67 us -> 2.83 us
  transfers between devices with their start and end apart: 10 -> 10, of which waited for: 5 -> 6; matrix products, arithmetic and copies ran while one was open for 20% -> 21% of each run, Pallas kernels for 0% -> 0%
where the time goes in v7:
time: 121 us; the launch traced here: 119 us
  starting transfers between devices  49.6 us (41%)
  waiting for transfers between devices  32.3 us (27%)
  matrix products  20.8 us (17%)
  other arithmetic  8.15 us (7%)
  local copies, waits for them, and re-layouts  7.23 us (6%)
  between operations  1.26 us (1%)
    all_to_all x1, starting transfers between devices, shards(): packed = lax.all_to_all(packed, 'height', 0, 0, tiled=True)  22.3 us
    all_to_all x1, waiting for transfers between devices, shards(): packed = lax.all_to_all(packed, 'height', 0, 0, tiled=True)  12.9 us
    ppermute x2, waiting for transfers between devices, halving_scatter(): lax.ppermute(send.astype(jnp.bfloat16), axis, route).astype(block.dtype)  12.7 us
    ppermute x2, starting transfers between devices, halving_scatter(): lax.ppermute(send.astype(jnp.bfloat16), axis, route).astype(block.dtype)  12 us
    dot_general x24, matrix products, flat_dot(): jnp.dot(left.reshape(-1, left.shape[-1]), weight, preferred_element_type=...  10.6 us
    dot_general x12, matrix products, outer_sum(): lax.dot_general(left.reshape(-1, channels), right.reshape(-1, channels),...  10.2 us
    ppermute x2, starting transfers between devices, extended(): lax.ppermute(tail, axis, [(i, (i + 1) % count) for i in range(ends)])  6.74 us
    ppermute x2, starting transfers between devices, shifted(): return lax.ppermute(block, axis, route)  3.97 us
  transfers between devices with their start and end apart: 10, of which 6 were waited for; matrix products, arithmetic and copies ran while one was open for 21% of the time, Pallas kernels for 0%

profile of v7, /device:TPU:6, one launch (start us, length us, event | category | flops | bytes accessed | tf_op | source)
XLA Modules:
  0.0 119.3 jit_solution(13167006338556657322)
XLA Ops:
  0.6 1.2 fusion.34
  1.8 1.2 fusion.29
  3.0 3.5 %collective-permute-start = (bf16[2,1,64,256]{3,2,1,0:T(8,128)(2,1)S(1)}, bf16[2,1,64,256]{3,2,1,0:T(8,128)(2,1)S(1)}, u32[]{:S(2)}, u32[]{:S(2)}) collective-permute-start(bf16[2,1,64,256]{3,2,1,0:T(8,128)(2,1)S(1)} %get-tuple-element.12), channel_id=1, source_target_pairs={{0,1},{1,2},{2,3},{3,4},{4,5},{5,6},{6,7},{7,8},{8,9},{9,10},{10,1... | collective-permute-start | bytes 196616 | tf_op jit(solution)/shard_map/ppermute | solution.py:19
  6.5 1.3 %collective-permute-start.1 = (bf16[2,1,64,256]{3,2,1,0:T(8,128)(2,1)S(1)}, bf16[2,1,64,256]{3,2,1,0:T(8,128)(2,1)S(1)}, u32[]{:S(2)}, u32[]{:S(2)}) collective-permute-start(bf16[2,1,64,256]{3,2,1,0:T(8,128)(2,1)S(1)} %get-tuple-element.13), channel_id=1, source_target_pairs={{1,0},{2,1},{3,2},{4,3},{5,4},{6,5},{7,6},{8,7},{9,8},{10,9},{11,1... | collective-permute-start | bytes 196616 | tf_op jit(solution)/shard_map/ppermute | solution.py:21
  7.8 1.9 %collective-permute-start.3 = (bf16[2,4,64,256]{3,2,1,0:T(8,128)(2,1)}, bf16[2,4,64,256]{3,2,1,0:T(8,128)(2,1)S(1)}, u32[]{:S(2)}, u32[]{:S(2)}) collective-permute-start(bf16[2,4,64,256]{3,2,1,0:T(8,128)(2,1)} %param.5), channel_id=1, source_target_pairs={{96,0},{192,96},{288,192},{384,288},{480,384},{576,480},{672,576},... | collective-permute-start | bytes 786440 | tf_op jit(solution)/shard_map/ppermute | solution.py:31
  9.8 2.1 %fusion.93 = f32[2,4,64,256]{3,2,1,0:T(8,128)} fusion(bf16[2,4,64,256]{3,2,1,0:T(8,128)(2,1)} %param.5, bf16[3,256,256]{2,1,0:T(8,128)(2,1)} %param.7), kind=kOutput, calls=%fused_computation.145 | convolution fusion | flops 67108864 | bytes 917504 | tf_op jit(solution)/shard_map/dot_general | solution.py:41
  15.0 2.1 %collective-permute-start.2 = (bf16[2,4,64,256]{3,2,1,0:T(8,128)(2,1)S(1)}, bf16[2,4,64,256]{3,2,1,0:T(8,128)(2,1)S(1)}, u32[]{:S(2)}, u32[]{:S(2)}) collective-permute-start(bf16[2,4,64,256]{3,2,1,0:T(8,128)(2,1)S(1)} %fusion.11), channel_id=1, source_target_pairs={{0,96},{96,192},{192,288},{288,384},{384,480},{480,576},{576,672},... | collective-permute-start | bytes 786440 | tf_op jit(solution)/shard_map/ppermute | solution.py:31
  19.0 1.2 fusion.12
  28.9 2.6 %concatenate.37 = f32[4,2,96,768]{3,2,1,0:T(8,128)S(1)} reshape(f32[9,256,256]{2,1,0:T(8,128)} %fusion.15) | data formatting | bytes 4718592 | tf_op jit(solution)/shard_map/concatenate | solution.py:139
  32.6 1.4 %fusion.1 = f32[4,96,1024]{2,1,0:T(8,128)} fusion(s32[]{:T(128)S(6)} %select_n.46, f32[4,2,96,768]{3,2,1,0:T(8,128)S(1)} %concatenate.37, f32[4,2,96,256]{3,2,1,0:T(8,128)S(1)} %bitcast.235), kind=kLoop, calls=%fused_computation.5 | loop fusion | flops 393216 | bytes 4718596 | tf_op jit(solution)/shard_map/jit(dynamic_index_in_dim)/squeeze | solution.py:64
  34.0 1.9 %collective-permute-start.4 = (f32[4,96,1024]{2,1,0:T(8,128)}, f32[4,96,1024]{2,1,0:T(8,128)}, u32[]{:S(2)}, u32[]{:S(2)}) collective-permute-start(f32[4,96,1024]{2,1,0:T(8,128)} %fusion.1), channel_id=1, source_target_pairs={{0,96},{96,0},{192,288},{288,192},{384,480},{480,384},{576,672},{6... | collective-permute-start | bytes 4718600 | tf_op jit(solution)/shard_map/ppermute | solution.py:69
  35.9 3.7 %collective-permute-done.4 = f32[4,96,1024]{2,1,0:T(8,128)} collective-permute-done((f32[4,96,1024]{2,1,0:T(8,128)}, f32[4,96,1024]{2,1,0:T(8,128)}, u32[]{:S(2)}, u32[]{:S(2)}) %collective-permute-start.4) | collective-permute-done | bytes 1572896 | tf_op jit(solution)/shard_map/ppermute | solution.py:69
  39.6 1.6 %fusion.4 = f32[4,96,1024]{2,1,0:T(8,128)S(1)} fusion(f32[4,96,1024]{2,1,0:T(8,128)} %collective-permute-done.4, s32[]{:T(128)S(6)} %select_n.45, f32[4,2,96,768]{3,2,1,0:T(8,128)S(1)} %concatenate.37, f32[4,2,96,256]{3,2,1,0:T(8,128)S(1)} %bitcast.236), kind=kLoop, calls=%fused_computation.8 | loop fusion | flops 786432 | bytes 6291460 | tf_op jit(solution)/shard_map/add | solution.py:70
  42.4 3.7 %collective-permute-start.5 = (bf16[2,96,1024]{2,1,0:T(8,128)(2,1)S(1)}, bf16[2,96,1024]{2,1,0:T(8,128)(2,1)S(1)}, u32[]{:S(2)}, u32[]{:S(2)}) collective-permute-start(bf16[2,96,1024]{2,1,0:T(8,128)(2,1)S(1)} %fusion.40), channel_id=1, source_target_pairs={{0,192},{96,288},{192,0},{288,96},{384,576},{480,672},{576,384},{6... | collective-permute-start | bytes 1179656 | tf_op jit(solution)/shard_map/ppermute | solution.py:67
  46.2 1.3 %fusion.95 = f32[2,4,64,256]{3,2,1,0:T(8,128)S(1)} fusion(bf16[2,4,64,256]{3,2,1,0:T(8,128)(2,1)} %copy-done.6, bf16[3,256,256]{2,1,0:T(8,128)(2,1)} %param.7), kind=kOutput, calls=%fused_computation.147 | convolution fusion | flops 67108864 | bytes 917504 | tf_op jit(solution)/shard_map/dot_general | solution.py:41
  47.5 8.3 %collective-permute-done.5 = bf16[2,96,1024]{2,1,0:T(8,128)(2,1)S(1)} collective-permute-done((bf16[2,96,1024]{2,1,0:T(8,128)(2,1)S(1)}, bf16[2,96,1024]{2,1,0:T(8,128)(2,1)S(1)}, u32[]{:S(2)}, u32[]{:S(2)}) %collective-permute-start.5) | collective-permute-done | bytes 393248 | tf_op jit(solution)/shard_map/ppermute | solution.py:67
  55.8 1.2 %bitcast_add_fusion = f32[2,96,1024]{2,1,0:T(8,128)S(1)} fusion(bf16[2,96,1024]{2,1,0:T(8,128)(2,1)S(1)} %collective-permute-done.5, f32[2,2,96,1024]{3,2,1,0:T(8,128)} %bitcast.238, s32[]{:T(128)S(6)} %select_n.49), kind=kLoop, calls=%fused_computation.62 | loop fusion | flops 393216 | bytes 1966084 | tf_op jit(solution)/shard_map/add | solution.py:70
  57.1 8.3 %collective-permute-start.6 = (bf16[1,96,1024]{2,1,0:T(8,128)(2,1)S(1)}, bf16[1,96,1024]{2,1,0:T(8,128)(2,1)S(1)}, u32[]{:S(2)}, u32[]{:S(2)}) collective-permute-start(bf16[1,96,1024]{2,1,0:T(8,128)(2,1)S(1)} %dynamic-slice_convert_fusion.1), channel_id=1, source_target_pairs={{0,384},{96,480},{192,576},{288,672},{384,0},{480,96},{576,192},{6... | collective-permute-start | bytes 589832 | tf_op jit(solution)/shard_map/ppermute | solution.py:67
  65.6 4.4 %collective-permute-done.6 = bf16[1,96,1024]{2,1,0:T(8,128)(2,1)S(1)} collective-permute-done((bf16[1,96,1024]{2,1,0:T(8,128)(2,1)S(1)}, bf16[1,96,1024]{2,1,0:T(8,128)(2,1)S(1)}, u32[]{:S(2)}, u32[]{:S(2)}) %collective-permute-start.6) | collective-permute-done | bytes 196640 | tf_op jit(solution)/shard_map/ppermute | solution.py:67
  70.1 1.4 %collective-permute-start.8 = (bf16[2,1,64,256]{3,2,1,0:T(8,128)(2,1)S(1)}, bf16[2,1,64,256]{3,2,1,0:T(8,128)(2,1)S(1)}, u32[]{:S(2)}, u32[]{:S(2)}) collective-permute-start(bf16[2,1,64,256]{3,2,1,0:T(8,128)(2,1)S(1)} %get-tuple-element.11), channel_id=1, source_target_pairs={{1,0},{2,1},{3,2},{4,3},{5,4},{6,5},{7,6},{8,7},{9,8},{10,9},{11,1... | collective-permute-start | bytes 196616 | tf_op jit(solution)/shard_map/ppermute | solution.py:21
  73.7 22.3 %all-to-all-start = ((f32[96,1,1024]{2,1,0:T(1,128)}), f32[96,1,1024]{2,1,0:T(1,128)S(1)}, u32[]{:S(2)}, u32[]{:S(2)}) async-start(f32[96,1,1024]{2,1,0:T(1,128)} %copy.8), calls=%async_computation | async-start | bytes 786432 | tf_op jit(solution)/shard_map/all_to_all | solution.py:156
  96.0 3.3 %collective-permute-start.7 = (bf16[2,1,64,256]{3,2,1,0:T(8,128)(2,1)S(1)}, bf16[2,1,64,256]{3,2,1,0:T(8,128)(2,1)S(1)}, u32[]{:S(2)}, u32[]{:S(2)}) collective-permute-start(bf16[2,1,64,256]{3,2,1,0:T(8,128)(2,1)S(1)} %get-tuple-element.10), channel_id=1, source_target_pairs={{0,1},{1,2},{2,3},{3,4},{4,5},{5,6},{6,7},{7,8},{8,9},{9,10},{10,1... | collective-permute-start | bytes 196616 | tf_op jit(solution)/shard_map/ppermute | solution.py:19
  99.6 2.1 %collective-permute-done.7 = bf16[2,1,64,256]{3,2,1,0:T(8,128)(2,1)S(1)} collective-permute-done((bf16[2,1,64,256]{3,2,1,0:T(8,128)(2,1)S(1)}, bf16[2,1,64,256]{3,2,1,0:T(8,128)(2,1)S(1)}, u32[]{:S(2)}, u32[]{:S(2)}) %collective-permute-start.7) | collective-permute-done | bytes 65568 | tf_op jit(solution)/shard_map/ppermute | solution.py:19
  105.5 12.9 %all-to-all-done = f32[96,1,1024]{2,1,0:T(1,128)S(1)} async-done(((f32[96,1,1024]{2,1,0:T(1,128)}), f32[96,1,1024]{2,1,0:T(1,128)S(1)}, u32[]{:S(2)}, u32[]{:S(2)}) %all-to-all-start) | async-done | bytes 393248 | tf_op jit(solution)/shard_map/all_to_all | solution.py:156
  (85 shorter events, 23.4 us)
Async XLA Ops:
  0.6 12.2 %copy-start.1 = (bf16[3,3,256,256]{3,2,1,0:T(8,128)(2,1)S(1)}, bf16[3,3,256,256]{3,2,1,0:T(8,128)(2,1)}, u32[]{:S(2)}) copy-start(bf16[3,3,256,256]{3,2,1,0:T(8,128)(2,1)} %param.6) | copy-start | bytes 3538948
  3.0 8.8 %collective-permute-start = (bf16[2,1,64,256]{3,2,1,0:T(8,128)(2,1)S(1)}, bf16[2,1,64,256]{3,2,1,0:T(8,128)(2,1)S(1)}, u32[]{:S(2)}, u32[]{:S(2)}) collective-permute-start(bf16[2,1,64,256]{3,2,1,0:T(8,128)(2,1)S(1)} %get-tuple-element.12), channel_id=1, source_target_pairs={{0,1},{1,2},{2,3},{3,4},{4,5},{5,6},{6,7},{7,8},{8,9},{9,10},{10,1... | collective-permute-start | bytes 196616 | tf_op jit(solution)/shard_map/ppermute | solution.py:19
  6.5 6.2 %collective-permute-start.1 = (bf16[2,1,64,256]{3,2,1,0:T(8,128)(2,1)S(1)}, bf16[2,1,64,256]{3,2,1,0:T(8,128)(2,1)S(1)}, u32[]{:S(2)}, u32[]{:S(2)}) collective-permute-start(bf16[2,1,64,256]{3,2,1,0:T(8,128)(2,1)S(1)} %get-tuple-element.13), channel_id=1, source_target_pairs={{1,0},{2,1},{3,2},{4,3},{5,4},{6,5},{7,6},{8,7},{9,8},{10,9},{11,1... | collective-permute-start | bytes 196616 | tf_op jit(solution)/shard_map/ppermute | solution.py:21
  7.8 10.2 %collective-permute-start.3 = (bf16[2,4,64,256]{3,2,1,0:T(8,128)(2,1)}, bf16[2,4,64,256]{3,2,1,0:T(8,128)(2,1)S(1)}, u32[]{:S(2)}, u32[]{:S(2)}) collective-permute-start(bf16[2,4,64,256]{3,2,1,0:T(8,128)(2,1)} %param.5), channel_id=1, source_target_pairs={{96,0},{192,96},{288,192},{384,288},{480,384},{576,480},{672,576},... | collective-permute-start | bytes 786440 | tf_op jit(solution)/shard_map/ppermute | solution.py:31
  14.5 2.6 %copy-start.4 = (bf16[2,4,64,256]{3,2,1,0:T(8,128)(2,1)S(1)}, bf16[2,4,64,256]{3,2,1,0:T(8,128)(2,1)}, u32[]{:S(2)}) copy-start(bf16[2,4,64,256]{3,2,1,0:T(8,128)(2,1)} %param.5) | copy-start | bytes 786436
  14.7 4.0 %copy-start.9 = (bf16[3,256,256]{2,1,0:T(8,128)(2,1)S(1)}, bf16[3,256,256]{2,1,0:T(8,128)(2,1)}, u32[]{:S(2)}) copy-start(bf16[3,256,256]{2,1,0:T(8,128)(2,1)} %param.7) | copy-start | bytes 1179652
  14.7 4.3 %copy-start.8 = (f32[2,4,64,256]{3,2,1,0:T(8,128)S(1)}, f32[2,4,64,256]{3,2,1,0:T(8,128)}, u32[]{:S(2)}) copy-start(f32[2,4,64,256]{3,2,1,0:T(8,128)} %fusion.93) | copy-start | bytes 1572868
  15.0 16.8 %copy-start.6 = (bf16[2,4,64,256]{3,2,1,0:T(8,128)(2,1)}, bf16[2,4,64,256]{3,2,1,0:T(8,128)(2,1)S(1)}, u32[]{:S(2)}) copy-start(bf16[2,4,64,256]{3,2,1,0:T(8,128)(2,1)S(1)} %fusion.11) | copy-start | bytes 786436
  15.0 16.5 %collective-permute-start.2 = (bf16[2,4,64,256]{3,2,1,0:T(8,128)(2,1)S(1)}, bf16[2,4,64,256]{3,2,1,0:T(8,128)(2,1)S(1)}, u32[]{:S(2)}, u32[]{:S(2)}) collective-permute-start(bf16[2,4,64,256]{3,2,1,0:T(8,128)(2,1)S(1)} %fusion.11), channel_id=1, source_target_pairs={{0,96},{96,192},{192,288},{288,384},{384,480},{480,576},{576,672},... | collective-permute-start | bytes 786440 | tf_op jit(solution)/shard_map/ppermute | solution.py:31
  31.5 1.0 copy-start.14
  31.5 0.7 copy-start.11
  34.0 5.6 %collective-permute-start.4 = (f32[4,96,1024]{2,1,0:T(8,128)}, f32[4,96,1024]{2,1,0:T(8,128)}, u32[]{:S(2)}, u32[]{:S(2)}) collective-permute-start(f32[4,96,1024]{2,1,0:T(8,128)} %fusion.1), channel_id=1, source_target_pairs={{0,96},{96,0},{192,288},{288,192},{384,480},{480,384},{576,672},{6... | collective-permute-start | bytes 4718600 | tf_op jit(solution)/shard_map/ppermute | solution.py:69
  41.2 1.2 copy-start
  42.4 13.3 %collective-permute-start.5 = (bf16[2,96,1024]{2,1,0:T(8,128)(2,1)S(1)}, bf16[2,96,1024]{2,1,0:T(8,128)(2,1)S(1)}, u32[]{:S(2)}, u32[]{:S(2)}) collective-permute-start(bf16[2,96,1024]{2,1,0:T(8,128)(2,1)S(1)} %fusion.40), channel_id=1, source_target_pairs={{0,192},{96,288},{192,0},{288,96},{384,576},{480,672},{576,384},{6... | collective-permute-start | bytes 1179656 | tf_op jit(solution)/shard_map/ppermute | solution.py:67
  46.2 19.2 %copy-start.10 = (bf16[3,256,256]{2,1,0:T(8,128)(2,1)S(1)}, bf16[3,256,256]{2,1,0:T(8,128)(2,1)}, u32[]{:S(2)}) copy-start(bf16[3,256,256]{2,1,0:T(8,128)(2,1)} %param.7) | copy-start | bytes 1179652
  46.2 19.2 %copy-start.12 = (bf16[2,4,64,256]{3,2,1,0:T(8,128)(2,1)S(1)}, bf16[2,4,64,256]{3,2,1,0:T(8,128)(2,1)}, u32[]{:S(2)}) copy-start(bf16[2,4,64,256]{3,2,1,0:T(8,128)(2,1)} %copy-done.11) | copy-start | bytes 786436
  57.0 14.6 %copy-start.3 = (bf16[2,4,64,256]{3,2,1,0:T(8,128)(2,1)S(1)}, bf16[2,4,64,256]{3,2,1,0:T(8,128)(2,1)}, u32[]{:S(2)}) copy-start(bf16[2,4,64,256]{3,2,1,0:T(8,128)(2,1)} %param.4) | copy-start | bytes 786436
  57.0 14.6 %copy-start.7 = (bf16[2,4,64,256]{3,2,1,0:T(8,128)(2,1)S(1)}, bf16[2,4,64,256]{3,2,1,0:T(8,128)(2,1)}, u32[]{:S(2)}) copy-start(bf16[2,4,64,256]{3,2,1,0:T(8,128)(2,1)} %copy-done.6) | copy-start | bytes 786436
  57.1 13.0 %collective-permute-start.6 = (bf16[1,96,1024]{2,1,0:T(8,128)(2,1)S(1)}, bf16[1,96,1024]{2,1,0:T(8,128)(2,1)S(1)}, u32[]{:S(2)}, u32[]{:S(2)}) collective-permute-start(bf16[1,96,1024]{2,1,0:T(8,128)(2,1)S(1)} %dynamic-slice_convert_fusion.1), channel_id=1, source_target_pairs={{0,384},{96,480},{192,576},{288,672},{384,0},{480,96},{576,192},{6... | collective-permute-start | bytes 589832 | tf_op jit(solution)/shard_map/ppermute | solution.py:67
  70.1 29.2 %copy-start.2 = (bf16[3,3,256,256]{3,2,1,0:T(8,128)(2,1)S(1)}, bf16[3,3,256,256]{3,2,1,0:T(8,128)(2,1)}, u32[]{:S(2)}) copy-start(bf16[3,3,256,256]{3,2,1,0:T(8,128)(2,1)} %param.6) | copy-start | bytes 3538948
  70.1 29.1 %collective-permute-start.8 = (bf16[2,1,64,256]{3,2,1,0:T(8,128)(2,1)S(1)}, bf16[2,1,64,256]{3,2,1,0:T(8,128)(2,1)S(1)}, u32[]{:S(2)}, u32[]{:S(2)}) collective-permute-start(bf16[2,1,64,256]{3,2,1,0:T(8,128)(2,1)S(1)} %get-tuple-element.11), channel_id=1, source_target_pairs={{1,0},{2,1},{3,2},{4,3},{5,4},{6,5},{7,6},{8,7},{9,8},{10,9},{11,1... | collective-permute-start | bytes 196616 | tf_op jit(solution)/shard_map/ppermute | solution.py:21
  73.7 44.7 %all-to-all-start = ((f32[96,1,1024]{2,1,0:T(1,128)}), f32[96,1,1024]{2,1,0:T(1,128)S(1)}, u32[]{:S(2)}, u32[]{:S(2)}) async-start(f32[96,1,1024]{2,1,0:T(1,128)} %copy.8), calls=%async_computation | async-start | bytes 786432 | tf_op jit(solution)/shard_map/all_to_all | solution.py:156
  96.0 5.6 %collective-permute-start.7 = (bf16[2,1,64,256]{3,2,1,0:T(8,128)(2,1)S(1)}, bf16[2,1,64,256]{3,2,1,0:T(8,128)(2,1)S(1)}, u32[]{:S(2)}, u32[]{:S(2)}) collective-permute-start(bf16[2,1,64,256]{3,2,1,0:T(8,128)(2,1)S(1)} %get-tuple-element.10), channel_id=1, source_target_pairs={{0,1},{1,2},{2,3},{3,4},{4,5},{5,6},{6,7},{7,8},{8,9},{9,10},{10,1... | collective-permute-start | bytes 196616 | tf_op jit(solution)/shard_map/ppermute | solution.py:19
  103.7 1.0 copy-start.5
  (2 other events, 1.3 us)

commit v8 on v7

--- a/solution.py
+++ b/solution.py
@@ -153,8 +153,8 @@
             )
     unused, pullback = jax.vjp(activate, clip_wide)
     grad_clip = (cotangent.astype(jnp.float32) + pullback(grad_act)[0]).astype(jnp.bfloat16)
-    packed = lax.all_to_all(packed, "height", 0, 0, tiled=True)
-    packed = jnp.sum(packed, axis=0)
+    packed = lax.all_to_all(packed.astype(jnp.bfloat16), "height", 0, 0, tiled=True)
+    packed = jnp.sum(packed.astype(jnp.float32), axis=0)
     packed = packed * grad_scale
     spatial_part = packed[: spatial_rows.shape[1]]
     temporal_part = packed[spatial_rows.shape[1] :]

time: 121 us -> 120 us (level)
  waiting for transfers between devices: 32.3 us -> 29.1 us
    ppermute x2, waiting for transfers between devices: 2.07 us -> 0.01 us  [extended(): lax.ppermute(tail, axis, [(i, (i + 1) % count) for i in range(ends)])]
    unnamed x32 -> x34, local copies, waits for them, and re-layouts: 2.83 us -> 3.77 us
  transfers between devices with their start and end apart: 10 -> 10, of which waited for: 6 -> 5; matrix products, arithmetic and copies ran while one was open for 21% -> 22% of each run, Pallas kernels for 0% -> 0%
where the time goes in v8:
time: 120 us; the launch traced here: 118 us
  starting transfers between devices  50 us (42%)
  waiting for transfers between devices  29.1 us (24%)
  matrix products  20.9 us (17%)
  other arithmetic  8.98 us (7%)
  local copies, waits for them, and re-layouts  7.52 us (6%)
  between operations  1.27 us (1%)
    all_to_all x1, starting transfers between devices, shards(): lax.all_to_all(packed.astype(jnp.bfloat16), 'height', 0, 0, tiled=True)  21.4 us
    ppermute x2, waiting for transfers between devices, halving_scatter(): lax.ppermute(send.astype(jnp.bfloat16), axis, route).astype(block.dtype)  12.7 us
    ppermute x2, starting transfers between devices, halving_scatter(): lax.ppermute(send.astype(jnp.bfloat16), axis, route).astype(block.dtype)  12.1 us
    all_to_all x1, waiting for transfers between devices, shards(): lax.all_to_all(packed.astype(jnp.bfloat16), 'height', 0, 0, tiled=True)  11.8 us
    dot_general x24, matrix products, flat_dot(): jnp.dot(left.reshape(-1, left.shape[-1]), weight, preferred_element_type=...  10.6 us
    dot_general x12, matrix products, outer_sum(): lax.dot_general(left.reshape(-1, channels), right.reshape(-1, channels),...  10.3 us
    ppermute x2, starting transfers between devices, extended(): lax.ppermute(tail, axis, [(i, (i + 1) % count) for i in range(ends)])  7.92 us
    ppermute x2, starting transfers between devices, shifted(): return lax.ppermute(block, axis, route)  3.97 us
  transfers between devices with their start and end apart: 10, of which 5 were waited for; matrix products, arithmetic and copies ran while one was open for 22% of the time, Pallas kernels for 0%

profile of v8, /device:TPU:6, one launch (start us, length us, event | category | flops | bytes accessed | tf_op | source)
XLA Modules:
  0.0 117.7 jit_solution(12178920175373556863)
XLA Ops:
  0.6 1.2 %fusion.34 = f32[2,4,64]{2,1,0:T(4,128)S(1)} fusion(bf16[2,4,64,256]{3,2,1,0:T(8,128)(2,1)} %param.4), kind=kLoop, calls=%fused_computation.77 | loop fusion | flops 392704 | bytes 264192 | tf_op jit(solution)/shard_map/reduce_sum | solution.py:35
  1.8 1.2 fusion.29
  3.0 3.5 %collective-permute-start = (bf16[2,1,64,256]{3,2,1,0:T(8,128)(2,1)S(1)}, bf16[2,1,64,256]{3,2,1,0:T(8,128)(2,1)S(1)}, u32[]{:S(2)}, u32[]{:S(2)}) collective-permute-start(bf16[2,1,64,256]{3,2,1,0:T(8,128)(2,1)S(1)} %get-tuple-element.12), channel_id=1, source_target_pairs={{0,1},{1,2},{2,3},{3,4},{4,5},{5,6},{6,7},{7,8},{8,9},{9,10},{10,1... | collective-permute-start | bytes 196616 | tf_op jit(solution)/shard_map/ppermute | solution.py:19
  6.5 1.3 %collective-permute-start.1 = (bf16[2,1,64,256]{3,2,1,0:T(8,128)(2,1)S(1)}, bf16[2,1,64,256]{3,2,1,0:T(8,128)(2,1)S(1)}, u32[]{:S(2)}, u32[]{:S(2)}) collective-permute-start(bf16[2,1,64,256]{3,2,1,0:T(8,128)(2,1)S(1)} %get-tuple-element.13), channel_id=1, source_target_pairs={{1,0},{2,1},{3,2},{4,3},{5,4},{6,5},{7,6},{8,7},{9,8},{10,9},{11,1... | collective-permute-start | bytes 196616 | tf_op jit(solution)/shard_map/ppermute | solution.py:21
  7.8 1.9 %collective-permute-start.3 = (bf16[2,4,64,256]{3,2,1,0:T(8,128)(2,1)}, bf16[2,4,64,256]{3,2,1,0:T(8,128)(2,1)S(1)}, u32[]{:S(2)}, u32[]{:S(2)}) collective-permute-start(bf16[2,4,64,256]{3,2,1,0:T(8,128)(2,1)} %param.5), channel_id=1, source_target_pairs={{96,0},{192,96},{288,192},{384,288},{480,384},{576,480},{672,576},... | collective-permute-start | bytes 786440 | tf_op jit(solution)/shard_map/ppermute | solution.py:31
  9.8 2.1 %fusion.93 = f32[2,4,64,256]{3,2,1,0:T(8,128)} fusion(bf16[2,4,64,256]{3,2,1,0:T(8,128)(2,1)} %param.5, bf16[3,256,256]{2,1,0:T(8,128)(2,1)} %param.7), kind=kOutput, calls=%fused_computation.147 | convolution fusion | flops 67108864 | bytes 917504 | tf_op jit(solution)/shard_map/dot_general | solution.py:41
  15.0 2.1 %collective-permute-start.2 = (bf16[2,4,64,256]{3,2,1,0:T(8,128)(2,1)S(1)}, bf16[2,4,64,256]{3,2,1,0:T(8,128)(2,1)S(1)}, u32[]{:S(2)}, u32[]{:S(2)}) collective-permute-start(bf16[2,4,64,256]{3,2,1,0:T(8,128)(2,1)S(1)} %fusion.11), channel_id=1, source_target_pairs={{0,96},{96,192},{192,288},{288,384},{384,480},{480,576},{576,672},... | collective-permute-start | bytes 786440 | tf_op jit(solution)/shard_map/ppermute | solution.py:31
  19.0 1.2 fusion.12
  28.9 2.6 %concatenate.37 = f32[4,2,96,768]{3,2,1,0:T(8,128)S(1)} reshape(f32[9,256,256]{2,1,0:T(8,128)} %fusion.15) | data formatting | bytes 4718592 | tf_op jit(solution)/shard_map/concatenate | solution.py:139
  32.6 1.4 %fusion.1 = f32[4,96,1024]{2,1,0:T(8,128)} fusion(s32[]{:T(128)S(6)} %select_n.46, f32[4,2,96,768]{3,2,1,0:T(8,128)S(1)} %concatenate.37, f32[4,2,96,256]{3,2,1,0:T(8,128)S(1)} %bitcast.237), kind=kLoop, calls=%fused_computation.5 | loop fusion | flops 393216 | bytes 4718596 | tf_op jit(solution)/shard_map/jit(dynamic_index_in_dim)/squeeze | solution.py:64
  34.0 1.9 %collective-permute-start.4 = (f32[4,96,1024]{2,1,0:T(8,128)}, f32[4,96,1024]{2,1,0:T(8,128)}, u32[]{:S(2)}, u32[]{:S(2)}) collective-permute-start(f32[4,96,1024]{2,1,0:T(8,128)} %fusion.1), channel_id=1, source_target_pairs={{0,96},{96,0},{192,288},{288,192},{384,480},{480,384},{576,672},{6... | collective-permute-start | bytes 4718600 | tf_op jit(solution)/shard_map/ppermute | solution.py:69
  36.0 3.7 %collective-permute-done.4 = f32[4,96,1024]{2,1,0:T(8,128)} collective-permute-done((f32[4,96,1024]{2,1,0:T(8,128)}, f32[4,96,1024]{2,1,0:T(8,128)}, u32[]{:S(2)}, u32[]{:S(2)}) %collective-permute-start.4) | collective-permute-done | bytes 1572896 | tf_op jit(solution)/shard_map/ppermute | solution.py:69
  39.7 1.6 %fusion.4 = f32[4,96,1024]{2,1,0:T(8,128)S(1)} fusion(f32[4,96,1024]{2,1,0:T(8,128)} %collective-permute-done.4, s32[]{:T(128)S(6)} %select_n.45, f32[4,2,96,768]{3,2,1,0:T(8,128)S(1)} %concatenate.37, f32[4,2,96,256]{3,2,1,0:T(8,128)S(1)} %bitcast.238), kind=kLoop, calls=%fused_computation.8 | loop fusion | flops 786432 | bytes 6291460 | tf_op jit(solution)/shard_map/add | solution.py:70
  41.3 1.2 copy-done
  42.5 3.7 %collective-permute-start.5 = (bf16[2,96,1024]{2,1,0:T(8,128)(2,1)S(1)}, bf16[2,96,1024]{2,1,0:T(8,128)(2,1)S(1)}, u32[]{:S(2)}, u32[]{:S(2)}) collective-permute-start(bf16[2,96,1024]{2,1,0:T(8,128)(2,1)S(1)} %fusion.40), channel_id=1, source_target_pairs={{0,192},{96,288},{192,0},{288,96},{384,576},{480,672},{576,384},{6... | collective-permute-start | bytes 1179656 | tf_op jit(solution)/shard_map/ppermute | solution.py:67
  46.3 1.3 %fusion.95 = f32[2,4,64,256]{3,2,1,0:T(8,128)S(1)} fusion(bf16[2,4,64,256]{3,2,1,0:T(8,128)(2,1)} %copy-done.6, bf16[3,256,256]{2,1,0:T(8,128)(2,1)} %param.7), kind=kOutput, calls=%fused_computation.149 | convolution fusion | flops 67108864 | bytes 917504 | tf_op jit(solution)/shard_map/dot_general | solution.py:41
  47.5 8.3 %collective-permute-done.5 = bf16[2,96,1024]{2,1,0:T(8,128)(2,1)S(1)} collective-permute-done((bf16[2,96,1024]{2,1,0:T(8,128)(2,1)S(1)}, bf16[2,96,1024]{2,1,0:T(8,128)(2,1)S(1)}, u32[]{:S(2)}, u32[]{:S(2)}) %collective-permute-start.5) | collective-permute-done | bytes 393248 | tf_op jit(solution)/shard_map/ppermute | solution.py:67
  55.8 1.2 %bitcast_add_fusion = f32[2,96,1024]{2,1,0:T(8,128)S(1)} fusion(bf16[2,96,1024]{2,1,0:T(8,128)(2,1)S(1)} %collective-permute-done.5, f32[2,2,96,1024]{3,2,1,0:T(8,128)} %bitcast.240, s32[]{:T(128)S(6)} %select_n.49), kind=kLoop, calls=%fused_computation.62 | loop fusion | flops 393216 | bytes 1966084 | tf_op jit(solution)/shard_map/add | solution.py:70
  57.1 8.4 %collective-permute-start.6 = (bf16[1,96,1024]{2,1,0:T(8,128)(2,1)S(1)}, bf16[1,96,1024]{2,1,0:T(8,128)(2,1)S(1)}, u32[]{:S(2)}, u32[]{:S(2)}) collective-permute-start(bf16[1,96,1024]{2,1,0:T(8,128)(2,1)S(1)} %dynamic-slice_convert_fusion.1), channel_id=1, source_target_pairs={{0,384},{96,480},{192,576},{288,672},{384,0},{480,96},{576,192},{6... | collective-permute-start | bytes 589832 | tf_op jit(solution)/shard_map/ppermute | solution.py:67
  65.8 4.4 %collective-permute-done.6 = bf16[1,96,1024]{2,1,0:T(8,128)(2,1)S(1)} collective-permute-done((bf16[1,96,1024]{2,1,0:T(8,128)(2,1)S(1)}, bf16[1,96,1024]{2,1,0:T(8,128)(2,1)S(1)}, u32[]{:S(2)}, u32[]{:S(2)}) %collective-permute-start.6) | collective-permute-done | bytes 196640 | tf_op jit(solution)/shard_map/ppermute | solution.py:67
  70.3 4.4 %collective-permute-start.7 = (bf16[2,1,64,256]{3,2,1,0:T(8,128)(2,1)S(1)}, bf16[2,1,64,256]{3,2,1,0:T(8,128)(2,1)S(1)}, u32[]{:S(2)}, u32[]{:S(2)}) collective-permute-start(bf16[2,1,64,256]{3,2,1,0:T(8,128)(2,1)S(1)} %get-tuple-element.10), channel_id=1, source_target_pairs={{0,1},{1,2},{2,3},{3,4},{4,5},{5,6},{6,7},{7,8},{8,9},{9,10},{10,1... | collective-permute-start | bytes 196616 | tf_op jit(solution)/shard_map/ppermute | solution.py:19
  74.8 1.4 %collective-permute-start.8 = (bf16[2,1,64,256]{3,2,1,0:T(8,128)(2,1)S(1)}, bf16[2,1,64,256]{3,2,1,0:T(8,128)(2,1)S(1)}, u32[]{:S(2)}, u32[]{:S(2)}) collective-permute-start(bf16[2,1,64,256]{3,2,1,0:T(8,128)(2,1)S(1)} %get-tuple-element.11), channel_id=1, source_target_pairs={{1,0},{2,1},{3,2},{4,3},{5,4},{6,5},{7,6},{8,7},{9,8},{10,9},{11,1... | collective-permute-start | bytes 196616 | tf_op jit(solution)/shard_map/ppermute | solution.py:21
  79.2 21.4 %all-to-all-start = ((bf16[96,2,512]{2,1,0:T(2,128)(2,1)}), bf16[96,2,512]{2,1,0:T(2,128)(2,1)S(1)}, u32[]{:S(2)}, u32[]{:S(2)}) async-start(bf16[96,2,512]{2,1,0:T(2,128)(2,1)} %reshape.200), calls=%async_computation | async-start | bytes 393216 | tf_op jit(solution)/shard_map/all_to_all | solution.py:156
  104.8 11.8 %all-to-all-done = bf16[96,2,512]{2,1,0:T(2,128)(2,1)S(1)} async-done(((bf16[96,2,512]{2,1,0:T(2,128)(2,1)}), bf16[96,2,512]{2,1,0:T(2,128)(2,1)S(1)}, u32[]{:S(2)}, u32[]{:S(2)}) %all-to-all-start) | async-done | bytes 196640 | tf_op jit(solution)/shard_map/all_to_all | solution.py:156
  (88 shorter events, 23.4 us)
Async XLA Ops:
  0.6 12.2 %copy-start.1 = (bf16[3,3,256,256]{3,2,1,0:T(8,128)(2,1)S(1)}, bf16[3,3,256,256]{3,2,1,0:T(8,128)(2,1)}, u32[]{:S(2)}) copy-start(bf16[3,3,256,256]{3,2,1,0:T(8,128)(2,1)} %param.6) | copy-start | bytes 3538948
  3.0 8.8 %collective-permute-start = (bf16[2,1,64,256]{3,2,1,0:T(8,128)(2,1)S(1)}, bf16[2,1,64,256]{3,2,1,0:T(8,128)(2,1)S(1)}, u32[]{:S(2)}, u32[]{:S(2)}) collective-permute-start(bf16[2,1,64,256]{3,2,1,0:T(8,128)(2,1)S(1)} %get-tuple-element.12), channel_id=1, source_target_pairs={{0,1},{1,2},{2,3},{3,4},{4,5},{5,6},{6,7},{7,8},{8,9},{9,10},{10,1... | collective-permute-start | bytes 196616 | tf_op jit(solution)/shard_map/ppermute | solution.py:19
  6.5 6.2 %collective-permute-start.1 = (bf16[2,1,64,256]{3,2,1,0:T(8,128)(2,1)S(1)}, bf16[2,1,64,256]{3,2,1,0:T(8,128)(2,1)S(1)}, u32[]{:S(2)}, u32[]{:S(2)}) collective-permute-start(bf16[2,1,64,256]{3,2,1,0:T(8,128)(2,1)S(1)} %get-tuple-element.13), channel_id=1, source_target_pairs={{1,0},{2,1},{3,2},{4,3},{5,4},{6,5},{7,6},{8,7},{9,8},{10,9},{11,1... | collective-permute-start | bytes 196616 | tf_op jit(solution)/shard_map/ppermute | solution.py:21
  7.8 10.2 %collective-permute-start.3 = (bf16[2,4,64,256]{3,2,1,0:T(8,128)(2,1)}, bf16[2,4,64,256]{3,2,1,0:T(8,128)(2,1)S(1)}, u32[]{:S(2)}, u32[]{:S(2)}) collective-permute-start(bf16[2,4,64,256]{3,2,1,0:T(8,128)(2,1)} %param.5), channel_id=1, source_target_pairs={{96,0},{192,96},{288,192},{384,288},{480,384},{576,480},{672,576},... | collective-permute-start | bytes 786440 | tf_op jit(solution)/shard_map/ppermute | solution.py:31
  14.5 2.6 %copy-start.4 = (bf16[2,4,64,256]{3,2,1,0:T(8,128)(2,1)S(1)}, bf16[2,4,64,256]{3,2,1,0:T(8,128)(2,1)}, u32[]{:S(2)}) copy-start(bf16[2,4,64,256]{3,2,1,0:T(8,128)(2,1)} %param.5) | copy-start | bytes 786436
  14.7 4.0 %copy-start.9 = (bf16[3,256,256]{2,1,0:T(8,128)(2,1)S(1)}, bf16[3,256,256]{2,1,0:T(8,128)(2,1)}, u32[]{:S(2)}) copy-start(bf16[3,256,256]{2,1,0:T(8,128)(2,1)} %param.7) | copy-start | bytes 1179652
  14.7 4.3 %copy-start.8 = (f32[2,4,64,256]{3,2,1,0:T(8,128)S(1)}, f32[2,4,64,256]{3,2,1,0:T(8,128)}, u32[]{:S(2)}) copy-start(f32[2,4,64,256]{3,2,1,0:T(8,128)} %fusion.93) | copy-start | bytes 1572868
  15.0 16.9 %copy-start.6 = (bf16[2,4,64,256]{3,2,1,0:T(8,128)(2,1)}, bf16[2,4,64,256]{3,2,1,0:T(8,128)(2,1)S(1)}, u32[]{:S(2)}) copy-start(bf16[2,4,64,256]{3,2,1,0:T(8,128)(2,1)S(1)} %fusion.11) | copy-start | bytes 786436
  15.0 16.5 %collective-permute-start.2 = (bf16[2,4,64,256]{3,2,1,0:T(8,128)(2,1)S(1)}, bf16[2,4,64,256]{3,2,1,0:T(8,128)(2,1)S(1)}, u32[]{:S(2)}, u32[]{:S(2)}) collective-permute-start(bf16[2,4,64,256]{3,2,1,0:T(8,128)(2,1)S(1)} %fusion.11), channel_id=1, source_target_pairs={{0,96},{96,192},{192,288},{288,384},{384,480},{480,576},{576,672},... | collective-permute-start | bytes 786440 | tf_op jit(solution)/shard_map/ppermute | solution.py:31
  31.5 1.0 copy-start.14
  31.5 0.7 copy-start.11
  34.0 5.6 %collective-permute-start.4 = (f32[4,96,1024]{2,1,0:T(8,128)}, f32[4,96,1024]{2,1,0:T(8,128)}, u32[]{:S(2)}, u32[]{:S(2)}) collective-permute-start(f32[4,96,1024]{2,1,0:T(8,128)} %fusion.1), channel_id=1, source_target_pairs={{0,96},{96,0},{192,288},{288,192},{384,480},{480,384},{576,672},{6... | collective-permute-start | bytes 4718600 | tf_op jit(solution)/shard_map/ppermute | solution.py:69
  41.3 1.2 copy-start
  42.5 13.3 %collective-permute-start.5 = (bf16[2,96,1024]{2,1,0:T(8,128)(2,1)S(1)}, bf16[2,96,1024]{2,1,0:T(8,128)(2,1)S(1)}, u32[]{:S(2)}, u32[]{:S(2)}) collective-permute-start(bf16[2,96,1024]{2,1,0:T(8,128)(2,1)S(1)} %fusion.40), channel_id=1, source_target_pairs={{0,192},{96,288},{192,0},{288,96},{384,576},{480,672},{576,384},{6... | collective-permute-start | bytes 1179656 | tf_op jit(solution)/shard_map/ppermute | solution.py:67
  46.2 19.3 %copy-start.10 = (bf16[3,256,256]{2,1,0:T(8,128)(2,1)S(1)}, bf16[3,256,256]{2,1,0:T(8,128)(2,1)}, u32[]{:S(2)}) copy-start(bf16[3,256,256]{2,1,0:T(8,128)(2,1)} %param.7) | copy-start | bytes 1179652
  46.2 19.3 %copy-start.12 = (bf16[2,4,64,256]{3,2,1,0:T(8,128)(2,1)S(1)}, bf16[2,4,64,256]{3,2,1,0:T(8,128)(2,1)}, u32[]{:S(2)}) copy-start(bf16[2,4,64,256]{3,2,1,0:T(8,128)(2,1)} %copy-done.11) | copy-start | bytes 786436
  57.1 19.1 %copy-start.3 = (bf16[2,4,64,256]{3,2,1,0:T(8,128)(2,1)S(1)}, bf16[2,4,64,256]{3,2,1,0:T(8,128)(2,1)}, u32[]{:S(2)}) copy-start(bf16[2,4,64,256]{3,2,1,0:T(8,128)(2,1)} %param.4) | copy-start | bytes 786436
  57.1 19.1 %copy-start.7 = (bf16[2,4,64,256]{3,2,1,0:T(8,128)(2,1)S(1)}, bf16[2,4,64,256]{3,2,1,0:T(8,128)(2,1)}, u32[]{:S(2)}) copy-start(bf16[2,4,64,256]{3,2,1,0:T(8,128)(2,1)} %copy-done.6) | copy-start | bytes 786436
  57.1 13.1 %collective-permute-start.6 = (bf16[1,96,1024]{2,1,0:T(8,128)(2,1)S(1)}, bf16[1,96,1024]{2,1,0:T(8,128)(2,1)S(1)}, u32[]{:S(2)}, u32[]{:S(2)}) collective-permute-start(bf16[1,96,1024]{2,1,0:T(8,128)(2,1)S(1)} %dynamic-slice_convert_fusion.1), channel_id=1, source_target_pairs={{0,384},{96,480},{192,576},{288,672},{384,0},{480,96},{576,192},{6... | collective-permute-start | bytes 589832 | tf_op jit(solution)/shard_map/ppermute | solution.py:67
  70.3 30.3 %collective-permute-start.7 = (bf16[2,1,64,256]{3,2,1,0:T(8,128)(2,1)S(1)}, bf16[2,1,64,256]{3,2,1,0:T(8,128)(2,1)S(1)}, u32[]{:S(2)}, u32[]{:S(2)}) collective-permute-start(bf16[2,1,64,256]{3,2,1,0:T(8,128)(2,1)S(1)} %get-tuple-element.10), channel_id=1, source_target_pairs={{0,1},{1,2},{2,3},{3,4},{4,5},{5,6},{6,7},{7,8},{8,9},{9,10},{10,1... | collective-permute-start | bytes 196616 | tf_op jit(solution)/shard_map/ppermute | solution.py:19
  74.8 26.0 %copy-start.2 = (bf16[3,3,256,256]{3,2,1,0:T(8,128)(2,1)S(1)}, bf16[3,3,256,256]{3,2,1,0:T(8,128)(2,1)}, u32[]{:S(2)}) copy-start(bf16[3,3,256,256]{3,2,1,0:T(8,128)(2,1)} %param.6) | copy-start | bytes 3538948
  74.8 25.9 %collective-permute-start.8 = (bf16[2,1,64,256]{3,2,1,0:T(8,128)(2,1)S(1)}, bf16[2,1,64,256]{3,2,1,0:T(8,128)(2,1)S(1)}, u32[]{:S(2)}, u32[]{:S(2)}) collective-permute-start(bf16[2,1,64,256]{3,2,1,0:T(8,128)(2,1)S(1)} %get-tuple-element.11), channel_id=1, source_target_pairs={{1,0},{2,1},{3,2},{4,3},{5,4},{6,5},{7,6},{8,7},{9,8},{10,9},{11,1... | collective-permute-start | bytes 196616 | tf_op jit(solution)/shard_map/ppermute | solution.py:21
  79.2 37.4 %all-to-all-start = ((bf16[96,2,512]{2,1,0:T(2,128)(2,1)}), bf16[96,2,512]{2,1,0:T(2,128)(2,1)S(1)}, u32[]{:S(2)}, u32[]{:S(2)}) async-start(bf16[96,2,512]{2,1,0:T(2,128)(2,1)} %reshape.200), calls=%async_computation | async-start | bytes 393216 | tf_op jit(solution)/shard_map/all_to_all | solution.py:156
  103.0 1.0 copy-start.5
  (2 other events, 1.3 us)

commit v9 on v7

--- a/solution.py
+++ b/solution.py
@@ -119,16 +119,14 @@
             for time_lag in range(3)
         ]
     )
-    terms = []
-    for tap_row in range(3):
-        for tap_col in range(3):
-            terms.append(
-                outer_sum(
-                    padded[:, tap_row : tap_row + row_count, tap_col : tap_col + col_count],
-                    grad_mid,
-                )
-            )
-    grad_spatial = jnp.stack(terms)
+    grad_spatial = lax.conv_general_dilated(
+        padded,
+        grad_mid,
+        window_strides=(1, 1),
+        padding="VALID",
+        dimension_numbers=("CHWN", "IHWO", "HWNC"),
+        preferred_element_type=jnp.float32,
+    ).reshape(9, channels, channels)
     grad_mid_late, unused_history = lax.optimization_barrier((grad_mid, earlier))
     time_shards = lax.axis_size("tm")
     row_shards = lax.axis_size("height")

time: 121 us -> 116 us (0.959)
  matrix products: 20.8 us -> 16.5 us
    dot_general x12 -> x3, matrix products: 10.2 us -> 1.49 us  [outer_sum(): lax.dot_general(left.reshape(-1, channels), right.reshape(-1, channels),...]
    conv_general_dilated x0 -> x1, matrix products: none -> 3.59 us  [shards(): lax.conv_general_dilated(padded, grad_mid, window_strides=(1, 1), padding...]
    unnamed x32 -> x30, local copies, waits for them, and re-layouts: 2.83 us -> 2.13 us
  transfers between devices with their start and end apart: 10 -> 10, of which waited for: 6 -> 6; matrix products, arithmetic and copies ran while one was open for 21% -> 18% of each run, Pallas kernels for 0% -> 0%
where the time goes in v9:
time: 116 us; the launch traced here: 114 us
  starting transfers between devices  49.6 us (43%)
  waiting for transfers between devices  32.4 us (28%)
  matrix products  16.5 us (14%)
  other arithmetic  8.12 us (7%)
  local copies, waits for them, and re-layouts  6.53 us (6%)
  between operations  1.25 us (1%)
    all_to_all x1, starting transfers between devices, shards(): packed = lax.all_to_all(packed, 'height', 0, 0, tiled=True)  22.4 us
    all_to_all x1, waiting for transfers between devices, shards(): packed = lax.all_to_all(packed, 'height', 0, 0, tiled=True)  12.9 us
    ppermute x2, waiting for transfers between devices, halving_scatter(): lax.ppermute(send.astype(jnp.bfloat16), axis, route).astype(block.dtype)  12.8 us
    ppermute x2, starting transfers between devices, halving_scatter(): lax.ppermute(send.astype(jnp.bfloat16), axis, route).astype(block.dtype)  11.8 us
    dot_general x24, matrix products, flat_dot(): jnp.dot(left.reshape(-1, left.shape[-1]), weight, preferred_element_type=...  11.4 us
    ppermute x2, starting transfers between devices, extended(): lax.ppermute(tail, axis, [(i, (i + 1) % count) for i in range(ends)])  6.74 us
    ppermute x2, starting transfers between devices, shifted(): return lax.ppermute(block, axis, route)  4.2 us
    ppermute x1, waiting for transfers between devices, halving_scatter(): sent = lax.ppermute(send, axis, route)  3.67 us
  transfers between devices with their start and end apart: 10, of which 6 were waited for; matrix products, arithmetic and copies ran while one was open for 18% of the time, Pallas kernels for 0%

profile of v9, /device:TPU:6, one launch (start us, length us, event | category | flops | bytes accessed | tf_op | source)
XLA Modules:
  0.0 114.5 jit_solution(10574525362265917312)
XLA Ops:
  1.8 1.3 %fusion.20 = bf16[2,4,64,256]{3,2,1,0:T(8,128)(2,1)S(1)} fusion(bf16[2,4,64,256]{3,2,1,0:T(8,128)(2,1)} %param.4, f32[2,4,64]{2,1,0:T(4,128)S(1)} %fusion.113), kind=kLoop, calls=%fused_computation.54 | loop fusion | flops 917504 | bytes 526336 | tf_op jit(solution)/shard_map/convert_element_type | solution.py:89
  3.1 3.5 %collective-permute-start = (bf16[2,1,64,256]{3,2,1,0:T(8,128)(2,1)S(1)}, bf16[2,1,64,256]{3,2,1,0:T(8,128)(2,1)S(1)}, u32[]{:S(2)}, u32[]{:S(2)}) collective-permute-start(bf16[2,1,64,256]{3,2,1,0:T(8,128)(2,1)S(1)} %get-tuple-element.12), channel_id=1, source_target_pairs={{0,1},{1,2},{2,3},{3,4},{4,5},{5,6},{6,7},{7,8},{8,9},{9,10},{10,1... | collective-permute-start | bytes 196616 | tf_op jit(solution)/shard_map/ppermute | solution.py:19
  6.6 1.3 %collective-permute-start.1 = (bf16[2,1,64,256]{3,2,1,0:T(8,128)(2,1)S(1)}, bf16[2,1,64,256]{3,2,1,0:T(8,128)(2,1)S(1)}, u32[]{:S(2)}, u32[]{:S(2)}) collective-permute-start(bf16[2,1,64,256]{3,2,1,0:T(8,128)(2,1)S(1)} %get-tuple-element.13), channel_id=1, source_target_pairs={{1,0},{2,1},{3,2},{4,3},{5,4},{6,5},{7,6},{8,7},{9,8},{10,9},{11,1... | collective-permute-start | bytes 196616 | tf_op jit(solution)/shard_map/ppermute | solution.py:21
  7.9 1.9 %collective-permute-start.3 = (bf16[2,4,64,256]{3,2,1,0:T(8,128)(2,1)}, bf16[2,4,64,256]{3,2,1,0:T(8,128)(2,1)}, u32[]{:S(2)}, u32[]{:S(2)}) collective-permute-start(bf16[2,4,64,256]{3,2,1,0:T(8,128)(2,1)} %param.5), channel_id=1, source_target_pairs={{96,0},{192,96},{288,192},{384,288},{480,384},{576,480},{672,576},... | collective-permute-start | bytes 786440 | tf_op jit(solution)/shard_map/ppermute | solution.py:31
  9.8 2.0 %fusion.85 = f32[2,4,64,256]{3,2,1,0:T(8,128)} fusion(bf16[2,4,64,256]{3,2,1,0:T(8,128)(2,1)S(1)} %copy-done.4, bf16[3,256,256]{2,1,0:T(8,128)(2,1)} %param.7), kind=kOutput, calls=%fused_computation.129 | convolution fusion | flops 67108864 | bytes 917504 | tf_op jit(solution)/shard_map/dot_general | solution.py:41
  15.0 2.3 %collective-permute-start.2 = (bf16[2,4,64,256]{3,2,1,0:T(8,128)(2,1)S(1)}, bf16[2,4,64,256]{3,2,1,0:T(8,128)(2,1)S(1)}, u32[]{:S(2)}, u32[]{:S(2)}) collective-permute-start(bf16[2,4,64,256]{3,2,1,0:T(8,128)(2,1)S(1)} %fusion.11), channel_id=1, source_target_pairs={{0,96},{96,192},{192,288},{288,384},{384,480},{480,576},{576,672},... | collective-permute-start | bytes 786440 | tf_op jit(solution)/shard_map/ppermute | solution.py:31
  18.2 1.2 %fusion.79 = f32[2,4,64,256]{3,2,1,0:T(8,128)S(1)} fusion(bf16[2,4,64,256]{3,2,1,0:T(8,128)(2,1)} %collective-permute-done.3, bf16[3,256,256]{2,1,0:T(8,128)(2,1)S(1)} %copy-done.9), kind=kOutput, calls=%fused_computation.123 | convolution fusion | flops 67108864 | bytes 917504 | tf_op jit(solution)/shard_map/dot_general | solution.py:41
  20.6 3.6 %fusion.36 = f32[3,3,256,256]{3,2,1,0:T(8,128)} fusion(bf16[2,6,64,256]{3,2,1,0:T(8,128)(2,1)S(1)} %pad_maximum_fusion.2, bf16[2,4,64,256]{3,2,1,0:T(8,128)(2,1)S(1)} %fusion.12), kind=kOutput, calls=%fused_computation.72 | convolution fusion | flops 597688320 | bytes 3014656 | tf_op jit(solution)/shard_map/conv_general_dilated | solution.py:122
  24.2 2.6 %concatenate.37 = f32[4,2,96,768]{3,2,1,0:T(8,128)S(1)} reshape(f32[3,3,256,256]{3,2,1,0:T(8,128)} %fusion.36) | data formatting | bytes 4718592 | tf_op jit(solution)/shard_map/concatenate | solution.py:137
  27.9 1.4 %fusion.1 = f32[4,96,1024]{2,1,0:T(8,128)} fusion(s32[]{:T(128)S(6)} %select_n.46, f32[4,2,96,768]{3,2,1,0:T(8,128)S(1)} %concatenate.37, f32[4,2,96,256]{3,2,1,0:T(8,128)S(1)} %bitcast.155), kind=kLoop, calls=%fused_computation.5 | loop fusion | flops 393216 | bytes 4718596 | tf_op jit(solution)/shard_map/jit(dynamic_index_in_dim)/squeeze | solution.py:64
  29.3 1.9 %collective-permute-start.4 = (f32[4,96,1024]{2,1,0:T(8,128)}, f32[4,96,1024]{2,1,0:T(8,128)}, u32[]{:S(2)}, u32[]{:S(2)}) collective-permute-start(f32[4,96,1024]{2,1,0:T(8,128)} %fusion.1), channel_id=1, source_target_pairs={{0,96},{96,0},{192,288},{288,192},{384,480},{480,384},{576,672},{6... | collective-permute-start | bytes 4718600 | tf_op jit(solution)/shard_map/ppermute | solution.py:69
  31.3 3.7 %collective-permute-done.4 = f32[4,96,1024]{2,1,0:T(8,128)} collective-permute-done((f32[4,96,1024]{2,1,0:T(8,128)}, f32[4,96,1024]{2,1,0:T(8,128)}, u32[]{:S(2)}, u32[]{:S(2)}) %collective-permute-start.4) | collective-permute-done | bytes 1572896 | tf_op jit(solution)/shard_map/ppermute | solution.py:69
  35.0 1.6 %fusion.4 = f32[4,96,1024]{2,1,0:T(8,128)S(1)} fusion(f32[4,96,1024]{2,1,0:T(8,128)} %collective-permute-done.4, s32[]{:T(128)S(6)} %select_n.45, f32[4,2,96,768]{3,2,1,0:T(8,128)S(1)} %concatenate.37, f32[4,2,96,256]{3,2,1,0:T(8,128)S(1)} %bitcast.156), kind=kLoop, calls=%fused_computation.8 | loop fusion | flops 786432 | bytes 6291460 | tf_op jit(solution)/shard_map/add | solution.py:70
  37.8 3.5 %collective-permute-start.5 = (bf16[2,96,1024]{2,1,0:T(8,128)(2,1)S(1)}, bf16[2,96,1024]{2,1,0:T(8,128)(2,1)S(1)}, u32[]{:S(2)}, u32[]{:S(2)}) collective-permute-start(bf16[2,96,1024]{2,1,0:T(8,128)(2,1)S(1)} %fusion.35), channel_id=1, source_target_pairs={{0,192},{96,288},{192,0},{288,96},{384,576},{480,672},{576,384},{6... | collective-permute-start | bytes 1179656 | tf_op jit(solution)/shard_map/ppermute | solution.py:67
  41.3 1.2 %fusion.87 = f32[2,4,64,256]{3,2,1,0:T(8,128)S(1)} fusion(bf16[2,4,64,256]{3,2,1,0:T(8,128)(2,1)} %copy-done.6, bf16[3,256,256]{2,1,0:T(8,128)(2,1)} %param.7), kind=kOutput, calls=%fused_computation.131 | convolution fusion | flops 67108864 | bytes 917504 | tf_op jit(solution)/shard_map/dot_general | solution.py:41
  42.5 8.3 %collective-permute-done.5 = bf16[2,96,1024]{2,1,0:T(8,128)(2,1)S(1)} collective-permute-done((bf16[2,96,1024]{2,1,0:T(8,128)(2,1)S(1)}, bf16[2,96,1024]{2,1,0:T(8,128)(2,1)S(1)}, u32[]{:S(2)}, u32[]{:S(2)}) %collective-permute-start.5) | collective-permute-done | bytes 393248 | tf_op jit(solution)/shard_map/ppermute | solution.py:67
  50.9 1.2 %bitcast_add_fusion = f32[2,96,1024]{2,1,0:T(8,128)S(1)} fusion(bf16[2,96,1024]{2,1,0:T(8,128)(2,1)S(1)} %collective-permute-done.5, f32[2,2,96,1024]{3,2,1,0:T(8,128)} %bitcast.158, s32[]{:T(128)S(6)} %select_n.49), kind=kLoop, calls=%fused_computation.44 | loop fusion | flops 393216 | bytes 1966084 | tf_op jit(solution)/shard_map/add | solution.py:70
  52.2 8.4 %collective-permute-start.6 = (bf16[1,96,1024]{2,1,0:T(8,128)(2,1)S(1)}, bf16[1,96,1024]{2,1,0:T(8,128)(2,1)S(1)}, u32[]{:S(2)}, u32[]{:S(2)}) collective-permute-start(bf16[1,96,1024]{2,1,0:T(8,128)(2,1)S(1)} %dynamic-slice_convert_fusion.1), channel_id=1, source_target_pairs={{0,384},{96,480},{192,576},{288,672},{384,0},{480,96},{576,192},{6... | collective-permute-start | bytes 589832 | tf_op jit(solution)/shard_map/ppermute | solution.py:67
  60.8 4.4 %collective-permute-done.6 = bf16[1,96,1024]{2,1,0:T(8,128)(2,1)S(1)} collective-permute-done((bf16[1,96,1024]{2,1,0:T(8,128)(2,1)S(1)}, bf16[1,96,1024]{2,1,0:T(8,128)(2,1)S(1)}, u32[]{:S(2)}, u32[]{:S(2)}) %collective-permute-start.6) | collective-permute-done | bytes 196640 | tf_op jit(solution)/shard_map/ppermute | solution.py:67
  65.3 1.3 %collective-permute-start.8 = (bf16[2,1,64,256]{3,2,1,0:T(8,128)(2,1)S(1)}, bf16[2,1,64,256]{3,2,1,0:T(8,128)(2,1)S(1)}, u32[]{:S(2)}, u32[]{:S(2)}) collective-permute-start(bf16[2,1,64,256]{3,2,1,0:T(8,128)(2,1)S(1)} %get-tuple-element.11), channel_id=1, source_target_pairs={{1,0},{2,1},{3,2},{4,3},{5,4},{6,5},{7,6},{8,7},{9,8},{10,9},{11,1... | collective-permute-start | bytes 196616 | tf_op jit(solution)/shard_map/ppermute | solution.py:21
  68.8 22.4 %all-to-all-start = ((f32[96,1,1024]{2,1,0:T(1,128)}), f32[96,1,1024]{2,1,0:T(1,128)S(1)}, u32[]{:S(2)}, u32[]{:S(2)}) async-start(f32[96,1,1024]{2,1,0:T(1,128)} %copy.14), calls=%async_computation | async-start | bytes 786432 | tf_op jit(solution)/shard_map/all_to_all | solution.py:154
  91.1 3.3 %collective-permute-start.7 = (bf16[2,1,64,256]{3,2,1,0:T(8,128)(2,1)S(1)}, bf16[2,1,64,256]{3,2,1,0:T(8,128)(2,1)S(1)}, u32[]{:S(2)}, u32[]{:S(2)}) collective-permute-start(bf16[2,1,64,256]{3,2,1,0:T(8,128)(2,1)S(1)} %get-tuple-element.10), channel_id=1, source_target_pairs={{0,1},{1,2},{2,3},{3,4},{4,5},{5,6},{6,7},{7,8},{8,9},{9,10},{10,1... | collective-permute-start | bytes 196616 | tf_op jit(solution)/shard_map/ppermute | solution.py:19
  94.7 2.1 %collective-permute-done.7 = bf16[2,1,64,256]{3,2,1,0:T(8,128)(2,1)S(1)} collective-permute-done((bf16[2,1,64,256]{3,2,1,0:T(8,128)(2,1)S(1)}, bf16[2,1,64,256]{3,2,1,0:T(8,128)(2,1)S(1)}, u32[]{:S(2)}, u32[]{:S(2)}) %collective-permute-start.7) | collective-permute-done | bytes 65568 | tf_op jit(solution)/shard_map/ppermute | solution.py:19
  100.7 12.9 %all-to-all-done = f32[96,1,1024]{2,1,0:T(1,128)S(1)} async-done(((f32[96,1,1024]{2,1,0:T(1,128)}), f32[96,1,1024]{2,1,0:T(1,128)S(1)}, u32[]{:S(2)}, u32[]{:S(2)}) %all-to-all-start) | async-done | bytes 393248 | tf_op jit(solution)/shard_map/all_to_all | solution.py:154
  (75 shorter events, 16.1 us)
Async XLA Ops:
  0.6 9.2 %copy-start.4 = (bf16[2,4,64,256]{3,2,1,0:T(8,128)(2,1)S(1)}, bf16[2,4,64,256]{3,2,1,0:T(8,128)(2,1)}, u32[]{:S(2)}) copy-start(bf16[2,4,64,256]{3,2,1,0:T(8,128)(2,1)} %param.5) | copy-start | bytes 786436
  1.8 11.0 %copy-start.1 = (bf16[3,3,256,256]{3,2,1,0:T(8,128)(2,1)S(1)}, bf16[3,3,256,256]{3,2,1,0:T(8,128)(2,1)}, u32[]{:S(2)}) copy-start(bf16[3,3,256,256]{3,2,1,0:T(8,128)(2,1)} %param.6) | copy-start | bytes 3538948
  3.1 8.7 %collective-permute-start = (bf16[2,1,64,256]{3,2,1,0:T(8,128)(2,1)S(1)}, bf16[2,1,64,256]{3,2,1,0:T(8,128)(2,1)S(1)}, u32[]{:S(2)}, u32[]{:S(2)}) collective-permute-start(bf16[2,1,64,256]{3,2,1,0:T(8,128)(2,1)S(1)} %get-tuple-element.12), channel_id=1, source_target_pairs={{0,1},{1,2},{2,3},{3,4},{4,5},{5,6},{6,7},{7,8},{8,9},{9,10},{10,1... | collective-permute-start | bytes 196616 | tf_op jit(solution)/shard_map/ppermute | solution.py:19
  6.6 6.2 %collective-permute-start.1 = (bf16[2,1,64,256]{3,2,1,0:T(8,128)(2,1)S(1)}, bf16[2,1,64,256]{3,2,1,0:T(8,128)(2,1)S(1)}, u32[]{:S(2)}, u32[]{:S(2)}) collective-permute-start(bf16[2,1,64,256]{3,2,1,0:T(8,128)(2,1)S(1)} %get-tuple-element.13), channel_id=1, source_target_pairs={{1,0},{2,1},{3,2},{4,3},{5,4},{6,5},{7,6},{8,7},{9,8},{10,9},{11,1... | collective-permute-start | bytes 196616 | tf_op jit(solution)/shard_map/ppermute | solution.py:21
  7.9 10.4 %collective-permute-start.3 = (bf16[2,4,64,256]{3,2,1,0:T(8,128)(2,1)}, bf16[2,4,64,256]{3,2,1,0:T(8,128)(2,1)}, u32[]{:S(2)}, u32[]{:S(2)}) collective-permute-start(bf16[2,4,64,256]{3,2,1,0:T(8,128)(2,1)} %param.5), channel_id=1, source_target_pairs={{96,0},{192,96},{288,192},{384,288},{480,384},{576,480},{672,576},... | collective-permute-start | bytes 786440 | tf_op jit(solution)/shard_map/ppermute | solution.py:31
  14.7 3.5 %copy-start.9 = (bf16[3,256,256]{2,1,0:T(8,128)(2,1)S(1)}, bf16[3,256,256]{2,1,0:T(8,128)(2,1)}, u32[]{:S(2)}) copy-start(bf16[3,256,256]{2,1,0:T(8,128)(2,1)} %param.7) | copy-start | bytes 1179652
  15.0 12.1 %copy-start.6 = (bf16[2,4,64,256]{3,2,1,0:T(8,128)(2,1)}, bf16[2,4,64,256]{3,2,1,0:T(8,128)(2,1)S(1)}, u32[]{:S(2)}) copy-start(bf16[2,4,64,256]{3,2,1,0:T(8,128)(2,1)S(1)} %fusion.11) | copy-start | bytes 786436
  15.0 4.5 %copy-start.8 = (f32[2,4,64,256]{3,2,1,0:T(8,128)S(1)}, f32[2,4,64,256]{3,2,1,0:T(8,128)}, u32[]{:S(2)}) copy-start(f32[2,4,64,256]{3,2,1,0:T(8,128)} %fusion.85) | copy-start | bytes 1572868
  15.0 11.8 %collective-permute-start.2 = (bf16[2,4,64,256]{3,2,1,0:T(8,128)(2,1)S(1)}, bf16[2,4,64,256]{3,2,1,0:T(8,128)(2,1)S(1)}, u32[]{:S(2)}, u32[]{:S(2)}) collective-permute-start(bf16[2,4,64,256]{3,2,1,0:T(8,128)(2,1)S(1)} %fusion.11), channel_id=1, source_target_pairs={{0,96},{96,192},{192,288},{288,384},{384,480},{480,576},{576,672},... | collective-permute-start | bytes 786440 | tf_op jit(solution)/shard_map/ppermute | solution.py:31
  26.8 1.0 copy-start.13
  26.8 0.7 copy-start.11
  29.3 5.6 %collective-permute-start.4 = (f32[4,96,1024]{2,1,0:T(8,128)}, f32[4,96,1024]{2,1,0:T(8,128)}, u32[]{:S(2)}, u32[]{:S(2)}) collective-permute-start(f32[4,96,1024]{2,1,0:T(8,128)} %fusion.1), channel_id=1, source_target_pairs={{0,96},{96,0},{192,288},{288,192},{384,480},{480,384},{576,672},{6... | collective-permute-start | bytes 4718600 | tf_op jit(solution)/shard_map/ppermute | solution.py:69
  36.6 1.2 %copy-start = (f32[4,96,1024]{2,1,0:T(8,128)}, f32[4,96,1024]{2,1,0:T(8,128)S(1)}, u32[]{:S(2)}) copy-start(f32[4,96,1024]{2,1,0:T(8,128)S(1)} %fusion.4) | copy-start | bytes 4718596
  37.8 13.1 %collective-permute-start.5 = (bf16[2,96,1024]{2,1,0:T(8,128)(2,1)S(1)}, bf16[2,96,1024]{2,1,0:T(8,128)(2,1)S(1)}, u32[]{:S(2)}, u32[]{:S(2)}) collective-permute-start(bf16[2,96,1024]{2,1,0:T(8,128)(2,1)S(1)} %fusion.35), channel_id=1, source_target_pairs={{0,192},{96,288},{192,0},{288,96},{384,576},{480,672},{576,384},{6... | collective-permute-start | bytes 1179656 | tf_op jit(solution)/shard_map/ppermute | solution.py:67
  42.5 18.1 %copy-start.10 = (bf16[3,256,256]{2,1,0:T(8,128)(2,1)S(1)}, bf16[3,256,256]{2,1,0:T(8,128)(2,1)}, u32[]{:S(2)}) copy-start(bf16[3,256,256]{2,1,0:T(8,128)(2,1)} %param.7) | copy-start | bytes 1179652
  42.5 18.0 %copy-start.12 = (bf16[2,4,64,256]{3,2,1,0:T(8,128)(2,1)S(1)}, bf16[2,4,64,256]{3,2,1,0:T(8,128)(2,1)}, u32[]{:S(2)}) copy-start(bf16[2,4,64,256]{3,2,1,0:T(8,128)(2,1)} %copy-done.11) | copy-start | bytes 786436
  52.2 14.4 %copy-start.3 = (bf16[2,4,64,256]{3,2,1,0:T(8,128)(2,1)S(1)}, bf16[2,4,64,256]{3,2,1,0:T(8,128)(2,1)}, u32[]{:S(2)}) copy-start(bf16[2,4,64,256]{3,2,1,0:T(8,128)(2,1)} %param.4) | copy-start | bytes 786436
  52.2 14.4 %copy-start.7 = (bf16[2,4,64,256]{3,2,1,0:T(8,128)(2,1)S(1)}, bf16[2,4,64,256]{3,2,1,0:T(8,128)(2,1)}, u32[]{:S(2)}) copy-start(bf16[2,4,64,256]{3,2,1,0:T(8,128)(2,1)} %copy-done.6) | copy-start | bytes 786436
  52.2 13.0 %collective-permute-start.6 = (bf16[1,96,1024]{2,1,0:T(8,128)(2,1)S(1)}, bf16[1,96,1024]{2,1,0:T(8,128)(2,1)S(1)}, u32[]{:S(2)}, u32[]{:S(2)}) collective-permute-start(bf16[1,96,1024]{2,1,0:T(8,128)(2,1)S(1)} %dynamic-slice_convert_fusion.1), channel_id=1, source_target_pairs={{0,384},{96,480},{192,576},{288,672},{384,0},{480,96},{576,192},{6... | collective-permute-start | bytes 589832 | tf_op jit(solution)/shard_map/ppermute | solution.py:67
  65.3 29.1 %collective-permute-start.8 = (bf16[2,1,64,256]{3,2,1,0:T(8,128)(2,1)S(1)}, bf16[2,1,64,256]{3,2,1,0:T(8,128)(2,1)S(1)}, u32[]{:S(2)}, u32[]{:S(2)}) collective-permute-start(bf16[2,1,64,256]{3,2,1,0:T(8,128)(2,1)S(1)} %get-tuple-element.11), channel_id=1, source_target_pairs={{1,0},{2,1},{3,2},{4,3},{5,4},{6,5},{7,6},{8,7},{9,8},{10,9},{11,1... | collective-permute-start | bytes 196616 | tf_op jit(solution)/shard_map/ppermute | solution.py:21
  67.6 26.8 %copy-start.2 = (bf16[3,3,256,256]{3,2,1,0:T(8,128)(2,1)S(1)}, bf16[3,3,256,256]{3,2,1,0:T(8,128)(2,1)}, u32[]{:S(2)}) copy-start(bf16[3,3,256,256]{3,2,1,0:T(8,128)(2,1)} %param.6) | copy-start | bytes 3538948
  68.8 44.8 %all-to-all-start = ((f32[96,1,1024]{2,1,0:T(1,128)}), f32[96,1,1024]{2,1,0:T(1,128)S(1)}, u32[]{:S(2)}, u32[]{:S(2)}) async-start(f32[96,1,1024]{2,1,0:T(1,128)} %copy.14), calls=%async_computation | async-start | bytes 786432 | tf_op jit(solution)/shard_map/all_to_all | solution.py:154
  91.1 5.6 %collective-permute-start.7 = (bf16[2,1,64,256]{3,2,1,0:T(8,128)(2,1)S(1)}, bf16[2,1,64,256]{3,2,1,0:T(8,128)(2,1)S(1)}, u32[]{:S(2)}, u32[]{:S(2)}) collective-permute-start(bf16[2,1,64,256]{3,2,1,0:T(8,128)(2,1)S(1)} %get-tuple-element.10), channel_id=1, source_target_pairs={{0,1},{1,2},{2,3},{3,4},{4,5},{5,6},{6,7},{7,8},{8,9},{9,10},{10,1... | collective-permute-start | bytes 196616 | tf_op jit(solution)/shard_map/ppermute | solution.py:19
  98.8 1.0 copy-start.5
  (1 other events, 0.6 us)

commit v10 on v9

--- a/solution.py
+++ b/solution.py
@@ -89,13 +89,14 @@
     activated = activate(clip_wide).astype(jnp.bfloat16)
     act_ext = extended(activated, (("height", 1),), 1)
     padded = jnp.pad(act_ext, ((0, 0), (0, 0), (1, 1), (0, 0)))
-    spatial = jnp.zeros(clip.shape, jnp.float32)
-    for tap_row in range(3):
-        for tap_col in range(3):
-            spatial = spatial + flat_dot(
-                padded[:, tap_row : tap_row + row_count, tap_col : tap_col + col_count],
-                spatial_weight[tap_row, tap_col],
-            )
+    spatial = lax.conv_general_dilated(
+        padded,
+        spatial_weight,
+        window_strides=(1, 1),
+        padding="VALID",
+        dimension_numbers=("NHWC", "HWIO", "NHWC"),
+        preferred_element_type=jnp.float32,
+    )
     middle = spatial.astype(jnp.bfloat16)
     earlier = shifted(middle, "tm", 1)
     history = jnp.concatenate([earlier, middle], axis=0)
@@ -113,12 +114,14 @@
             future[time_lag : time_lag + frame_count], temporal_weight[time_lag].T
         )
     grad_mid = grad_wide.astype(jnp.bfloat16)
-    grad_temporal = jnp.stack(
-        [
-            outer_sum(history[2 - time_lag : 2 - time_lag + frame_count], cotangent)
-            for time_lag in range(3)
-        ]
-    )
+    grad_temporal = lax.conv_general_dilated(
+        history.reshape(history.shape[0], -1, channels),
+        cotangent.reshape(frame_count, -1, channels),
+        window_strides=(1,),
+        padding="VALID",
+        dimension_numbers=("WCN", "WIO", "WNC"),
+        preferred_element_type=jnp.float32,
+    )[::-1]
     grad_spatial = lax.conv_general_dilated(
         padded,
         grad_mid,

time: 116 us -> 116 us (level)
  matrix products: 16.5 us -> 12.4 us
  local copies, waits for them, and re-layouts: 6.53 us -> 9.33 us
    dot_general x24 -> x15, matrix products: 11.4 us -> 6.66 us  [flat_dot(): jnp.dot(left.reshape(-1, left.shape[-1]), weight, preferred_element_type=...]
    conv_general_dilated x0 -> x2, matrix products: none -> 2.14 us  [the longest x1 1.29 us: shards(): lax.conv_general_dilated(history.reshape(history.shape[0], -1, channels),...]
    dot_general x3 -> x0, matrix products: 1.49 us -> none  [outer_sum(): lax.dot_general(left.reshape(-1, channels), right.reshape(-1, channels),...]
    rev x0 -> x1, local copies, waits for them, and re-layouts: none -> 1.18 us  [shards(): lax.conv_general_dilated(history.reshape(history.shape[0], -1, channels),...]
    unnamed x30 -> x32, local copies, waits for them, and re-layouts: 2.13 us -> 3.12 us
  transfers between devices with their start and end apart: 10 -> 10, of which waited for: 6 -> 6; matrix products, arithmetic and copies ran while one was open for 18% -> 15% of each run, Pallas kernels for 0% -> 0%
where the time goes in v10:
time: 116 us; the launch traced here: 114 us
  starting transfers between devices  49.5 us (43%)
  waiting for transfers between devices  33.2 us (29%)
  matrix products  12.4 us (11%)
  local copies, waits for them, and re-layouts  9.33 us (8%)
  other arithmetic  8.49 us (7%)
  between operations  1.28 us (1%)
    all_to_all x1, starting transfers between devices, shards(): packed = lax.all_to_all(packed, 'height', 0, 0, tiled=True)  22.5 us
    all_to_all x1, waiting for transfers between devices, shards(): packed = lax.all_to_all(packed, 'height', 0, 0, tiled=True)  12.9 us
    ppermute x2, waiting for transfers between devices, halving_scatter(): lax.ppermute(send.astype(jnp.bfloat16), axis, route).astype(block.dtype)  12.8 us
    ppermute x2, starting transfers between devices, halving_scatter(): lax.ppermute(send.astype(jnp.bfloat16), axis, route).astype(block.dtype)  11.9 us
    ppermute x2, starting transfers between devices, extended(): lax.ppermute(tail, axis, [(i, (i + 1) % count) for i in range(ends)])  6.74 us
    dot_general x15, matrix products, flat_dot(): jnp.dot(left.reshape(-1, left.shape[-1]), weight, preferred_element_type=...  6.66 us
    ppermute x2, starting transfers between devices, shifted(): return lax.ppermute(block, axis, route)  3.84 us
    ppermute x1, waiting for transfers between devices, halving_scatter(): sent = lax.ppermute(send, axis, route)  3.67 us
  transfers between devices with their start and end apart: 10, of which 6 were waited for; matrix products, arithmetic and copies ran while one was open for 15% of the time, Pallas kernels for 0%

profile of v10, /device:TPU:6, one launch (start us, length us, event | category | flops | bytes accessed | tf_op | source)
XLA Modules:
  0.0 114.2 jit_solution(14855785326996305500)
XLA Ops:
  3.0 3.5 %collective-permute-start = (bf16[2,1,64,256]{3,2,1,0:T(8,128)(2,1)S(1)}, bf16[2,1,64,256]{3,2,1,0:T(8,128)(2,1)S(1)}, u32[]{:S(2)}, u32[]{:S(2)}) collective-permute-start(bf16[2,1,64,256]{3,2,1,0:T(8,128)(2,1)S(1)} %get-tuple-element.14), channel_id=1, source_target_pairs={{0,1},{1,2},{2,3},{3,4},{4,5},{5,6},{6,7},{7,8},{8,9},{9,10},{10,1... | collective-permute-start | bytes 196616 | tf_op jit(solution)/shard_map/ppermute | solution.py:19
  6.5 1.3 %collective-permute-start.1 = (bf16[2,1,64,256]{3,2,1,0:T(8,128)(2,1)S(1)}, bf16[2,1,64,256]{3,2,1,0:T(8,128)(2,1)S(1)}, u32[]{:S(2)}, u32[]{:S(2)}) collective-permute-start(bf16[2,1,64,256]{3,2,1,0:T(8,128)(2,1)S(1)} %get-tuple-element.15), channel_id=1, source_target_pairs={{1,0},{2,1},{3,2},{4,3},{5,4},{6,5},{7,6},{8,7},{9,8},{10,9},{11,1... | collective-permute-start | bytes 196616 | tf_op jit(solution)/shard_map/ppermute | solution.py:21
  7.8 1.9 %collective-permute-start.3 = (bf16[2,4,64,256]{3,2,1,0:T(8,128)(2,1)}, bf16[2,4,64,256]{3,2,1,0:T(8,128)(2,1)S(1)}, u32[]{:S(2)}, u32[]{:S(2)}) collective-permute-start(bf16[2,4,64,256]{3,2,1,0:T(8,128)(2,1)} %param.5), channel_id=1, source_target_pairs={{96,0},{192,96},{288,192},{384,288},{480,384},{576,480},{672,576},... | collective-permute-start | bytes 786440 | tf_op jit(solution)/shard_map/ppermute | solution.py:31
  10.9 1.7 %collective-permute-done.1 = bf16[2,1,64,256]{3,2,1,0:T(8,128)(2,1)S(1)} collective-permute-done((bf16[2,1,64,256]{3,2,1,0:T(8,128)(2,1)S(1)}, bf16[2,1,64,256]{3,2,1,0:T(8,128)(2,1)S(1)}, u32[]{:S(2)}, u32[]{:S(2)}) %collective-permute-start.1) | collective-permute-done | bytes 65568 | tf_op jit(solution)/shard_map/ppermute | solution.py:21
  15.6 1.9 %collective-permute-start.2 = (bf16[2,4,64,256]{3,2,1,0:T(8,128)(2,1)S(1)}, bf16[2,4,64,256]{3,2,1,0:T(8,128)(2,1)S(1)}, u32[]{:S(2)}, u32[]{:S(2)}) collective-permute-start(bf16[2,4,64,256]{3,2,1,0:T(8,128)(2,1)S(1)} %bitcast.133), channel_id=1, source_target_pairs={{0,96},{96,192},{192,288},{288,384},{384,480},{480,576},{576,672},... | collective-permute-start | bytes 786440 | tf_op jit(solution)/shard_map/ppermute | solution.py:31
  18.1 3.6 %fusion.38 = f32[3,3,256,256]{3,2,1,0:T(8,128)} fusion(bf16[2,6,64,256]{3,2,1,0:T(8,128)(2,1)S(1)} %get-tuple-element.10, bf16[2,4,64,256]{3,2,1,0:T(8,128)(2,1)S(1)} %fusion.11), kind=kOutput, calls=%fused_computation.65 | convolution fusion | flops 597688320 | bytes 3014656 | tf_op jit(solution)/shard_map/conv_general_dilated | solution.py:125
  21.7 2.6 %concatenate.29 = f32[4,2,96,768]{3,2,1,0:T(8,128)S(1)} reshape(f32[3,3,256,256]{3,2,1,0:T(8,128)} %fusion.38) | data formatting | bytes 4718592 | tf_op jit(solution)/shard_map/concatenate | solution.py:140
  25.0 1.3 %fusion.96 = f32[3,256,256]{2,1,0:T(8,128)} fusion(bf16[4,256,256]{2,1,0:T(8,128)(2,1)S(1)} %bitcast.138, bf16[2,256,256]{2,1,0:T(8,128)(2,1)S(1)} %bitcast.132), kind=kOutput, calls=%fused_computation.129 | convolution fusion | flops 201326592 | bytes 1572864 | tf_op jit(solution)/shard_map/conv_general_dilated | solution.py:117
  26.3 1.2 %rev.3 = f32[3,256,256]{2,1,0:T(8,128)S(1)} reverse(f32[3,256,256]{2,1,0:T(8,128)} %fusion.96), dimensions={0} | reverse | bytes 1572864 | tf_op jit(solution)/shard_map/rev | solution.py:117
  27.5 1.4 %fusion.1 = f32[4,96,1024]{2,1,0:T(8,128)} fusion(s32[]{:T(128)S(6)} %select_n.46, f32[4,2,96,768]{3,2,1,0:T(8,128)S(1)} %concatenate.29, f32[4,2,96,256]{3,2,1,0:T(8,128)S(1)} %bitcast.128), kind=kLoop, calls=%fused_computation.6 | loop fusion | flops 393216 | bytes 4718596 | tf_op jit(solution)/shard_map/jit(dynamic_index_in_dim)/squeeze | solution.py:64
  28.9 1.9 %collective-permute-start.4 = (f32[4,96,1024]{2,1,0:T(8,128)}, f32[4,96,1024]{2,1,0:T(8,128)}, u32[]{:S(2)}, u32[]{:S(2)}) collective-permute-start(f32[4,96,1024]{2,1,0:T(8,128)} %fusion.1), channel_id=1, source_target_pairs={{0,96},{96,0},{192,288},{288,192},{384,480},{480,384},{576,672},{6... | collective-permute-start | bytes 4718600 | tf_op jit(solution)/shard_map/ppermute | solution.py:69
  30.8 3.7 %collective-permute-done.4 = f32[4,96,1024]{2,1,0:T(8,128)} collective-permute-done((f32[4,96,1024]{2,1,0:T(8,128)}, f32[4,96,1024]{2,1,0:T(8,128)}, u32[]{:S(2)}, u32[]{:S(2)}) %collective-permute-start.4) | collective-permute-done | bytes 1572896 | tf_op jit(solution)/shard_map/ppermute | solution.py:69
  34.5 1.6 %fusion.4 = f32[4,96,1024]{2,1,0:T(8,128)S(1)} fusion(f32[4,96,1024]{2,1,0:T(8,128)} %collective-permute-done.4, s32[]{:T(128)S(6)} %select_n.45, f32[4,2,96,768]{3,2,1,0:T(8,128)S(1)} %concatenate.29, f32[4,2,96,256]{3,2,1,0:T(8,128)S(1)} %bitcast.129), kind=kLoop, calls=%fused_computation.9 | loop fusion | flops 786432 | bytes 6291460 | tf_op jit(solution)/shard_map/add | solution.py:70
  37.3 3.7 %collective-permute-start.5 = (bf16[2,96,1024]{2,1,0:T(8,128)(2,1)S(1)}, bf16[2,96,1024]{2,1,0:T(8,128)(2,1)S(1)}, u32[]{:S(2)}, u32[]{:S(2)}) collective-permute-start(bf16[2,96,1024]{2,1,0:T(8,128)(2,1)S(1)} %fusion.37), channel_id=1, source_target_pairs={{0,192},{96,288},{192,0},{288,96},{384,576},{480,672},{576,384},{6... | collective-permute-start | bytes 1179656 | tf_op jit(solution)/shard_map/ppermute | solution.py:67
  41.1 1.2 %fusion.72 = f32[2,4,64,256]{3,2,1,0:T(8,128)S(1)} fusion(bf16[3,256,256]{2,1,0:T(8,128)(2,1)} %param.7, bf16[4,2,64,256]{3,0,2,1:T(4,128)(2,1)} %copy-done.6), kind=kOutput, calls=%fused_computation.102 | convolution fusion | flops 67108864 | bytes 917504 | tf_op jit(solution)/shard_map/dot_general | solution.py:41
  42.3 8.3 %collective-permute-done.5 = bf16[2,96,1024]{2,1,0:T(8,128)(2,1)S(1)} collective-permute-done((bf16[2,96,1024]{2,1,0:T(8,128)(2,1)S(1)}, bf16[2,96,1024]{2,1,0:T(8,128)(2,1)S(1)}, u32[]{:S(2)}, u32[]{:S(2)}) %collective-permute-start.5) | collective-permute-done | bytes 393248 | tf_op jit(solution)/shard_map/ppermute | solution.py:67
  50.6 1.2 %bitcast_add_fusion = f32[2,96,1024]{2,1,0:T(8,128)S(1)} fusion(bf16[2,96,1024]{2,1,0:T(8,128)(2,1)S(1)} %collective-permute-done.5, f32[2,2,96,1024]{3,2,1,0:T(8,128)} %bitcast.131, s32[]{:T(128)S(6)} %select_n.49), kind=kLoop, calls=%fused_computation.34 | loop fusion | flops 393216 | bytes 1966084 | tf_op jit(solution)/shard_map/add | solution.py:70
  51.9 8.2 %collective-permute-start.6 = (bf16[1,96,1024]{2,1,0:T(8,128)(2,1)S(1)}, bf16[1,96,1024]{2,1,0:T(8,128)(2,1)S(1)}, u32[]{:S(2)}, u32[]{:S(2)}) collective-permute-start(bf16[1,96,1024]{2,1,0:T(8,128)(2,1)S(1)} %dynamic-slice_convert_fusion.1), channel_id=1, source_target_pairs={{0,384},{96,480},{192,576},{288,672},{384,0},{480,96},{576,192},{6... | collective-permute-start | bytes 589832 | tf_op jit(solution)/shard_map/ppermute | solution.py:67
  60.4 4.4 %collective-permute-done.6 = bf16[1,96,1024]{2,1,0:T(8,128)(2,1)S(1)} collective-permute-done((bf16[1,96,1024]{2,1,0:T(8,128)(2,1)S(1)}, bf16[1,96,1024]{2,1,0:T(8,128)(2,1)S(1)}, u32[]{:S(2)}, u32[]{:S(2)}) %collective-permute-start.6) | collective-permute-done | bytes 196640 | tf_op jit(solution)/shard_map/ppermute | solution.py:67
  64.9 1.3 %collective-permute-start.8 = (bf16[2,1,64,256]{3,2,1,0:T(8,128)(2,1)S(1)}, bf16[2,1,64,256]{3,2,1,0:T(8,128)(2,1)S(1)}, u32[]{:S(2)}, u32[]{:S(2)}) collective-permute-start(bf16[2,1,64,256]{3,2,1,0:T(8,128)(2,1)S(1)} %get-tuple-element.13), channel_id=1, source_target_pairs={{1,0},{2,1},{3,2},{4,3},{5,4},{6,5},{7,6},{8,7},{9,8},{10,9},{11,1... | collective-permute-start | bytes 196616 | tf_op jit(solution)/shard_map/ppermute | solution.py:21
  68.3 22.5 %all-to-all-start = ((f32[96,1,1024]{2,1,0:T(1,128)}), f32[96,1,1024]{2,1,0:T(1,128)S(1)}, u32[]{:S(2)}, u32[]{:S(2)}) async-start(f32[96,1,1024]{2,1,0:T(1,128)} %copy.30), calls=%async_computation | async-start | bytes 786432 | tf_op jit(solution)/shard_map/all_to_all | solution.py:157
  90.9 3.3 %collective-permute-start.7 = (bf16[2,1,64,256]{3,2,1,0:T(8,128)(2,1)S(1)}, bf16[2,1,64,256]{3,2,1,0:T(8,128)(2,1)S(1)}, u32[]{:S(2)}, u32[]{:S(2)}) collective-permute-start(bf16[2,1,64,256]{3,2,1,0:T(8,128)(2,1)S(1)} %get-tuple-element.12), channel_id=1, source_target_pairs={{0,1},{1,2},{2,3},{3,4},{4,5},{5,6},{6,7},{7,8},{8,9},{9,10},{10,1... | collective-permute-start | bytes 196616 | tf_op jit(solution)/shard_map/ppermute | solution.py:19
  94.4 2.1 %collective-permute-done.7 = bf16[2,1,64,256]{3,2,1,0:T(8,128)(2,1)S(1)} collective-permute-done((bf16[2,1,64,256]{3,2,1,0:T(8,128)(2,1)S(1)}, bf16[2,1,64,256]{3,2,1,0:T(8,128)(2,1)S(1)}, u32[]{:S(2)}, u32[]{:S(2)}) %collective-permute-start.7) | collective-permute-done | bytes 65568 | tf_op jit(solution)/shard_map/ppermute | solution.py:19
  100.4 12.9 %all-to-all-done = f32[96,1,1024]{2,1,0:T(1,128)S(1)} async-done(((f32[96,1,1024]{2,1,0:T(1,128)}), f32[96,1,1024]{2,1,0:T(1,128)S(1)}, u32[]{:S(2)}, u32[]{:S(2)}) %all-to-all-start) | async-done | bytes 393248 | tf_op jit(solution)/shard_map/all_to_all | solution.py:157
  (73 shorter events, 16.1 us)
Async XLA Ops:
  0.6 9.1 %copy-start.2 = (bf16[2,4,64,256]{3,2,1,0:T(8,128)(2,1)S(1)}, bf16[2,4,64,256]{3,2,1,0:T(8,128)(2,1)}, u32[]{:S(2)}) copy-start(bf16[2,4,64,256]{3,2,1,0:T(8,128)(2,1)} %param.5) | copy-start | bytes 786436
  3.0 7.9 %collective-permute-start = (bf16[2,1,64,256]{3,2,1,0:T(8,128)(2,1)S(1)}, bf16[2,1,64,256]{3,2,1,0:T(8,128)(2,1)S(1)}, u32[]{:S(2)}, u32[]{:S(2)}) collective-permute-start(bf16[2,1,64,256]{3,2,1,0:T(8,128)(2,1)S(1)} %get-tuple-element.14), channel_id=1, source_target_pairs={{0,1},{1,2},{2,3},{3,4},{4,5},{5,6},{6,7},{7,8},{8,9},{9,10},{10,1... | collective-permute-start | bytes 196616 | tf_op jit(solution)/shard_map/ppermute | solution.py:19
  6.5 6.2 %collective-permute-start.1 = (bf16[2,1,64,256]{3,2,1,0:T(8,128)(2,1)S(1)}, bf16[2,1,64,256]{3,2,1,0:T(8,128)(2,1)S(1)}, u32[]{:S(2)}, u32[]{:S(2)}) collective-permute-start(bf16[2,1,64,256]{3,2,1,0:T(8,128)(2,1)S(1)} %get-tuple-element.15), channel_id=1, source_target_pairs={{1,0},{2,1},{3,2},{4,3},{5,4},{6,5},{7,6},{8,7},{9,8},{10,9},{11,1... | collective-permute-start | bytes 196616 | tf_op jit(solution)/shard_map/ppermute | solution.py:21
  7.8 9.7 %collective-permute-start.3 = (bf16[2,4,64,256]{3,2,1,0:T(8,128)(2,1)}, bf16[2,4,64,256]{3,2,1,0:T(8,128)(2,1)S(1)}, u32[]{:S(2)}, u32[]{:S(2)}) collective-permute-start(bf16[2,4,64,256]{3,2,1,0:T(8,128)(2,1)} %param.5), channel_id=1, source_target_pairs={{96,0},{192,96},{288,192},{384,288},{480,384},{576,480},{672,576},... | collective-permute-start | bytes 786440 | tf_op jit(solution)/shard_map/ppermute | solution.py:31
  13.1 1.3 %copy-start.11 = (bf16[3,3,256,256]{3,2,1,0:T(8,128)(2,1)S(1)}, bf16[3,3,256,256]{3,2,1,0:T(8,128)(2,1)}, u32[]{:S(2)}) copy-start(bf16[3,3,256,256]{3,2,1,0:T(8,128)(2,1)} %param.6) | copy-start | bytes 3538948
  13.1 1.3 %copy-start.14 = (pred[16,9]{0,1:T(8,128)(4,1)S(1)}, pred[16,9]{0,1:T(8,128)(4,1)}, u32[]{:S(2)}) copy-start(pred[16,9]{0,1:T(8,128)(4,1)} %constant.105) | copy-start | bytes 436
  15.3 2.3 %copy-start.9 = (bf16[3,256,256]{2,1,0:T(8,128)(2,1)S(1)}, bf16[3,256,256]{2,1,0:T(8,128)(2,1)}, u32[]{:S(2)}) copy-start(bf16[3,256,256]{2,1,0:T(8,128)(2,1)} %param.7) | copy-start | bytes 1179652
  15.5 2.0 %copy-start.6 = (bf16[4,2,64,256]{3,0,2,1:T(4,128)(2,1)}, bf16[4,2,64,256]{3,0,2,1:T(4,128)(2,1)S(1)}, u32[]{:S(2)}) copy-start(bf16[4,2,64,256]{3,0,2,1:T(4,128)(2,1)S(1)} %slice.126) | copy-start | bytes 786436
  15.6 8.7 %copy-start.7 = (bf16[4,2,64,256]{3,2,0,1:T(8,128)(2,1)}, bf16[4,2,64,256]{3,2,0,1:T(8,128)(2,1)S(1)}, u32[]{:S(2)}) copy-start(bf16[4,2,64,256]{3,2,0,1:T(8,128)(2,1)S(1)} %copy.55) | copy-start | bytes 786436
  15.6 8.7 %collective-permute-start.2 = (bf16[2,4,64,256]{3,2,1,0:T(8,128)(2,1)S(1)}, bf16[2,4,64,256]{3,2,1,0:T(8,128)(2,1)S(1)}, u32[]{:S(2)}, u32[]{:S(2)}) collective-permute-start(bf16[2,4,64,256]{3,2,1,0:T(8,128)(2,1)S(1)} %bitcast.133), channel_id=1, source_target_pairs={{0,96},{96,192},{192,288},{288,384},{384,480},{480,576},{576,672},... | collective-permute-start | bytes 786440 | tf_op jit(solution)/shard_map/ppermute | solution.py:31
  24.3 0.7 copy-start.4
  28.9 5.6 %collective-permute-start.4 = (f32[4,96,1024]{2,1,0:T(8,128)}, f32[4,96,1024]{2,1,0:T(8,128)}, u32[]{:S(2)}, u32[]{:S(2)}) collective-permute-start(f32[4,96,1024]{2,1,0:T(8,128)} %fusion.1), channel_id=1, source_target_pairs={{0,96},{96,0},{192,288},{288,192},{384,480},{480,384},{576,672},{6... | collective-permute-start | bytes 4718600 | tf_op jit(solution)/shard_map/ppermute | solution.py:69
  36.1 1.2 %copy-start = (f32[4,96,1024]{2,1,0:T(8,128)}, f32[4,96,1024]{2,1,0:T(8,128)S(1)}, u32[]{:S(2)}) copy-start(f32[4,96,1024]{2,1,0:T(8,128)S(1)} %fusion.4) | copy-start | bytes 4718596
  37.3 13.3 %collective-permute-start.5 = (bf16[2,96,1024]{2,1,0:T(8,128)(2,1)S(1)}, bf16[2,96,1024]{2,1,0:T(8,128)(2,1)S(1)}, u32[]{:S(2)}, u32[]{:S(2)}) collective-permute-start(bf16[2,96,1024]{2,1,0:T(8,128)(2,1)S(1)} %fusion.37), channel_id=1, source_target_pairs={{0,192},{96,288},{192,0},{288,96},{384,576},{480,672},{576,384},{6... | collective-permute-start | bytes 1179656 | tf_op jit(solution)/shard_map/ppermute | solution.py:67
  42.3 17.9 %copy-start.5 = (bf16[2,4,64,256]{3,2,1,0:T(8,128)(2,1)S(1)}, bf16[2,4,64,256]{3,2,1,0:T(8,128)(2,1)}, u32[]{:S(2)}) copy-start(bf16[2,4,64,256]{3,2,1,0:T(8,128)(2,1)} %copy-done.4) | copy-start | bytes 786436
  42.3 17.9 %copy-start.10 = (bf16[3,256,256]{2,1,0:T(8,128)(2,1)S(1)}, bf16[3,256,256]{2,1,0:T(8,128)(2,1)}, u32[]{:S(2)}) copy-start(bf16[3,256,256]{2,1,0:T(8,128)(2,1)} %param.7) | copy-start | bytes 1179652
  51.9 14.3 %copy-start.1 = (bf16[2,4,64,256]{3,2,1,0:T(8,128)(2,1)S(1)}, bf16[2,4,64,256]{3,2,1,0:T(8,128)(2,1)}, u32[]{:S(2)}) copy-start(bf16[2,4,64,256]{3,2,1,0:T(8,128)(2,1)} %param.4) | copy-start | bytes 786436
  51.9 14.3 %copy-start.8 = (bf16[4,2,64,256]{3,2,0,1:T(8,128)(2,1)S(1)}, bf16[4,2,64,256]{3,2,0,1:T(8,128)(2,1)}, u32[]{:S(2)}) copy-start(bf16[4,2,64,256]{3,2,0,1:T(8,128)(2,1)} %copy-done.7) | copy-start | bytes 786436
  51.9 12.9 %collective-permute-start.6 = (bf16[1,96,1024]{2,1,0:T(8,128)(2,1)S(1)}, bf16[1,96,1024]{2,1,0:T(8,128)(2,1)S(1)}, u32[]{:S(2)}, u32[]{:S(2)}) collective-permute-start(bf16[1,96,1024]{2,1,0:T(8,128)(2,1)S(1)} %dynamic-slice_convert_fusion.1), channel_id=1, source_target_pairs={{0,384},{96,480},{192,576},{288,672},{384,0},{480,96},{576,192},{6... | collective-permute-start | bytes 589832 | tf_op jit(solution)/shard_map/ppermute | solution.py:67
  64.9 29.3 %collective-permute-start.8 = (bf16[2,1,64,256]{3,2,1,0:T(8,128)(2,1)S(1)}, bf16[2,1,64,256]{3,2,1,0:T(8,128)(2,1)S(1)}, u32[]{:S(2)}, u32[]{:S(2)}) collective-permute-start(bf16[2,1,64,256]{3,2,1,0:T(8,128)(2,1)S(1)} %get-tuple-element.13), channel_id=1, source_target_pairs={{1,0},{2,1},{3,2},{4,3},{5,4},{6,5},{7,6},{8,7},{9,8},{10,9},{11,1... | collective-permute-start | bytes 196616 | tf_op jit(solution)/shard_map/ppermute | solution.py:21
  67.2 27.0 %copy-start.12 = (bf16[3,3,256,256]{3,2,1,0:T(8,128)(2,1)S(1)}, bf16[3,3,256,256]{3,2,1,0:T(8,128)(2,1)}, u32[]{:S(2)}) copy-start(bf16[3,3,256,256]{3,2,1,0:T(8,128)(2,1)} %param.6) | copy-start | bytes 3538948
  68.3 45.0 %all-to-all-start = ((f32[96,1,1024]{2,1,0:T(1,128)}), f32[96,1,1024]{2,1,0:T(1,128)S(1)}, u32[]{:S(2)}, u32[]{:S(2)}) async-start(f32[96,1,1024]{2,1,0:T(1,128)} %copy.30), calls=%async_computation | async-start | bytes 786432 | tf_op jit(solution)/shard_map/all_to_all | solution.py:157
  90.9 5.6 %collective-permute-start.7 = (bf16[2,1,64,256]{3,2,1,0:T(8,128)(2,1)S(1)}, bf16[2,1,64,256]{3,2,1,0:T(8,128)(2,1)S(1)}, u32[]{:S(2)}, u32[]{:S(2)}) collective-permute-start(bf16[2,1,64,256]{3,2,1,0:T(8,128)(2,1)S(1)} %get-tuple-element.12), channel_id=1, source_target_pairs={{0,1},{1,2},{2,3},{3,4},{4,5},{5,6},{6,7},{7,8},{8,9},{9,10},{10,1... | collective-permute-start | bytes 196616 | tf_op jit(solution)/shard_map/ppermute | solution.py:19
  98.5 1.0 copy-start.3
  (1 other events, 0.6 us)

commit v11 on v10

--- a/solution.py
+++ b/solution.py
@@ -139,7 +139,7 @@
     temporal_rows = grad_temporal.reshape(devices, -1)
     packed = jnp.concatenate([spatial_rows, temporal_rows], axis=1)
     packed = packed.reshape(time_shards, row_shards, packed.shape[-1])
-    packed, grad_mid_late = halving_scatter(packed, "tm", grad_mid_late, 2, narrow_from=2)
+    packed, grad_mid_late = halving_scatter(packed, "tm", grad_mid_late, 1, narrow_from=2)
     packed = packed[0]
     grad_ext = extended(grad_mid_late, (("height", 1),), 1)
     grad_pad = jnp.pad(grad_ext, ((0, 0), (0, 0), (1, 1), (0, 0)))

time: 116 us -> 115 us (level)
  waiting for transfers between devices: 33.2 us -> 34.4 us
    all_to_all x1, waiting for transfers between devices: 12.9 us -> 19.2 us  [shards(): packed = lax.all_to_all(packed, 'height', 0, 0, tiled=True)]
    ppermute x2, waiting for transfers between devices: 2.07 us -> 0.01 us  [extended(): lax.ppermute(tail, axis, [(i, (i + 1) % count) for i in range(ends)])]
    ppermute x2, waiting for transfers between devices: 12.8 us -> 11 us  [halving_scatter(): lax.ppermute(send.astype(jnp.bfloat16), axis, route).astype(block.dtype)]
    all_to_all x1, starting transfers between devices: 22.5 us -> 21.2 us  [shards(): packed = lax.all_to_all(packed, 'height', 0, 0, tiled=True)]
    ppermute x1, waiting for transfers between devices: 3.67 us -> 2.4 us  [halving_scatter(): sent = lax.ppermute(send, axis, route)]
    add x3 -> x2, other arithmetic: 2.89 us -> 1.71 us  [halving_scatter(): block = keep + sent]
    unnamed x32 -> x30, local copies, waits for them, and re-layouts: 3.12 us -> 1.96 us
  transfers between devices with their start and end apart: 10 -> 10, of which waited for: 6 -> 5; matrix products, arithmetic and copies ran while one was open for 15% -> 15% of each run, Pallas kernels for 0% -> 0%
where the time goes in v11:
time: 115 us; the launch traced here: 112 us
  starting transfers between devices  48.9 us (43%)
  waiting for transfers between devices  34.4 us (30%)
  matrix products  12.4 us (11%)
  local copies, waits for them, and re-layouts  8.18 us (7%)
  other arithmetic  7.36 us (6%)
  between operations  1.28 us (1%)
    all_to_all x1, starting transfers between devices, shards(): packed = lax.all_to_all(packed, 'height', 0, 0, tiled=True)  21.2 us
    all_to_all x1, waiting for transfers between devices, shards(): packed = lax.all_to_all(packed, 'height', 0, 0, tiled=True)  19.2 us
    ppermute x2, starting transfers between devices, halving_scatter(): lax.ppermute(send.astype(jnp.bfloat16), axis, route).astype(block.dtype)  12.3 us
    ppermute x2, waiting for transfers between devices, halving_scatter(): lax.ppermute(send.astype(jnp.bfloat16), axis, route).astype(block.dtype)  11 us
    ppermute x2, starting transfers between devices, extended(): lax.ppermute(tail, axis, [(i, (i + 1) % count) for i in range(ends)])  6.97 us
    dot_general x15, matrix products, flat_dot(): jnp.dot(left.reshape(-1, left.shape[-1]), weight, preferred_element_type=...  6.64 us
    ppermute x2, starting transfers between devices, shifted(): return lax.ppermute(block, axis, route)  3.84 us
    conv_general_dilated x1, matrix products, shards(): lax.conv_general_dilated(padded, grad_mid, window_strides=(1, 1), padding...  3.59 us
  transfers between devices with their start and end apart: 10, of which 5 were waited for; matrix products, arithmetic and copies ran while one was open for 15% of the time, Pallas kernels for 0%

profile of v11, /device:TPU:6, one launch (start us, length us, event | category | flops | bytes accessed | tf_op | source)
XLA Modules:
  0.0 112.4 jit_solution(6352660779672335605)
XLA Ops:
  1.8 1.2 %fusion.22 = bf16[2,4,64,256]{3,2,1,0:T(8,128)(2,1)S(1)} fusion(bf16[2,4,64,256]{3,2,1,0:T(8,128)(2,1)} %param.4, f32[2,4,64]{2,1,0:T(4,128)S(1)} %fusion.89), kind=kLoop, calls=%fused_computation.47 | loop fusion | flops 917504 | bytes 526336 | tf_op jit(solution)/shard_map/convert_element_type | solution.py:89
  3.0 3.5 %collective-permute-start = (bf16[2,1,64,256]{3,2,1,0:T(8,128)(2,1)S(1)}, bf16[2,1,64,256]{3,2,1,0:T(8,128)(2,1)S(1)}, u32[]{:S(2)}, u32[]{:S(2)}) collective-permute-start(bf16[2,1,64,256]{3,2,1,0:T(8,128)(2,1)S(1)} %get-tuple-element.14), channel_id=1, source_target_pairs={{0,1},{1,2},{2,3},{3,4},{4,5},{5,6},{6,7},{7,8},{8,9},{9,10},{10,1... | collective-permute-start | bytes 196616 | tf_op jit(solution)/shard_map/ppermute | solution.py:19
  6.5 1.3 %collective-permute-start.1 = (bf16[2,1,64,256]{3,2,1,0:T(8,128)(2,1)S(1)}, bf16[2,1,64,256]{3,2,1,0:T(8,128)(2,1)S(1)}, u32[]{:S(2)}, u32[]{:S(2)}) collective-permute-start(bf16[2,1,64,256]{3,2,1,0:T(8,128)(2,1)S(1)} %get-tuple-element.15), channel_id=1, source_target_pairs={{1,0},{2,1},{3,2},{4,3},{5,4},{6,5},{7,6},{8,7},{9,8},{10,9},{11,1... | collective-permute-start | bytes 196616 | tf_op jit(solution)/shard_map/ppermute | solution.py:21
  7.8 1.9 %collective-permute-start.3 = (bf16[2,4,64,256]{3,2,1,0:T(8,128)(2,1)}, bf16[2,4,64,256]{3,2,1,0:T(8,128)(2,1)S(1)}, u32[]{:S(2)}, u32[]{:S(2)}) collective-permute-start(bf16[2,4,64,256]{3,2,1,0:T(8,128)(2,1)} %param.5), channel_id=1, source_target_pairs={{96,0},{192,96},{288,192},{384,288},{480,384},{576,480},{672,576},... | collective-permute-start | bytes 786440 | tf_op jit(solution)/shard_map/ppermute | solution.py:31
  10.9 1.7 %collective-permute-done.1 = bf16[2,1,64,256]{3,2,1,0:T(8,128)(2,1)S(1)} collective-permute-done((bf16[2,1,64,256]{3,2,1,0:T(8,128)(2,1)S(1)}, bf16[2,1,64,256]{3,2,1,0:T(8,128)(2,1)S(1)}, u32[]{:S(2)}, u32[]{:S(2)}) %collective-permute-start.1) | collective-permute-done | bytes 65568 | tf_op jit(solution)/shard_map/ppermute | solution.py:21
  15.6 1.9 %collective-permute-start.2 = (bf16[2,4,64,256]{3,2,1,0:T(8,128)(2,1)S(1)}, bf16[2,4,64,256]{3,2,1,0:T(8,128)(2,1)S(1)}, u32[]{:S(2)}, u32[]{:S(2)}) collective-permute-start(bf16[2,4,64,256]{3,2,1,0:T(8,128)(2,1)S(1)} %bitcast.134), channel_id=1, source_target_pairs={{0,96},{96,192},{192,288},{288,384},{384,480},{480,576},{576,672},... | collective-permute-start | bytes 786440 | tf_op jit(solution)/shard_map/ppermute | solution.py:31
  18.1 3.6 %fusion.38 = f32[3,3,256,256]{3,2,1,0:T(8,128)} fusion(bf16[2,6,64,256]{3,2,1,0:T(8,128)(2,1)S(1)} %get-tuple-element.10, bf16[2,4,64,256]{3,2,1,0:T(8,128)(2,1)S(1)} %fusion.11), kind=kOutput, calls=%fused_computation.65 | convolution fusion | flops 597688320 | bytes 3014656 | tf_op jit(solution)/shard_map/conv_general_dilated | solution.py:125
  21.7 2.6 %concatenate.29 = f32[4,2,96,768]{3,2,1,0:T(8,128)S(1)} reshape(f32[3,3,256,256]{3,2,1,0:T(8,128)} %fusion.38) | data formatting | bytes 4718592 | tf_op jit(solution)/shard_map/concatenate | solution.py:140
  25.0 1.3 %fusion.96 = f32[3,256,256]{2,1,0:T(8,128)} fusion(bf16[4,256,256]{2,1,0:T(8,128)(2,1)S(1)} %bitcast.139, bf16[2,256,256]{2,1,0:T(8,128)(2,1)S(1)} %bitcast.133), kind=kOutput, calls=%fused_computation.129 | convolution fusion | flops 201326592 | bytes 1572864 | tf_op jit(solution)/shard_map/conv_general_dilated | solution.py:117
  26.3 1.2 %rev.3 = f32[3,256,256]{2,1,0:T(8,128)S(1)} reverse(f32[3,256,256]{2,1,0:T(8,128)} %fusion.96), dimensions={0} | reverse | bytes 1572864 | tf_op jit(solution)/shard_map/rev | solution.py:117
  27.4 1.4 %fusion.1 = f32[4,96,1024]{2,1,0:T(8,128)} fusion(s32[]{:T(128)S(6)} %select_n.46, f32[4,2,96,768]{3,2,1,0:T(8,128)S(1)} %concatenate.29, f32[4,2,96,256]{3,2,1,0:T(8,128)S(1)} %bitcast.129), kind=kLoop, calls=%fused_computation.6 | loop fusion | flops 393216 | bytes 4718596 | tf_op jit(solution)/shard_map/jit(dynamic_index_in_dim)/squeeze | solution.py:64
  28.9 1.9 %collective-permute-start.4 = (f32[4,96,1024]{2,1,0:T(8,128)}, f32[4,96,1024]{2,1,0:T(8,128)}, u32[]{:S(2)}, u32[]{:S(2)}) collective-permute-start(f32[4,96,1024]{2,1,0:T(8,128)} %fusion.1), channel_id=1, source_target_pairs={{0,96},{96,0},{192,288},{288,192},{384,480},{480,384},{576,672},{6... | collective-permute-start | bytes 4718600 | tf_op jit(solution)/shard_map/ppermute | solution.py:69
  30.9 1.2 %fusion.72 = f32[2,4,64,256]{3,2,1,0:T(8,128)S(1)} fusion(bf16[3,256,256]{2,1,0:T(8,128)(2,1)} %param.7, bf16[4,2,64,256]{3,0,2,1:T(4,128)(2,1)} %copy-done.5), kind=kOutput, calls=%fused_computation.102 | convolution fusion | flops 67108864 | bytes 917504 | tf_op jit(solution)/shard_map/dot_general | solution.py:41
  32.1 2.4 %collective-permute-done.4 = f32[4,96,1024]{2,1,0:T(8,128)} collective-permute-done((f32[4,96,1024]{2,1,0:T(8,128)}, f32[4,96,1024]{2,1,0:T(8,128)}, u32[]{:S(2)}, u32[]{:S(2)}) %collective-permute-start.4) | collective-permute-done | bytes 1572896 | tf_op jit(solution)/shard_map/ppermute | solution.py:69
  34.5 1.6 %fusion.4 = f32[4,96,1024]{2,1,0:T(8,128)S(1)} fusion(f32[4,96,1024]{2,1,0:T(8,128)} %collective-permute-done.4, s32[]{:T(128)S(6)} %select_n.45, f32[4,2,96,768]{3,2,1,0:T(8,128)S(1)} %concatenate.29, f32[4,2,96,256]{3,2,1,0:T(8,128)S(1)} %bitcast.130), kind=kLoop, calls=%fused_computation.9 | loop fusion | flops 786432 | bytes 6291460 | tf_op jit(solution)/shard_map/add | solution.py:70
  36.2 3.8 %collective-permute-start.5 = (bf16[2,96,1024]{2,1,0:T(8,128)(2,1)S(1)}, bf16[2,96,1024]{2,1,0:T(8,128)(2,1)S(1)}, u32[]{:S(2)}, u32[]{:S(2)}) collective-permute-start(bf16[2,96,1024]{2,1,0:T(8,128)(2,1)S(1)} %fusion.37), channel_id=1, source_target_pairs={{0,192},{96,288},{192,0},{288,96},{384,576},{480,672},{576,384},{6... | collective-permute-start | bytes 1179656 | tf_op jit(solution)/shard_map/ppermute | solution.py:67
  41.2 8.4 %collective-permute-done.5 = bf16[2,96,1024]{2,1,0:T(8,128)(2,1)S(1)} collective-permute-done((bf16[2,96,1024]{2,1,0:T(8,128)(2,1)S(1)}, bf16[2,96,1024]{2,1,0:T(8,128)(2,1)S(1)}, u32[]{:S(2)}, u32[]{:S(2)}) %collective-permute-start.5) | collective-permute-done | bytes 393248 | tf_op jit(solution)/shard_map/ppermute | solution.py:67
  49.8 3.5 %collective-permute-start.6 = (bf16[2,1,64,256]{3,2,1,0:T(8,128)(2,1)S(1)}, bf16[2,1,64,256]{3,2,1,0:T(8,128)(2,1)S(1)}, u32[]{:S(2)}, u32[]{:S(2)}) collective-permute-start(bf16[2,1,64,256]{3,2,1,0:T(8,128)(2,1)S(1)} %get-tuple-element.12), channel_id=1, source_target_pairs={{0,1},{1,2},{2,3},{3,4},{4,5},{5,6},{6,7},{7,8},{8,9},{9,10},{10,1... | collective-permute-start | bytes 196616 | tf_op jit(solution)/shard_map/ppermute | solution.py:19
  53.2 1.3 %collective-permute-start.7 = (bf16[2,1,64,256]{3,2,1,0:T(8,128)(2,1)S(1)}, bf16[2,1,64,256]{3,2,1,0:T(8,128)(2,1)S(1)}, u32[]{:S(2)}, u32[]{:S(2)}) collective-permute-start(bf16[2,1,64,256]{3,2,1,0:T(8,128)(2,1)S(1)} %get-tuple-element.13), channel_id=1, source_target_pairs={{1,0},{2,1},{3,2},{4,3},{5,4},{6,5},{7,6},{8,7},{9,8},{10,9},{11,1... | collective-permute-start | bytes 196616 | tf_op jit(solution)/shard_map/ppermute | solution.py:21
  54.6 8.5 %collective-permute-start.8 = (bf16[1,96,1024]{2,1,0:T(8,128)(2,1)S(1)}, bf16[1,96,1024]{2,1,0:T(8,128)(2,1)S(1)}, u32[]{:S(2)}, u32[]{:S(2)}) collective-permute-start(bf16[1,96,1024]{2,1,0:T(8,128)(2,1)S(1)} %dynamic-slice_convert_fusion.1), channel_id=1, source_target_pairs={{0,384},{96,480},{192,576},{288,672},{384,0},{480,96},{576,192},{6... | collective-permute-start | bytes 589832 | tf_op jit(solution)/shard_map/ppermute | solution.py:67
  64.9 2.6 %collective-permute-done.8 = bf16[1,96,1024]{2,1,0:T(8,128)(2,1)S(1)} collective-permute-done((bf16[1,96,1024]{2,1,0:T(8,128)(2,1)S(1)}, bf16[1,96,1024]{2,1,0:T(8,128)(2,1)S(1)}, u32[]{:S(2)}, u32[]{:S(2)}) %collective-permute-start.8) | collective-permute-done | bytes 196640 | tf_op jit(solution)/shard_map/ppermute | solution.py:67
  67.6 1.2 %copy.30 = f32[96,1,1024]{2,1,0:T(1,128)} copy(f32[96,1,1024]{2,0,1:T(8,128)S(1)} %add_bitcast_fusion) | data formatting | bytes 786432 | tf_op jit(solution)/shard_map/all_to_all | solution.py:157
  68.7 21.2 %all-to-all-start = ((f32[96,1,1024]{2,1,0:T(1,128)}), f32[96,1,1024]{2,1,0:T(1,128)S(1)}, u32[]{:S(2)}, u32[]{:S(2)}) async-start(f32[96,1,1024]{2,1,0:T(1,128)} %copy.30), calls=%async_computation | async-start | bytes 786432 | tf_op jit(solution)/shard_map/all_to_all | solution.py:157
  92.4 19.2 %all-to-all-done = f32[96,1,1024]{2,1,0:T(1,128)S(1)} async-done(((f32[96,1,1024]{2,1,0:T(1,128)}), f32[96,1,1024]{2,1,0:T(1,128)S(1)}, u32[]{:S(2)}, u32[]{:S(2)}) %all-to-all-start) | async-done | bytes 393248 | tf_op jit(solution)/shard_map/all_to_all | solution.py:157
  (71 shorter events, 12.7 us)
Async XLA Ops:
  0.6 9.1 %copy-start.1 = (bf16[2,4,64,256]{3,2,1,0:T(8,128)(2,1)S(1)}, bf16[2,4,64,256]{3,2,1,0:T(8,128)(2,1)}, u32[]{:S(2)}) copy-start(bf16[2,4,64,256]{3,2,1,0:T(8,128)(2,1)} %param.5) | copy-start | bytes 786436
  3.0 7.9 %collective-permute-start = (bf16[2,1,64,256]{3,2,1,0:T(8,128)(2,1)S(1)}, bf16[2,1,64,256]{3,2,1,0:T(8,128)(2,1)S(1)}, u32[]{:S(2)}, u32[]{:S(2)}) collective-permute-start(bf16[2,1,64,256]{3,2,1,0:T(8,128)(2,1)S(1)} %get-tuple-element.14), channel_id=1, source_target_pairs={{0,1},{1,2},{2,3},{3,4},{4,5},{5,6},{6,7},{7,8},{8,9},{9,10},{10,1... | collective-permute-start | bytes 196616 | tf_op jit(solution)/shard_map/ppermute | solution.py:19
  6.5 6.2 %collective-permute-start.1 = (bf16[2,1,64,256]{3,2,1,0:T(8,128)(2,1)S(1)}, bf16[2,1,64,256]{3,2,1,0:T(8,128)(2,1)S(1)}, u32[]{:S(2)}, u32[]{:S(2)}) collective-permute-start(bf16[2,1,64,256]{3,2,1,0:T(8,128)(2,1)S(1)} %get-tuple-element.15), channel_id=1, source_target_pairs={{1,0},{2,1},{3,2},{4,3},{5,4},{6,5},{7,6},{8,7},{9,8},{10,9},{11,1... | collective-permute-start | bytes 196616 | tf_op jit(solution)/shard_map/ppermute | solution.py:21
  7.8 9.7 %collective-permute-start.3 = (bf16[2,4,64,256]{3,2,1,0:T(8,128)(2,1)}, bf16[2,4,64,256]{3,2,1,0:T(8,128)(2,1)S(1)}, u32[]{:S(2)}, u32[]{:S(2)}) collective-permute-start(bf16[2,4,64,256]{3,2,1,0:T(8,128)(2,1)} %param.5), channel_id=1, source_target_pairs={{96,0},{192,96},{288,192},{384,288},{480,384},{576,480},{672,576},... | collective-permute-start | bytes 786440 | tf_op jit(solution)/shard_map/ppermute | solution.py:31
  13.1 1.3 %copy-start.10 = (bf16[3,3,256,256]{3,2,1,0:T(8,128)(2,1)S(1)}, bf16[3,3,256,256]{3,2,1,0:T(8,128)(2,1)}, u32[]{:S(2)}) copy-start(bf16[3,3,256,256]{3,2,1,0:T(8,128)(2,1)} %param.6) | copy-start | bytes 3538948
  13.1 1.3 %copy-start.13 = (pred[16,9]{0,1:T(8,128)(4,1)S(1)}, pred[16,9]{0,1:T(8,128)(4,1)}, u32[]{:S(2)}) copy-start(pred[16,9]{0,1:T(8,128)(4,1)} %constant.105) | copy-start | bytes 436
  15.3 2.3 %copy-start.8 = (bf16[3,256,256]{2,1,0:T(8,128)(2,1)S(1)}, bf16[3,256,256]{2,1,0:T(8,128)(2,1)}, u32[]{:S(2)}) copy-start(bf16[3,256,256]{2,1,0:T(8,128)(2,1)} %param.7) | copy-start | bytes 1179652
  15.5 2.0 %copy-start.5 = (bf16[4,2,64,256]{3,0,2,1:T(4,128)(2,1)}, bf16[4,2,64,256]{3,0,2,1:T(4,128)(2,1)S(1)}, u32[]{:S(2)}) copy-start(bf16[4,2,64,256]{3,0,2,1:T(4,128)(2,1)S(1)} %slice.126) | copy-start | bytes 786436
  15.6 8.7 %copy-start.6 = (bf16[4,2,64,256]{3,2,0,1:T(8,128)(2,1)}, bf16[4,2,64,256]{3,2,0,1:T(8,128)(2,1)S(1)}, u32[]{:S(2)}) copy-start(bf16[4,2,64,256]{3,2,0,1:T(8,128)(2,1)S(1)} %copy.55) | copy-start | bytes 786436
  15.6 8.7 %collective-permute-start.2 = (bf16[2,4,64,256]{3,2,1,0:T(8,128)(2,1)S(1)}, bf16[2,4,64,256]{3,2,1,0:T(8,128)(2,1)S(1)}, u32[]{:S(2)}, u32[]{:S(2)}) collective-permute-start(bf16[2,4,64,256]{3,2,1,0:T(8,128)(2,1)S(1)} %bitcast.134), channel_id=1, source_target_pairs={{0,96},{96,192},{192,288},{288,384},{384,480},{480,576},{576,672},... | collective-permute-start | bytes 786440 | tf_op jit(solution)/shard_map/ppermute | solution.py:31
  24.3 0.7 copy-start.3
  28.9 5.6 %collective-permute-start.4 = (f32[4,96,1024]{2,1,0:T(8,128)}, f32[4,96,1024]{2,1,0:T(8,128)}, u32[]{:S(2)}, u32[]{:S(2)}) collective-permute-start(f32[4,96,1024]{2,1,0:T(8,128)} %fusion.1), channel_id=1, source_target_pairs={{0,96},{96,0},{192,288},{288,192},{384,480},{480,384},{576,672},{6... | collective-permute-start | bytes 4718600 | tf_op jit(solution)/shard_map/ppermute | solution.py:69
  32.1 7.9 %copy-start.4 = (bf16[2,4,64,256]{3,2,1,0:T(8,128)(2,1)S(1)}, bf16[2,4,64,256]{3,2,1,0:T(8,128)(2,1)}, u32[]{:S(2)}) copy-start(bf16[2,4,64,256]{3,2,1,0:T(8,128)(2,1)} %copy-done.3) | copy-start | bytes 786436
  32.1 7.9 %copy-start.9 = (bf16[3,256,256]{2,1,0:T(8,128)(2,1)S(1)}, bf16[3,256,256]{2,1,0:T(8,128)(2,1)}, u32[]{:S(2)}) copy-start(bf16[3,256,256]{2,1,0:T(8,128)(2,1)} %param.7) | copy-start | bytes 1179652
  36.1 4.1 %copy-start = (bf16[2,4,64,256]{3,2,1,0:T(8,128)(2,1)S(1)}, bf16[2,4,64,256]{3,2,1,0:T(8,128)(2,1)}, u32[]{:S(2)}) copy-start(bf16[2,4,64,256]{3,2,1,0:T(8,128)(2,1)} %param.4) | copy-start | bytes 786436
  36.1 4.1 %copy-start.7 = (bf16[4,2,64,256]{3,2,0,1:T(8,128)(2,1)S(1)}, bf16[4,2,64,256]{3,2,0,1:T(8,128)(2,1)}, u32[]{:S(2)}) copy-start(bf16[4,2,64,256]{3,2,0,1:T(8,128)(2,1)} %copy-done.6) | copy-start | bytes 786436
  36.2 13.4 %collective-permute-start.5 = (bf16[2,96,1024]{2,1,0:T(8,128)(2,1)S(1)}, bf16[2,96,1024]{2,1,0:T(8,128)(2,1)S(1)}, u32[]{:S(2)}, u32[]{:S(2)}) collective-permute-start(bf16[2,96,1024]{2,1,0:T(8,128)(2,1)S(1)} %fusion.37), channel_id=1, source_target_pairs={{0,192},{96,288},{192,0},{288,96},{384,576},{480,672},{576,384},{6... | collective-permute-start | bytes 1179656 | tf_op jit(solution)/shard_map/ppermute | solution.py:67
  41.2 21.9 %copy-start.11 = (bf16[3,3,256,256]{3,2,1,0:T(8,128)(2,1)S(1)}, bf16[3,3,256,256]{3,2,1,0:T(8,128)(2,1)}, u32[]{:S(2)}) copy-start(bf16[3,3,256,256]{3,2,1,0:T(8,128)(2,1)} %param.6) | copy-start | bytes 3538948
  49.8 13.7 %collective-permute-start.6 = (bf16[2,1,64,256]{3,2,1,0:T(8,128)(2,1)S(1)}, bf16[2,1,64,256]{3,2,1,0:T(8,128)(2,1)S(1)}, u32[]{:S(2)}, u32[]{:S(2)}) collective-permute-start(bf16[2,1,64,256]{3,2,1,0:T(8,128)(2,1)S(1)} %get-tuple-element.12), channel_id=1, source_target_pairs={{0,1},{1,2},{2,3},{3,4},{4,5},{5,6},{6,7},{7,8},{8,9},{9,10},{10,1... | collective-permute-start | bytes 196616 | tf_op jit(solution)/shard_map/ppermute | solution.py:19
  53.2 9.9 %collective-permute-start.7 = (bf16[2,1,64,256]{3,2,1,0:T(8,128)(2,1)S(1)}, bf16[2,1,64,256]{3,2,1,0:T(8,128)(2,1)S(1)}, u32[]{:S(2)}, u32[]{:S(2)}) collective-permute-start(bf16[2,1,64,256]{3,2,1,0:T(8,128)(2,1)S(1)} %get-tuple-element.13), channel_id=1, source_target_pairs={{1,0},{2,1},{3,2},{4,3},{5,4},{6,5},{7,6},{8,7},{9,8},{10,9},{11,1... | collective-permute-start | bytes 196616 | tf_op jit(solution)/shard_map/ppermute | solution.py:21
  54.6 12.9 %collective-permute-start.8 = (bf16[1,96,1024]{2,1,0:T(8,128)(2,1)S(1)}, bf16[1,96,1024]{2,1,0:T(8,128)(2,1)S(1)}, u32[]{:S(2)}, u32[]{:S(2)}) collective-permute-start(bf16[1,96,1024]{2,1,0:T(8,128)(2,1)S(1)} %dynamic-slice_convert_fusion.1), channel_id=1, source_target_pairs={{0,384},{96,480},{192,576},{288,672},{384,0},{480,96},{576,192},{6... | collective-permute-start | bytes 589832 | tf_op jit(solution)/shard_map/ppermute | solution.py:67
  68.7 42.9 %all-to-all-start = ((f32[96,1,1024]{2,1,0:T(1,128)}), f32[96,1,1024]{2,1,0:T(1,128)S(1)}, u32[]{:S(2)}, u32[]{:S(2)}) async-start(f32[96,1,1024]{2,1,0:T(1,128)} %copy.30), calls=%async_computation | async-start | bytes 786432 | tf_op jit(solution)/shard_map/all_to_all | solution.py:157
  90.5 1.0 copy-start.2
  111.9 0.6 copy-start.12

commit v12 on v11

--- a/solution.py
+++ b/solution.py
@@ -139,7 +139,7 @@
     temporal_rows = grad_temporal.reshape(devices, -1)
     packed = jnp.concatenate([spatial_rows, temporal_rows], axis=1)
     packed = packed.reshape(time_shards, row_shards, packed.shape[-1])
-    packed, grad_mid_late = halving_scatter(packed, "tm", grad_mid_late, 1, narrow_from=2)
+    packed, grad_mid_late = halving_scatter(packed, "tm", grad_mid_late, 0, narrow_from=2)
     packed = packed[0]
     grad_ext = extended(grad_mid_late, (("height", 1),), 1)
     grad_pad = jnp.pad(grad_ext, ((0, 0), (0, 0), (1, 1), (0, 0)))

time: 115 us -> 114 us (level); the launches traced: 112 us -> 114 us
  matrix products: 12.4 us -> 17.1 us
  waiting for transfers between devices: 34.4 us -> 31.2 us
    dot_general x15, matrix products: 6.64 us -> 11.4 us  [flat_dot(): jnp.dot(left.reshape(-1, left.shape[-1]), weight, preferred_element_type=...]
    ppermute x1, waiting for transfers between devices: 2.4 us -> 0.01 us  [halving_scatter(): sent = lax.ppermute(send, axis, route)]
    all_to_all x1, waiting for transfers between devices: 19.2 us -> 17.3 us  [shards(): packed = lax.all_to_all(packed, 'height', 0, 0, tiled=True)]
    ppermute x2, waiting for transfers between devices: 1.73 us -> 3.06 us  [extended(): lax.ppermute(head, axis, [((i + 1) % count, i) for i in range(ends)])]
  transfers between devices with their start and end apart: 10 -> 10, of which waited for: 5 -> 5; matrix products, arithmetic and copies ran while one was open for 15% -> 19% of each run, Pallas kernels for 0% -> 0%
where the time goes in v12:
time: 114 us
  starting transfers between devices  48.9 us (43%)
  waiting for transfers between devices  31.2 us (27%)
  matrix products  17.1 us (15%)
  local copies, waits for them, and re-layouts  7.76 us (7%)
  other arithmetic  7.46 us (7%)
  between operations  1.27 us (1%)
    all_to_all x1, starting transfers between devices, shards(): packed = lax.all_to_all(packed, 'height', 0, 0, tiled=True)  20.8 us
    all_to_all x1, waiting for transfers between devices, shards(): packed = lax.all_to_all(packed, 'height', 0, 0, tiled=True)  17.3 us
    ppermute x2, starting transfers between devices, halving_scatter(): lax.ppermute(send.astype(jnp.bfloat16), axis, route).astype(block.dtype)  12.8 us
    dot_general x15, matrix products, flat_dot(): jnp.dot(left.reshape(-1, left.shape[-1]), weight, preferred_element_type=...  11.4 us
    ppermute x2, waiting for transfers between devices, halving_scatter(): lax.ppermute(send.astype(jnp.bfloat16), axis, route).astype(block.dtype)  10.8 us
    ppermute x2, starting transfers between devices, extended(): lax.ppermute(tail, axis, [(i, (i + 1) % count) for i in range(ends)])  6.97 us
    ppermute x2, starting transfers between devices, shifted(): return lax.ppermute(block, axis, route)  3.84 us
    conv_general_dilated x1, matrix products, shards(): lax.conv_general_dilated(padded, grad_mid, window_strides=(1, 1), padding...  3.59 us
  transfers between devices with their start and end apart: 10, of which 5 were waited for; matrix products, arithmetic and copies ran while one was open for 19% of the time, Pallas kernels for 0%

profile of v12, /device:TPU:6, one launch (start us, length us, event | category | flops | bytes accessed | tf_op | source)
XLA Modules:
  0.0 113.7 jit_solution(12252439496285017872)
XLA Ops:
  3.0 3.5 %collective-permute-start = (bf16[2,1,64,256]{3,2,1,0:T(8,128)(2,1)S(1)}, bf16[2,1,64,256]{3,2,1,0:T(8,128)(2,1)S(1)}, u32[]{:S(2)}, u32[]{:S(2)}) collective-permute-start(bf16[2,1,64,256]{3,2,1,0:T(8,128)(2,1)S(1)} %get-tuple-element.14), channel_id=1, source_target_pairs={{0,1},{1,2},{2,3},{3,4},{4,5},{5,6},{6,7},{7,8},{8,9},{9,10},{10,1... | collective-permute-start | bytes 196616 | tf_op jit(solution)/shard_map/ppermute | solution.py:19
  6.5 1.3 %collective-permute-start.1 = (bf16[2,1,64,256]{3,2,1,0:T(8,128)(2,1)S(1)}, bf16[2,1,64,256]{3,2,1,0:T(8,128)(2,1)S(1)}, u32[]{:S(2)}, u32[]{:S(2)}) collective-permute-start(bf16[2,1,64,256]{3,2,1,0:T(8,128)(2,1)S(1)} %get-tuple-element.15), channel_id=1, source_target_pairs={{1,0},{2,1},{3,2},{4,3},{5,4},{6,5},{7,6},{8,7},{9,8},{10,9},{11,1... | collective-permute-start | bytes 196616 | tf_op jit(solution)/shard_map/ppermute | solution.py:21
  7.8 1.9 %collective-permute-start.3 = (bf16[2,4,64,256]{3,2,1,0:T(8,128)(2,1)}, bf16[2,4,64,256]{3,2,1,0:T(8,128)(2,1)S(1)}, u32[]{:S(2)}, u32[]{:S(2)}) collective-permute-start(bf16[2,4,64,256]{3,2,1,0:T(8,128)(2,1)} %param.5), channel_id=1, source_target_pairs={{96,0},{192,96},{288,192},{384,288},{480,384},{576,480},{672,576},... | collective-permute-start | bytes 786440 | tf_op jit(solution)/shard_map/ppermute | solution.py:31
  10.9 1.7 %collective-permute-done.1 = bf16[2,1,64,256]{3,2,1,0:T(8,128)(2,1)S(1)} collective-permute-done((bf16[2,1,64,256]{3,2,1,0:T(8,128)(2,1)S(1)}, bf16[2,1,64,256]{3,2,1,0:T(8,128)(2,1)S(1)}, u32[]{:S(2)}, u32[]{:S(2)}) %collective-permute-start.1) | collective-permute-done | bytes 65568 | tf_op jit(solution)/shard_map/ppermute | solution.py:21
  15.6 1.9 %collective-permute-start.2 = (bf16[2,4,64,256]{3,2,1,0:T(8,128)(2,1)S(1)}, bf16[2,4,64,256]{3,2,1,0:T(8,128)(2,1)S(1)}, u32[]{:S(2)}, u32[]{:S(2)}) collective-permute-start(bf16[2,4,64,256]{3,2,1,0:T(8,128)(2,1)S(1)} %bitcast.134), channel_id=1, source_target_pairs={{0,96},{96,192},{192,288},{288,384},{384,480},{480,576},{576,672},... | collective-permute-start | bytes 786440 | tf_op jit(solution)/shard_map/ppermute | solution.py:31
  18.1 3.6 %fusion.38 = f32[3,3,256,256]{3,2,1,0:T(8,128)} fusion(bf16[2,6,64,256]{3,2,1,0:T(8,128)(2,1)S(1)} %get-tuple-element.10, bf16[2,4,64,256]{3,2,1,0:T(8,128)(2,1)S(1)} %fusion.11), kind=kOutput, calls=%fused_computation.65 | convolution fusion | flops 597688320 | bytes 3014656 | tf_op jit(solution)/shard_map/conv_general_dilated | solution.py:125
  21.7 2.6 %concatenate.29 = f32[4,2,96,768]{3,2,1,0:T(8,128)S(1)} reshape(f32[3,3,256,256]{3,2,1,0:T(8,128)} %fusion.38) | data formatting | bytes 4718592 | tf_op jit(solution)/shard_map/concatenate | solution.py:140
  25.0 1.3 %fusion.96 = f32[3,256,256]{2,1,0:T(8,128)} fusion(bf16[4,256,256]{2,1,0:T(8,128)(2,1)S(1)} %bitcast.139, bf16[2,256,256]{2,1,0:T(8,128)(2,1)S(1)} %bitcast.133), kind=kOutput, calls=%fused_computation.129 | convolution fusion | flops 201326592 | bytes 1572864 | tf_op jit(solution)/shard_map/conv_general_dilated | solution.py:117
  27.4 1.4 %fusion.1 = f32[4,96,1024]{2,1,0:T(8,128)} fusion(s32[]{:T(128)S(6)} %select_n.46, f32[4,2,96,768]{3,2,1,0:T(8,128)S(1)} %concatenate.29, f32[4,2,96,256]{3,2,1,0:T(8,128)S(1)} %bitcast.129), kind=kLoop, calls=%fused_computation.6 | loop fusion | flops 393216 | bytes 4718596 | tf_op jit(solution)/shard_map/jit(dynamic_index_in_dim)/squeeze | solution.py:64
  28.9 1.9 %collective-permute-start.4 = (f32[4,96,1024]{2,1,0:T(8,128)}, f32[4,96,1024]{2,1,0:T(8,128)}, u32[]{:S(2)}, u32[]{:S(2)}) collective-permute-start(f32[4,96,1024]{2,1,0:T(8,128)} %fusion.1), channel_id=1, source_target_pairs={{0,96},{96,0},{192,288},{288,192},{384,480},{480,384},{576,672},{6... | collective-permute-start | bytes 4718600 | tf_op jit(solution)/shard_map/ppermute | solution.py:69
  30.9 1.3 %fusion.72 = f32[2,4,64,256]{3,2,1,0:T(8,128)S(1)} fusion(bf16[3,256,256]{2,1,0:T(8,128)(2,1)} %param.7, bf16[4,2,64,256]{3,0,2,1:T(4,128)(2,1)} %copy-done.4), kind=kOutput, calls=%fused_computation.102 | convolution fusion | flops 67108864 | bytes 917504 | tf_op jit(solution)/shard_map/dot_general | solution.py:41
  32.2 1.2 %fusion.66 = f32[2,4,64,256]{3,2,1,0:T(8,128)S(1)} fusion(bf16[2,4,64,256]{3,2,1,0:T(8,128)(2,1)} %copy-done.5, bf16[3,256,256]{2,1,0:T(8,128)(2,1)} %param.7), kind=kOutput, calls=%fused_computation.96 | convolution fusion | flops 67108864 | bytes 917504 | tf_op jit(solution)/shard_map/dot_general | solution.py:41
  33.4 1.9 %fusion.10 = bf16[2,4,64,256]{3,2,1,0:T(8,128)(2,1)} fusion(f32[2,4,64,256]{3,2,1,0:T(8,128)S(1)} %fusion.66, f32[2,4,64,256]{3,2,1,0:T(8,128)S(1)} %fusion.72, bf16[2,4,64,256]{3,2,1,0:T(8,128)(2,1)S(1)} %copy-done, bf16[3,256,256]{2,1,0:T(8,128)(2,1)} %param.7, bf16[2,4,64,256]{3,2,1,0:T(8,128)(2,1)S(1)} %bitcast.136, ...), kind=kOutput, calls=%fused_computation.27 | convolution fusion | flops 68812800 | bytes 2228224 | tf_op jit(solution)/shard_map/dot_general | solution.py:41
  35.3 1.7 %fusion.4 = f32[4,96,1024]{2,1,0:T(8,128)S(1)} fusion(f32[4,96,1024]{2,1,0:T(8,128)} %collective-permute-done.4, s32[]{:T(128)S(6)} %select_n.45, f32[4,2,96,768]{3,2,1,0:T(8,128)S(1)} %concatenate.29, f32[4,2,96,256]{3,2,1,0:T(8,128)S(1)} %bitcast.130), kind=kLoop, calls=%fused_computation.9 | loop fusion | flops 786432 | bytes 6291460 | tf_op jit(solution)/shard_map/add | solution.py:70
  37.0 3.5 %collective-permute-start.5 = (bf16[2,1,64,256]{3,2,1,0:T(8,128)(2,1)S(1)}, bf16[2,1,64,256]{3,2,1,0:T(8,128)(2,1)S(1)}, u32[]{:S(2)}, u32[]{:S(2)}) collective-permute-start(bf16[2,1,64,256]{3,2,1,0:T(8,128)(2,1)S(1)} %get-tuple-element.12), channel_id=1, source_target_pairs={{0,1},{1,2},{2,3},{3,4},{4,5},{5,6},{6,7},{7,8},{8,9},{9,10},{10,1... | collective-permute-start | bytes 196616 | tf_op jit(solution)/shard_map/ppermute | solution.py:19
  40.5 1.3 %collective-permute-start.6 = (bf16[2,1,64,256]{3,2,1,0:T(8,128)(2,1)S(1)}, bf16[2,1,64,256]{3,2,1,0:T(8,128)(2,1)S(1)}, u32[]{:S(2)}, u32[]{:S(2)}) collective-permute-start(bf16[2,1,64,256]{3,2,1,0:T(8,128)(2,1)S(1)} %get-tuple-element.13), channel_id=1, source_target_pairs={{1,0},{2,1},{3,2},{4,3},{5,4},{6,5},{7,6},{8,7},{9,8},{10,9},{11,1... | collective-permute-start | bytes 196616 | tf_op jit(solution)/shard_map/ppermute | solution.py:21
  41.9 4.0 %collective-permute-start.7 = (bf16[2,96,1024]{2,1,0:T(8,128)(2,1)S(1)}, bf16[2,96,1024]{2,1,0:T(8,128)(2,1)S(1)}, u32[]{:S(2)}, u32[]{:S(2)}) collective-permute-start(bf16[2,96,1024]{2,1,0:T(8,128)(2,1)S(1)} %fusion.37), channel_id=1, source_target_pairs={{0,192},{96,288},{192,0},{288,96},{384,576},{480,672},{576,384},{6... | collective-permute-start | bytes 1179656 | tf_op jit(solution)/shard_map/ppermute | solution.py:67
  45.9 1.3 %collective-permute-done.6 = bf16[2,1,64,256]{3,2,1,0:T(8,128)(2,1)S(1)} collective-permute-done((bf16[2,1,64,256]{3,2,1,0:T(8,128)(2,1)S(1)}, bf16[2,1,64,256]{3,2,1,0:T(8,128)(2,1)S(1)}, u32[]{:S(2)}, u32[]{:S(2)}) %collective-permute-start.6) | collective-permute-done | bytes 65568 | tf_op jit(solution)/shard_map/ppermute | solution.py:21
  48.7 6.3 %collective-permute-done.7 = bf16[2,96,1024]{2,1,0:T(8,128)(2,1)S(1)} collective-permute-done((bf16[2,96,1024]{2,1,0:T(8,128)(2,1)S(1)}, bf16[2,96,1024]{2,1,0:T(8,128)(2,1)S(1)}, u32[]{:S(2)}, u32[]{:S(2)}) %collective-permute-start.7) | collective-permute-done | bytes 393248 | tf_op jit(solution)/shard_map/ppermute | solution.py:67
  55.1 8.8 %collective-permute-start.8 = (bf16[1,96,1024]{2,1,0:T(8,128)(2,1)S(1)}, bf16[1,96,1024]{2,1,0:T(8,128)(2,1)S(1)}, u32[]{:S(2)}, u32[]{:S(2)}) collective-permute-start(bf16[1,96,1024]{2,1,0:T(8,128)(2,1)S(1)} %dynamic-slice_convert_fusion.1), channel_id=1, source_target_pairs={{0,384},{96,480},{192,576},{288,672},{384,0},{480,96},{576,192},{6... | collective-permute-start | bytes 589832 | tf_op jit(solution)/shard_map/ppermute | solution.py:67
  64.2 4.5 %collective-permute-done.8 = bf16[1,96,1024]{2,1,0:T(8,128)(2,1)S(1)} collective-permute-done((bf16[1,96,1024]{2,1,0:T(8,128)(2,1)S(1)}, bf16[1,96,1024]{2,1,0:T(8,128)(2,1)S(1)}, u32[]{:S(2)}, u32[]{:S(2)}) %collective-permute-start.8) | collective-permute-done | bytes 196640 | tf_op jit(solution)/shard_map/ppermute | solution.py:67
  69.9 20.8 %all-to-all-start = ((f32[96,1,1024]{2,1,0:T(1,128)}), f32[96,1,1024]{2,1,0:T(1,128)S(1)}, u32[]{:S(2)}, u32[]{:S(2)}) async-start(f32[96,1,1024]{2,1,0:T(1,128)} %copy.30), calls=%async_computation | async-start | bytes 786432 | tf_op jit(solution)/shard_map/all_to_all | solution.py:157
  93.1 1.4 %fusion.28 = (f32[2,4,64]{2,1,0:T(4,128)S(1)}, f32[2,4,64,256]{3,2,1,0:T(8,128)S(1)}) fusion(bf16[2,4,64,256]{3,2,1,0:T(8,128)(2,1)S(1)} %copy-done.1, f32[2,4,64]{2,1,0:T(4,128)S(1)} %fusion.89, f32[2,4,64,256]{3,2,1,0:T(8,128)S(1)} %fusion.47, f32[2,4,64,256]{3,2,1,0:T(8,128)S(1)} %convolution_add_fusion.3, bf16[3,3,256,256]{3,2,1,0:T(8,128)(2,1)} %param.6, ...), kind=kOutput, calls=%fused_computation.53 | convolution fusion | flops 69729792 | bytes 2297856 | tf_op jit(solution)/shard_map/dot_general | solution.py:41
  95.5 17.3 %all-to-all-done = f32[96,1,1024]{2,1,0:T(1,128)S(1)} async-done(((f32[96,1,1024]{2,1,0:T(1,128)}), f32[96,1,1024]{2,1,0:T(1,128)S(1)}, u32[]{:S(2)}, u32[]{:S(2)}) %all-to-all-start) | async-done | bytes 393248 | tf_op jit(solution)/shard_map/all_to_all | solution.py:157
  (71 shorter events, 16.0 us)
Async XLA Ops:
  0.6 9.1 %copy-start.2 = (bf16[2,4,64,256]{3,2,1,0:T(8,128)(2,1)S(1)}, bf16[2,4,64,256]{3,2,1,0:T(8,128)(2,1)}, u32[]{:S(2)}) copy-start(bf16[2,4,64,256]{3,2,1,0:T(8,128)(2,1)} %param.5) | copy-start | bytes 786436
  3.0 7.9 %collective-permute-start = (bf16[2,1,64,256]{3,2,1,0:T(8,128)(2,1)S(1)}, bf16[2,1,64,256]{3,2,1,0:T(8,128)(2,1)S(1)}, u32[]{:S(2)}, u32[]{:S(2)}) collective-permute-start(bf16[2,1,64,256]{3,2,1,0:T(8,128)(2,1)S(1)} %get-tuple-element.14), channel_id=1, source_target_pairs={{0,1},{1,2},{2,3},{3,4},{4,5},{5,6},{6,7},{7,8},{8,9},{9,10},{10,1... | collective-permute-start | bytes 196616 | tf_op jit(solution)/shard_map/ppermute | solution.py:19
  6.5 6.2 %collective-permute-start.1 = (bf16[2,1,64,256]{3,2,1,0:T(8,128)(2,1)S(1)}, bf16[2,1,64,256]{3,2,1,0:T(8,128)(2,1)S(1)}, u32[]{:S(2)}, u32[]{:S(2)}) collective-permute-start(bf16[2,1,64,256]{3,2,1,0:T(8,128)(2,1)S(1)} %get-tuple-element.15), channel_id=1, source_target_pairs={{1,0},{2,1},{3,2},{4,3},{5,4},{6,5},{7,6},{8,7},{9,8},{10,9},{11,1... | collective-permute-start | bytes 196616 | tf_op jit(solution)/shard_map/ppermute | solution.py:21
  7.8 9.7 %collective-permute-start.3 = (bf16[2,4,64,256]{3,2,1,0:T(8,128)(2,1)}, bf16[2,4,64,256]{3,2,1,0:T(8,128)(2,1)S(1)}, u32[]{:S(2)}, u32[]{:S(2)}) collective-permute-start(bf16[2,4,64,256]{3,2,1,0:T(8,128)(2,1)} %param.5), channel_id=1, source_target_pairs={{96,0},{192,96},{288,192},{384,288},{480,384},{576,480},{672,576},... | collective-permute-start | bytes 786440 | tf_op jit(solution)/shard_map/ppermute | solution.py:31
  13.1 1.3 %copy-start.10 = (bf16[3,3,256,256]{3,2,1,0:T(8,128)(2,1)S(1)}, bf16[3,3,256,256]{3,2,1,0:T(8,128)(2,1)}, u32[]{:S(2)}) copy-start(bf16[3,3,256,256]{3,2,1,0:T(8,128)(2,1)} %param.6) | copy-start | bytes 3538948
  13.1 1.3 %copy-start.13 = (pred[16,9]{0,1:T(8,128)(4,1)S(1)}, pred[16,9]{0,1:T(8,128)(4,1)}, u32[]{:S(2)}) copy-start(pred[16,9]{0,1:T(8,128)(4,1)} %constant.105) | copy-start | bytes 436
  15.3 2.3 %copy-start.9 = (bf16[3,256,256]{2,1,0:T(8,128)(2,1)S(1)}, bf16[3,256,256]{2,1,0:T(8,128)(2,1)}, u32[]{:S(2)}) copy-start(bf16[3,256,256]{2,1,0:T(8,128)(2,1)} %param.7) | copy-start | bytes 1179652
  15.5 2.0 %copy-start.4 = (bf16[4,2,64,256]{3,0,2,1:T(4,128)(2,1)}, bf16[4,2,64,256]{3,0,2,1:T(4,128)(2,1)S(1)}, u32[]{:S(2)}) copy-start(bf16[4,2,64,256]{3,0,2,1:T(4,128)(2,1)S(1)} %slice.126) | copy-start | bytes 786436
  15.6 8.7 %copy-start.7 = (bf16[4,2,64,256]{3,2,0,1:T(8,128)(2,1)}, bf16[4,2,64,256]{3,2,0,1:T(8,128)(2,1)S(1)}, u32[]{:S(2)}) copy-start(bf16[4,2,64,256]{3,2,0,1:T(8,128)(2,1)S(1)} %copy.55) | copy-start | bytes 786436
  15.6 8.7 %collective-permute-start.2 = (bf16[2,4,64,256]{3,2,1,0:T(8,128)(2,1)S(1)}, bf16[2,4,64,256]{3,2,1,0:T(8,128)(2,1)S(1)}, u32[]{:S(2)}, u32[]{:S(2)}) collective-permute-start(bf16[2,4,64,256]{3,2,1,0:T(8,128)(2,1)S(1)} %bitcast.134), channel_id=1, source_target_pairs={{0,96},{96,192},{192,288},{288,384},{384,480},{480,576},{576,672},... | collective-permute-start | bytes 786440 | tf_op jit(solution)/shard_map/ppermute | solution.py:31
  24.3 0.7 copy-start.5
  28.9 6.4 %collective-permute-start.4 = (f32[4,96,1024]{2,1,0:T(8,128)}, f32[4,96,1024]{2,1,0:T(8,128)}, u32[]{:S(2)}, u32[]{:S(2)}) collective-permute-start(f32[4,96,1024]{2,1,0:T(8,128)} %fusion.1), channel_id=1, source_target_pairs={{0,96},{96,0},{192,288},{288,192},{384,480},{480,384},{576,672},{6... | collective-permute-start | bytes 4718600 | tf_op jit(solution)/shard_map/ppermute | solution.py:69
  30.9 2.5 %copy-start = (bf16[2,4,64,256]{3,2,1,0:T(8,128)(2,1)S(1)}, bf16[2,4,64,256]{3,2,1,0:T(8,128)(2,1)}, u32[]{:S(2)}) copy-start(bf16[2,4,64,256]{3,2,1,0:T(8,128)(2,1)} %param.4) | copy-start | bytes 786436
  30.9 2.5 %copy-start.6 = (bf16[2,4,64,256]{3,2,1,0:T(8,128)(2,1)S(1)}, bf16[2,4,64,256]{3,2,1,0:T(8,128)(2,1)}, u32[]{:S(2)}) copy-start(bf16[2,4,64,256]{3,2,1,0:T(8,128)(2,1)} %copy-done.5) | copy-start | bytes 786436
  30.9 2.5 %copy-start.8 = (bf16[4,2,64,256]{3,2,0,1:T(8,128)(2,1)S(1)}, bf16[4,2,64,256]{3,2,0,1:T(8,128)(2,1)}, u32[]{:S(2)}) copy-start(bf16[4,2,64,256]{3,2,0,1:T(8,128)(2,1)} %copy-done.7) | copy-start | bytes 786436
  35.3 11.9 %copy-start.11 = (bf16[3,3,256,256]{3,2,1,0:T(8,128)(2,1)S(1)}, bf16[3,3,256,256]{3,2,1,0:T(8,128)(2,1)}, u32[]{:S(2)}) copy-start(bf16[3,3,256,256]{3,2,1,0:T(8,128)(2,1)} %param.6) | copy-start | bytes 3538948
  37.0 10.5 %collective-permute-start.5 = (bf16[2,1,64,256]{3,2,1,0:T(8,128)(2,1)S(1)}, bf16[2,1,64,256]{3,2,1,0:T(8,128)(2,1)S(1)}, u32[]{:S(2)}, u32[]{:S(2)}) collective-permute-start(bf16[2,1,64,256]{3,2,1,0:T(8,128)(2,1)S(1)} %get-tuple-element.12), channel_id=1, source_target_pairs={{0,1},{1,2},{2,3},{3,4},{4,5},{5,6},{6,7},{7,8},{8,9},{9,10},{10,1... | collective-permute-start | bytes 196616 | tf_op jit(solution)/shard_map/ppermute | solution.py:19
  40.5 6.7 %collective-permute-start.6 = (bf16[2,1,64,256]{3,2,1,0:T(8,128)(2,1)S(1)}, bf16[2,1,64,256]{3,2,1,0:T(8,128)(2,1)S(1)}, u32[]{:S(2)}, u32[]{:S(2)}) collective-permute-start(bf16[2,1,64,256]{3,2,1,0:T(8,128)(2,1)S(1)} %get-tuple-element.13), channel_id=1, source_target_pairs={{1,0},{2,1},{3,2},{4,3},{5,4},{6,5},{7,6},{8,7},{9,8},{10,9},{11,1... | collective-permute-start | bytes 196616 | tf_op jit(solution)/shard_map/ppermute | solution.py:21
  41.9 13.1 %collective-permute-start.7 = (bf16[2,96,1024]{2,1,0:T(8,128)(2,1)S(1)}, bf16[2,96,1024]{2,1,0:T(8,128)(2,1)S(1)}, u32[]{:S(2)}, u32[]{:S(2)}) collective-permute-start(bf16[2,96,1024]{2,1,0:T(8,128)(2,1)S(1)} %fusion.37), channel_id=1, source_target_pairs={{0,192},{96,288},{192,0},{288,96},{384,576},{480,672},{576,384},{6... | collective-permute-start | bytes 1179656 | tf_op jit(solution)/shard_map/ppermute | solution.py:67
  55.1 13.5 %collective-permute-start.8 = (bf16[1,96,1024]{2,1,0:T(8,128)(2,1)S(1)}, bf16[1,96,1024]{2,1,0:T(8,128)(2,1)S(1)}, u32[]{:S(2)}, u32[]{:S(2)}) collective-permute-start(bf16[1,96,1024]{2,1,0:T(8,128)(2,1)S(1)} %dynamic-slice_convert_fusion.1), channel_id=1, source_target_pairs={{0,384},{96,480},{192,576},{288,672},{384,0},{480,96},{576,192},{6... | collective-permute-start | bytes 589832 | tf_op jit(solution)/shard_map/ppermute | solution.py:67
  69.9 43.0 %all-to-all-start = ((f32[96,1,1024]{2,1,0:T(1,128)}), f32[96,1,1024]{2,1,0:T(1,128)S(1)}, u32[]{:S(2)}, u32[]{:S(2)}) async-start(f32[96,1,1024]{2,1,0:T(1,128)} %copy.30), calls=%async_computation | async-start | bytes 786432 | tf_op jit(solution)/shard_map/all_to_all | solution.py:157
  90.7 2.4 %copy-start.1 = (bf16[2,4,64,256]{3,2,1,0:T(8,128)(2,1)S(1)}, bf16[2,4,64,256]{3,2,1,0:T(8,128)(2,1)}, u32[]{:S(2)}) copy-start(bf16[2,4,64,256]{3,2,1,0:T(8,128)(2,1)} %param.4) | copy-start | bytes 786436
  93.1 1.5 %copy-start.3 = (bf16[2,4,64,256]{3,2,1,0:T(8,128)(2,1)S(1)}, bf16[2,4,64,256]{3,2,1,0:T(8,128)(2,1)}, u32[]{:S(2)}) copy-start(bf16[2,4,64,256]{3,2,1,0:T(8,128)(2,1)} %param.5) | copy-start | bytes 786436
  113.1 0.6 copy-start.12

commit v13 on v12

--- a/solution.py
+++ b/solution.py
@@ -143,15 +143,14 @@
     packed = packed[0]
     grad_ext = extended(grad_mid_late, (("height", 1),), 1)
     grad_pad = jnp.pad(grad_ext, ((0, 0), (0, 0), (1, 1), (0, 0)))
-    grad_act = jnp.zeros(clip.shape, jnp.float32)
-    for tap_row in range(3):
-        for tap_col in range(3):
-            grad_act = grad_act + flat_dot(
-                grad_pad[
-                    :, 2 - tap_row : 2 - tap_row + row_count, 2 - tap_col : 2 - tap_col + col_count
-                ],
-                spatial_weight[tap_row, tap_col].T,
-            )
+    grad_act = lax.conv_general_dilated(
+        grad_pad,
+        jnp.swapaxes(spatial_weight[::-1, ::-1], 2, 3),
+        window_strides=(1, 1),
+        padding="VALID",
+        dimension_numbers=("NHWC", "HWIO", "NHWC"),
+        preferred_element_type=jnp.float32,
+    )
     unused, pullback = jax.vjp(activate, clip_wide)
     grad_clip = (cotangent.astype(jnp.float32) + pullback(grad_act)[0]).astype(jnp.bfloat16)
     packed = lax.all_to_all(packed, "height", 0, 0, tiled=True)

time: 114 us -> 114 us (level)
  matrix products: 17.1 us -> 13.7 us
  other arithmetic: 7.46 us -> 10.6 us
  local copies, waits for them, and re-layouts: 7.76 us -> 10.3 us
  waiting for transfers between devices: 31.2 us -> 28.8 us
    dot_general x15 -> x6, matrix products: 11.4 us -> 6.06 us  [flat_dot(): jnp.dot(left.reshape(-1, left.shape[-1]), weight, preferred_element_type=...]
    ppermute x2, waiting for transfers between devices: 10.8 us -> 6.52 us  [halving_scatter(): lax.ppermute(send.astype(jnp.bfloat16), axis, route).astype(block.dtype)]
    ppermute x1, waiting for transfers between devices: 0.01 us -> 2.41 us  [halving_scatter(): sent = lax.ppermute(send, axis, route)]
    ppermute x2, waiting for transfers between devices: 3.06 us -> 1.66 us  [extended(): lax.ppermute(head, axis, [((i + 1) % count, i) for i in range(ends)])]
    unnamed x30 -> x25, local copies, waits for them, and re-layouts: 1.54 us -> 2.38 us
  transfers between devices with their start and end apart: 10 -> 10, of which waited for: 5 -> 4; matrix products, arithmetic and copies ran while one was open for 19% -> 18% of each run, Pallas kernels for 0% -> 0%
where the time goes in v13:
time: 114 us; the launch traced here: 113 us
  starting transfers between devices  48.6 us (43%)
  waiting for transfers between devices  28.8 us (25%)
  matrix products  13.7 us (12%)
  other arithmetic  10.6 us (9%)
  local copies, waits for them, and re-layouts  10.3 us (9%)
  between operations  1.24 us (1%)
    all_to_all x1, starting transfers between devices, shards(): packed = lax.all_to_all(packed, 'height', 0, 0, tiled=True)  20.3 us
    all_to_all x1, waiting for transfers between devices, shards(): packed = lax.all_to_all(packed, 'height', 0, 0, tiled=True)  18.2 us
    ppermute x2, starting transfers between devices, halving_scatter(): lax.ppermute(send.astype(jnp.bfloat16), axis, route).astype(block.dtype)  12.4 us
    ppermute x2, starting transfers between devices, extended(): lax.ppermute(tail, axis, [(i, (i + 1) % count) for i in range(ends)])  7.51 us
    ppermute x2, waiting for transfers between devices, halving_scatter(): lax.ppermute(send.astype(jnp.bfloat16), axis, route).astype(block.dtype)  6.52 us
    dot_general x6, matrix products, flat_dot(): jnp.dot(left.reshape(-1, left.shape[-1]), weight, preferred_element_type=...  6.06 us
    ppermute x2, starting transfers between devices, shifted(): return lax.ppermute(block, axis, route)  3.83 us
    conv_general_dilated x1, matrix products, shards(): lax.conv_general_dilated(padded, grad_mid, window_strides=(1, 1), padding...  3.63 us
  transfers between devices with their start and end apart: 10, of which 4 were waited for; matrix products, arithmetic and copies ran while one was open for 18% of the time, Pallas kernels for 0%

profile of v13, /device:TPU:6, one launch (start us, length us, event | category | flops | bytes accessed | tf_op | source)
XLA Modules:
  0.0 113.2 jit_solution(1639037507632501700)
XLA Ops:
  0.6 1.2 %fusion.30 = f32[2,4,64]{2,1,0:T(4,128)S(1)} fusion(bf16[2,4,64,256]{3,2,1,0:T(8,128)(2,1)} %param.4), kind=kLoop, calls=%fused_computation.47 | loop fusion | flops 392704 | bytes 264192 | tf_op jit(solution)/shard_map/reduce_sum | solution.py:35
  3.0 3.5 %collective-permute-start = (bf16[2,1,64,256]{3,2,1,0:T(8,128)(2,1)S(1)}, bf16[2,1,64,256]{3,2,1,0:T(8,128)(2,1)S(1)}, u32[]{:S(2)}, u32[]{:S(2)}) collective-permute-start(bf16[2,1,64,256]{3,2,1,0:T(8,128)(2,1)S(1)} %get-tuple-element.14), channel_id=1, source_target_pairs={{0,1},{1,2},{2,3},{3,4},{4,5},{5,6},{6,7},{7,8},{8,9},{9,10},{10,1... | collective-permute-start | bytes 196616 | tf_op jit(solution)/shard_map/ppermute | solution.py:19
  6.5 1.3 %collective-permute-start.1 = (bf16[2,1,64,256]{3,2,1,0:T(8,128)(2,1)S(1)}, bf16[2,1,64,256]{3,2,1,0:T(8,128)(2,1)S(1)}, u32[]{:S(2)}, u32[]{:S(2)}) collective-permute-start(bf16[2,1,64,256]{3,2,1,0:T(8,128)(2,1)S(1)} %get-tuple-element.15), channel_id=1, source_target_pairs={{1,0},{2,1},{3,2},{4,3},{5,4},{6,5},{7,6},{8,7},{9,8},{10,9},{11,1... | collective-permute-start | bytes 196616 | tf_op jit(solution)/shard_map/ppermute | solution.py:21
  7.8 1.9 %collective-permute-start.3 = (bf16[2,4,64,256]{3,2,1,0:T(8,128)(2,1)}, bf16[2,4,64,256]{3,2,1,0:T(8,128)(2,1)S(1)}, u32[]{:S(2)}, u32[]{:S(2)}) collective-permute-start(bf16[2,4,64,256]{3,2,1,0:T(8,128)(2,1)} %param.5), channel_id=1, source_target_pairs={{96,0},{192,96},{288,192},{384,288},{480,384},{576,480},{672,576},... | collective-permute-start | bytes 786440 | tf_op jit(solution)/shard_map/ppermute | solution.py:31
  9.8 1.2 %fusion.45 = f32[2,4,64,256]{3,2,1,0:T(8,128)S(1)} fusion(bf16[2,4,64,256]{3,2,1,0:T(8,128)(2,1)} %param.5, bf16[3,256,256]{2,1,0:T(8,128)(2,1)} %param.7), kind=kOutput, calls=%fused_computation.69 | convolution fusion | flops 67108864 | bytes 917504 | tf_op jit(solution)/shard_map/dot_general | solution.py:41
  11.0 1.7 %collective-permute-done.1 = bf16[2,1,64,256]{3,2,1,0:T(8,128)(2,1)S(1)} collective-permute-done((bf16[2,1,64,256]{3,2,1,0:T(8,128)(2,1)S(1)}, bf16[2,1,64,256]{3,2,1,0:T(8,128)(2,1)S(1)}, u32[]{:S(2)}, u32[]{:S(2)}) %collective-permute-start.1) | collective-permute-done | bytes 65568 | tf_op jit(solution)/shard_map/ppermute | solution.py:21
  16.0 1.9 %collective-permute-start.2 = (bf16[2,4,64,256]{3,2,1,0:T(8,128)(2,1)}, bf16[2,4,64,256]{3,2,1,0:T(8,128)(2,1)}, u32[]{:S(2)}, u32[]{:S(2)}) collective-permute-start(bf16[2,4,64,256]{3,2,1,0:T(8,128)(2,1)} %bitcast.77), channel_id=1, source_target_pairs={{0,96},{96,192},{192,288},{288,384},{384,480},{480,576},{576,672},... | collective-permute-start | bytes 786440 | tf_op jit(solution)/shard_map/ppermute | solution.py:31
  19.2 3.6 %fusion.36 = f32[3,3,256,256]{3,2,1,0:T(8,128)} fusion(bf16[2,6,64,256]{3,2,1,0:T(8,128)(2,1)S(1)} %get-tuple-element.10, bf16[2,4,64,256]{3,2,1,0:T(8,128)(2,1)S(1)} %fusion.10), kind=kOutput, calls=%fused_computation.57 | convolution fusion | flops 597688320 | bytes 3014656 | tf_op jit(solution)/shard_map/conv_general_dilated | solution.py:125
  22.9 2.6 %concatenate.23 = f32[4,2,96,768]{3,2,1,0:T(8,128)S(1)} reshape(f32[3,3,256,256]{3,2,1,0:T(8,128)} %fusion.36) | data formatting | bytes 4718592 | tf_op jit(solution)/shard_map/concatenate | solution.py:140
  26.5 2.3 %fusion.60 = f32[3,256,256]{2,1,0:T(8,128)} fusion(bf16[4,256,256]{2,1,0:T(8,128)(2,1)S(1)} %bitcast.89, bf16[2,256,256]{2,1,0:T(8,128)(2,1)} %bitcast.83), kind=kOutput, calls=%fused_computation.87 | convolution fusion | flops 201326592 | bytes 1572864 | tf_op jit(solution)/shard_map/conv_general_dilated | solution.py:117
  28.8 2.1 %rev.4 = f32[3,256,256]{2,1,0:T(8,128)} reverse(f32[3,256,256]{2,1,0:T(8,128)} %fusion.60), dimensions={0} | reverse | bytes 1572864 | tf_op jit(solution)/shard_map/rev | solution.py:117
  30.9 2.4 %fusion.1 = f32[4,96,1024]{2,1,0:T(8,128)} fusion(s32[]{:T(128)S(6)} %select_n.46, f32[4,2,96,768]{3,2,1,0:T(8,128)S(1)} %concatenate.23, f32[4,2,96,256]{3,2,1,0:T(8,128)} %bitcast.79), kind=kLoop, calls=%fused_computation.5 | loop fusion | flops 393216 | bytes 4718596 | tf_op jit(solution)/shard_map/jit(dynamic_index_in_dim)/squeeze | solution.py:64
  33.2 1.9 %collective-permute-start.4 = (f32[4,96,1024]{2,1,0:T(8,128)}, f32[4,96,1024]{2,1,0:T(8,128)}, u32[]{:S(2)}, u32[]{:S(2)}) collective-permute-start(f32[4,96,1024]{2,1,0:T(8,128)} %fusion.1), channel_id=1, source_target_pairs={{0,96},{96,0},{192,288},{288,192},{384,480},{480,384},{576,672},{6... | collective-permute-start | bytes 4718600 | tf_op jit(solution)/shard_map/ppermute | solution.py:69
  35.2 1.2 %fusion.47 = f32[2,4,64,256]{3,2,1,0:T(8,128)S(1)} fusion(bf16[3,256,256]{2,1,0:T(8,128)(2,1)} %param.7, bf16[4,2,64,256]{3,0,2,1:T(4,128)(2,1)} %copy-done.4), kind=kOutput, calls=%fused_computation.71 | convolution fusion | flops 67108864 | bytes 917504 | tf_op jit(solution)/shard_map/dot_general | solution.py:41
  36.5 2.4 %collective-permute-done.4 = f32[4,96,1024]{2,1,0:T(8,128)} collective-permute-done((f32[4,96,1024]{2,1,0:T(8,128)}, f32[4,96,1024]{2,1,0:T(8,128)}, u32[]{:S(2)}, u32[]{:S(2)}) %collective-permute-start.4) | collective-permute-done | bytes 1572896 | tf_op jit(solution)/shard_map/ppermute | solution.py:69
  38.9 1.7 %fusion.4 = f32[4,96,1024]{2,1,0:T(8,128)S(1)} fusion(f32[4,96,1024]{2,1,0:T(8,128)} %collective-permute-done.4, s32[]{:T(128)S(6)} %select_n.45, f32[4,2,96,768]{3,2,1,0:T(8,128)S(1)} %concatenate.23, f32[4,2,96,256]{3,2,1,0:T(8,128)} %bitcast.80), kind=kLoop, calls=%fused_computation.8 | loop fusion | flops 786432 | bytes 6291460 | tf_op jit(solution)/shard_map/add | solution.py:70
  40.6 3.7 %collective-permute-start.7 = (bf16[2,96,1024]{2,1,0:T(8,128)(2,1)S(1)}, bf16[2,96,1024]{2,1,0:T(8,128)(2,1)S(1)}, u32[]{:S(2)}, u32[]{:S(2)}) collective-permute-start(bf16[2,96,1024]{2,1,0:T(8,128)(2,1)S(1)} %fusion.35), channel_id=1, source_target_pairs={{0,192},{96,288},{192,0},{288,96},{384,576},{480,672},{576,384},{6... | collective-permute-start | bytes 1179656 | tf_op jit(solution)/shard_map/ppermute | solution.py:67
  45.5 1.9 %fusion.9 = bf16[2,4,64,256]{3,2,1,0:T(8,128)(2,1)} fusion(f32[2,4,64,256]{3,2,1,0:T(8,128)S(1)} %fusion.41, f32[2,4,64,256]{3,2,1,0:T(8,128)S(1)} %fusion.47, bf16[2,4,64,256]{3,2,1,0:T(8,128)(2,1)S(1)} %copy-done.1, bf16[3,256,256]{2,1,0:T(8,128)(2,1)S(1)} %copy-done.8, bf16[2,4,64,256]{3,2,1,0:T(8,128)(2,1)} %bitcast.77, ...), kind=kOutput, calls=%fused_computation.17 | convolution fusion | flops 68812800 | bytes 2228224 | tf_op jit(solution)/shard_map/dot_general | solution.py:41
  47.4 6.5 %collective-permute-done.7 = bf16[2,96,1024]{2,1,0:T(8,128)(2,1)S(1)} collective-permute-done((bf16[2,96,1024]{2,1,0:T(8,128)(2,1)S(1)}, bf16[2,96,1024]{2,1,0:T(8,128)(2,1)S(1)}, u32[]{:S(2)}, u32[]{:S(2)}) %collective-permute-start.7) | collective-permute-done | bytes 393248 | tf_op jit(solution)/shard_map/ppermute | solution.py:67
  54.1 8.7 %collective-permute-start.8 = (bf16[1,96,1024]{2,1,0:T(8,128)(2,1)S(1)}, bf16[1,96,1024]{2,1,0:T(8,128)(2,1)S(1)}, u32[]{:S(2)}, u32[]{:S(2)}) collective-permute-start(bf16[1,96,1024]{2,1,0:T(8,128)(2,1)S(1)} %dynamic-slice_convert_fusion.1), channel_id=1, source_target_pairs={{0,384},{96,480},{192,576},{288,672},{384,0},{480,96},{576,192},{6... | collective-permute-start | bytes 589832 | tf_op jit(solution)/shard_map/ppermute | solution.py:67
  62.9 4.0 %collective-permute-start.5 = (bf16[2,1,64,256]{3,2,1,0:T(8,128)(2,1)S(1)}, bf16[2,1,64,256]{3,2,1,0:T(8,128)(2,1)S(1)}, u32[]{:S(2)}, u32[]{:S(2)}) collective-permute-start(bf16[2,1,64,256]{3,2,1,0:T(8,128)(2,1)S(1)} %get-tuple-element.12), channel_id=1, source_target_pairs={{0,1},{1,2},{2,3},{3,4},{4,5},{5,6},{6,7},{7,8},{8,9},{9,10},{10,1... | collective-permute-start | bytes 196616 | tf_op jit(solution)/shard_map/ppermute | solution.py:19
  66.9 1.3 %collective-permute-start.6 = (bf16[2,1,64,256]{3,2,1,0:T(8,128)(2,1)S(1)}, bf16[2,1,64,256]{3,2,1,0:T(8,128)(2,1)S(1)}, u32[]{:S(2)}, u32[]{:S(2)}) collective-permute-start(bf16[2,1,64,256]{3,2,1,0:T(8,128)(2,1)S(1)} %get-tuple-element.13), channel_id=1, source_target_pairs={{1,0},{2,1},{3,2},{4,3},{5,4},{6,5},{7,6},{8,7},{9,8},{10,9},{11,1... | collective-permute-start | bytes 196616 | tf_op jit(solution)/shard_map/ppermute | solution.py:21
  69.4 20.3 %all-to-all-start = ((f32[96,1,1024]{2,1,0:T(1,128)}), f32[96,1,1024]{2,1,0:T(1,128)S(1)}, u32[]{:S(2)}, u32[]{:S(2)}) async-start(f32[96,1,1024]{2,1,0:T(1,128)} %copy.43), calls=%async_computation | async-start | bytes 786432 | tf_op jit(solution)/shard_map/all_to_all | solution.py:156
  94.1 18.2 %all-to-all-done = f32[96,1,1024]{2,1,0:T(1,128)S(1)} async-done(((f32[96,1,1024]{2,1,0:T(1,128)}), f32[96,1,1024]{2,1,0:T(1,128)S(1)}, u32[]{:S(2)}, u32[]{:S(2)}) %all-to-all-start) | async-done | bytes 393248 | tf_op jit(solution)/shard_map/all_to_all | solution.py:156
  (64 shorter events, 14.4 us)
Async XLA Ops:
  0.6 13.4 %copy-start = (bf16[3,3,256,256]{3,2,1,0:T(8,128)(2,1)S(1)}, bf16[3,3,256,256]{3,2,1,0:T(8,128)(2,1)}, u32[]{:S(2)}) copy-start(bf16[3,3,256,256]{3,2,1,0:T(8,128)(2,1)} %param.6) | copy-start | bytes 3538948
  3.0 8.0 %collective-permute-start = (bf16[2,1,64,256]{3,2,1,0:T(8,128)(2,1)S(1)}, bf16[2,1,64,256]{3,2,1,0:T(8,128)(2,1)S(1)}, u32[]{:S(2)}, u32[]{:S(2)}) collective-permute-start(bf16[2,1,64,256]{3,2,1,0:T(8,128)(2,1)S(1)} %get-tuple-element.14), channel_id=1, source_target_pairs={{0,1},{1,2},{2,3},{3,4},{4,5},{5,6},{6,7},{7,8},{8,9},{9,10},{10,1... | collective-permute-start | bytes 196616 | tf_op jit(solution)/shard_map/ppermute | solution.py:19
  6.5 6.2 %collective-permute-start.1 = (bf16[2,1,64,256]{3,2,1,0:T(8,128)(2,1)S(1)}, bf16[2,1,64,256]{3,2,1,0:T(8,128)(2,1)S(1)}, u32[]{:S(2)}, u32[]{:S(2)}) collective-permute-start(bf16[2,1,64,256]{3,2,1,0:T(8,128)(2,1)S(1)} %get-tuple-element.15), channel_id=1, source_target_pairs={{1,0},{2,1},{3,2},{4,3},{5,4},{6,5},{7,6},{8,7},{9,8},{10,9},{11,1... | collective-permute-start | bytes 196616 | tf_op jit(solution)/shard_map/ppermute | solution.py:21
  7.8 10.1 %collective-permute-start.3 = (bf16[2,4,64,256]{3,2,1,0:T(8,128)(2,1)}, bf16[2,4,64,256]{3,2,1,0:T(8,128)(2,1)S(1)}, u32[]{:S(2)}, u32[]{:S(2)}) collective-permute-start(bf16[2,4,64,256]{3,2,1,0:T(8,128)(2,1)} %param.5), channel_id=1, source_target_pairs={{96,0},{192,96},{288,192},{384,288},{480,384},{576,480},{672,576},... | collective-permute-start | bytes 786440 | tf_op jit(solution)/shard_map/ppermute | solution.py:31
  12.8 1.3 %copy-start.10 = (pred[16,9]{0,1:T(8,128)(4,1)S(1)}, pred[16,9]{0,1:T(8,128)(4,1)}, u32[]{:S(2)}) copy-start(pred[16,9]{0,1:T(8,128)(4,1)} %constant.106) | copy-start | bytes 436
  14.9 3.0 %copy-start.7 = (bf16[3,256,256]{2,1,0:T(8,128)(2,1)S(1)}, bf16[3,256,256]{2,1,0:T(8,128)(2,1)}, u32[]{:S(2)}) copy-start(bf16[3,256,256]{2,1,0:T(8,128)(2,1)} %param.7) | copy-start | bytes 1179652
  14.9 3.3 %copy-start.2 = (bf16[2,4,64,256]{3,2,1,0:T(8,128)(2,1)S(1)}, bf16[2,4,64,256]{3,2,1,0:T(8,128)(2,1)}, u32[]{:S(2)}) copy-start(bf16[2,4,64,256]{3,2,1,0:T(8,128)(2,1)} %param.5) | copy-start | bytes 786436
  15.2 3.3 %copy-start.4 = (bf16[4,2,64,256]{3,0,2,1:T(4,128)(2,1)}, bf16[4,2,64,256]{3,0,2,1:T(4,128)(2,1)S(1)}, u32[]{:S(2)}) copy-start(bf16[4,2,64,256]{3,0,2,1:T(4,128)(2,1)S(1)} %slice.54) | copy-start | bytes 786436
  16.0 9.4 %collective-permute-start.2 = (bf16[2,4,64,256]{3,2,1,0:T(8,128)(2,1)}, bf16[2,4,64,256]{3,2,1,0:T(8,128)(2,1)}, u32[]{:S(2)}, u32[]{:S(2)}) collective-permute-start(bf16[2,4,64,256]{3,2,1,0:T(8,128)(2,1)} %bitcast.77), channel_id=1, source_target_pairs={{0,96},{96,192},{192,288},{288,384},{384,480},{480,576},{576,672},... | collective-permute-start | bytes 786440 | tf_op jit(solution)/shard_map/ppermute | solution.py:31
  18.5 0.7 copy-start.5
  33.2 5.6 %collective-permute-start.4 = (f32[4,96,1024]{2,1,0:T(8,128)}, f32[4,96,1024]{2,1,0:T(8,128)}, u32[]{:S(2)}, u32[]{:S(2)}) collective-permute-start(f32[4,96,1024]{2,1,0:T(8,128)} %fusion.1), channel_id=1, source_target_pairs={{0,96},{96,0},{192,288},{288,192},{384,480},{480,384},{576,672},{6... | collective-permute-start | bytes 4718600 | tf_op jit(solution)/shard_map/ppermute | solution.py:69
  36.4 7.9 %copy-start.8 = (bf16[3,256,256]{2,1,0:T(8,128)(2,1)S(1)}, bf16[3,256,256]{2,1,0:T(8,128)(2,1)}, u32[]{:S(2)}) copy-start(bf16[3,256,256]{2,1,0:T(8,128)(2,1)} %param.7) | copy-start | bytes 1179652
  40.6 4.9 %copy-start.1 = (bf16[2,4,64,256]{3,2,1,0:T(8,128)(2,1)S(1)}, bf16[2,4,64,256]{3,2,1,0:T(8,128)(2,1)}, u32[]{:S(2)}) copy-start(bf16[2,4,64,256]{3,2,1,0:T(8,128)(2,1)} %param.4) | copy-start | bytes 786436
  40.6 13.3 %collective-permute-start.7 = (bf16[2,96,1024]{2,1,0:T(8,128)(2,1)S(1)}, bf16[2,96,1024]{2,1,0:T(8,128)(2,1)S(1)}, u32[]{:S(2)}, u32[]{:S(2)}) collective-permute-start(bf16[2,96,1024]{2,1,0:T(8,128)(2,1)S(1)} %fusion.35), channel_id=1, source_target_pairs={{0,192},{96,288},{192,0},{288,96},{384,576},{480,672},{576,384},{6... | collective-permute-start | bytes 1179656 | tf_op jit(solution)/shard_map/ppermute | solution.py:67
  47.4 15.4 %copy-start.6 = (bf16[2,4,64,256]{3,2,1,0:T(8,128)(2,1)S(1)}, bf16[2,4,64,256]{3,2,1,0:T(8,128)(2,1)}, u32[]{:S(2)}) copy-start(bf16[2,4,64,256]{3,2,1,0:T(8,128)(2,1)} %copy-done.5) | copy-start | bytes 786436
  54.1 14.1 %collective-permute-start.8 = (bf16[1,96,1024]{2,1,0:T(8,128)(2,1)S(1)}, bf16[1,96,1024]{2,1,0:T(8,128)(2,1)S(1)}, u32[]{:S(2)}, u32[]{:S(2)}) collective-permute-start(bf16[1,96,1024]{2,1,0:T(8,128)(2,1)S(1)} %dynamic-slice_convert_fusion.1), channel_id=1, source_target_pairs={{0,384},{96,480},{192,576},{288,672},{384,0},{480,96},{576,192},{6... | collective-permute-start | bytes 589832 | tf_op jit(solution)/shard_map/ppermute | solution.py:67
  62.9 26.9 %collective-permute-start.5 = (bf16[2,1,64,256]{3,2,1,0:T(8,128)(2,1)S(1)}, bf16[2,1,64,256]{3,2,1,0:T(8,128)(2,1)S(1)}, u32[]{:S(2)}, u32[]{:S(2)}) collective-permute-start(bf16[2,1,64,256]{3,2,1,0:T(8,128)(2,1)S(1)} %get-tuple-element.12), channel_id=1, source_target_pairs={{0,1},{1,2},{2,3},{3,4},{4,5},{5,6},{6,7},{7,8},{8,9},{9,10},{10,1... | collective-permute-start | bytes 196616 | tf_op jit(solution)/shard_map/ppermute | solution.py:19
  66.9 22.9 %collective-permute-start.6 = (bf16[2,1,64,256]{3,2,1,0:T(8,128)(2,1)S(1)}, bf16[2,1,64,256]{3,2,1,0:T(8,128)(2,1)S(1)}, u32[]{:S(2)}, u32[]{:S(2)}) collective-permute-start(bf16[2,1,64,256]{3,2,1,0:T(8,128)(2,1)S(1)} %get-tuple-element.13), channel_id=1, source_target_pairs={{1,0},{2,1},{3,2},{4,3},{5,4},{6,5},{7,6},{8,7},{9,8},{10,9},{11,1... | collective-permute-start | bytes 196616 | tf_op jit(solution)/shard_map/ppermute | solution.py:21
  69.4 42.9 %all-to-all-start = ((f32[96,1,1024]{2,1,0:T(1,128)}), f32[96,1,1024]{2,1,0:T(1,128)S(1)}, u32[]{:S(2)}, u32[]{:S(2)}) async-start(f32[96,1,1024]{2,1,0:T(1,128)} %copy.43), calls=%async_computation | async-start | bytes 786432 | tf_op jit(solution)/shard_map/all_to_all | solution.py:156
  92.0 1.0 copy-start.3
  112.6 0.6 copy-start.9

commit v14 on v13

--- a/solution.py
+++ b/solution.py
@@ -115,13 +115,13 @@
         )
     grad_mid = grad_wide.astype(jnp.bfloat16)
     grad_temporal = lax.conv_general_dilated(
-        history.reshape(history.shape[0], -1, channels),
-        cotangent.reshape(frame_count, -1, channels),
+        history[::-1].reshape(history.shape[0], -1, channels),
+        cotangent[::-1].reshape(frame_count, -1, channels),
         window_strides=(1,),
         padding="VALID",
         dimension_numbers=("WCN", "WIO", "WNC"),
         preferred_element_type=jnp.float32,
-    )[::-1]
+    )
     grad_spatial = lax.conv_general_dilated(
         padded,
         grad_mid,

time: 114 us -> 114 us (level)
    rev x1 -> x2, local copies, waits for them, and re-layouts: 2.09 us -> 2.61 us  [the longest x1 1.88 us: shards(): history[::-1].reshape(history.shape[0], -1, channels)]
    unnamed x25 -> x27, local copies, waits for them, and re-layouts: 2.38 us -> 2.39 us
  transfers between devices with their start and end apart: 10 -> 10, of which waited for: 4 -> 4; matrix products, arithmetic and copies ran while one was open for 18% -> 19% of each run, Pallas kernels for 0% -> 0%
where the time goes in v14:
time: 114 us; the launch traced here: 113 us
  starting transfers between devices  49.3 us (43%)
  waiting for transfers between devices  28.1 us (25%)
  matrix products  12.9 us (11%)
  local copies, waits for them, and re-layouts  10.8 us (9%)
  other arithmetic  10.4 us (9%)
  between operations  1.23 us (1%)
    all_to_all x1, starting transfers between devices, shards(): packed = lax.all_to_all(packed, 'height', 0, 0, tiled=True)  20.3 us
    all_to_all x1, waiting for transfers between devices, shards(): packed = lax.all_to_all(packed, 'height', 0, 0, tiled=True)  18.2 us
    ppermute x2, starting transfers between devices, halving_scatter(): lax.ppermute(send.astype(jnp.bfloat16), axis, route).astype(block.dtype)  12.6 us
    ppermute x2, starting transfers between devices, extended(): lax.ppermute(tail, axis, [(i, (i + 1) % count) for i in range(ends)])  8.02 us
    ppermute x2, waiting for transfers between devices, halving_scatter(): lax.ppermute(send.astype(jnp.bfloat16), axis, route).astype(block.dtype)  6.5 us
    dot_general x6, matrix products, flat_dot(): jnp.dot(left.reshape(-1, left.shape[-1]), weight, preferred_element_type=...  6.06 us
    ppermute x2, starting transfers between devices, shifted(): return lax.ppermute(block, axis, route)  3.83 us
    conv_general_dilated x1, matrix products, shards(): lax.conv_general_dilated(padded, grad_mid, window_strides=(1, 1), padding...  3.63 us
  transfers between devices with their start and end apart: 10, of which 4 were waited for; matrix products, arithmetic and copies ran while one was open for 19% of the time, Pallas kernels for 0%

profile of v14, /device:TPU:6, one launch (start us, length us, event | category | flops | bytes accessed | tf_op | source)
XLA Modules:
  0.0 112.8 jit_solution(7991779879762459506)
XLA Ops:
  0.7 1.2 %fusion.30 = f32[2,4,64]{2,1,0:T(4,128)S(1)} fusion(bf16[2,4,64,256]{3,2,1,0:T(8,128)(2,1)} %param.4), kind=kLoop, calls=%fused_computation.47 | loop fusion | flops 392704 | bytes 264192 | tf_op jit(solution)/shard_map/reduce_sum | solution.py:35
  3.1 3.5 %collective-permute-start = (bf16[2,1,64,256]{3,2,1,0:T(8,128)(2,1)S(1)}, bf16[2,1,64,256]{3,2,1,0:T(8,128)(2,1)S(1)}, u32[]{:S(2)}, u32[]{:S(2)}) collective-permute-start(bf16[2,1,64,256]{3,2,1,0:T(8,128)(2,1)S(1)} %get-tuple-element.14), channel_id=1, source_target_pairs={{0,1},{1,2},{2,3},{3,4},{4,5},{5,6},{6,7},{7,8},{8,9},{9,10},{10,1... | collective-permute-start | bytes 196616 | tf_op jit(solution)/shard_map/ppermute | solution.py:19
  6.6 1.3 %collective-permute-start.1 = (bf16[2,1,64,256]{3,2,1,0:T(8,128)(2,1)S(1)}, bf16[2,1,64,256]{3,2,1,0:T(8,128)(2,1)S(1)}, u32[]{:S(2)}, u32[]{:S(2)}) collective-permute-start(bf16[2,1,64,256]{3,2,1,0:T(8,128)(2,1)S(1)} %get-tuple-element.15), channel_id=1, source_target_pairs={{1,0},{2,1},{3,2},{4,3},{5,4},{6,5},{7,6},{8,7},{9,8},{10,9},{11,1... | collective-permute-start | bytes 196616 | tf_op jit(solution)/shard_map/ppermute | solution.py:21
  7.9 1.9 %collective-permute-start.3 = (bf16[2,4,64,256]{3,2,1,0:T(8,128)(2,1)}, bf16[2,4,64,256]{3,2,1,0:T(8,128)(2,1)S(1)}, u32[]{:S(2)}, u32[]{:S(2)}) collective-permute-start(bf16[2,4,64,256]{3,2,1,0:T(8,128)(2,1)} %param.5), channel_id=1, source_target_pairs={{96,0},{192,96},{288,192},{384,288},{480,384},{576,480},{672,576},... | collective-permute-start | bytes 786440 | tf_op jit(solution)/shard_map/ppermute | solution.py:31
  9.8 1.2 %fusion.45 = f32[2,4,64,256]{3,2,1,0:T(8,128)S(1)} fusion(bf16[2,4,64,256]{3,2,1,0:T(8,128)(2,1)} %param.5, bf16[3,256,256]{2,1,0:T(8,128)(2,1)} %param.7), kind=kOutput, calls=%fused_computation.69 | convolution fusion | flops 67108864 | bytes 917504 | tf_op jit(solution)/shard_map/dot_general | solution.py:41
  16.0 1.9 %collective-permute-start.2 = (bf16[2,4,64,256]{3,2,1,0:T(8,128)(2,1)}, bf16[2,4,64,256]{3,2,1,0:T(8,128)(2,1)}, u32[]{:S(2)}, u32[]{:S(2)}) collective-permute-start(bf16[2,4,64,256]{3,2,1,0:T(8,128)(2,1)} %bitcast.77), channel_id=1, source_target_pairs={{0,96},{96,192},{192,288},{288,384},{384,480},{480,576},{576,672},... | collective-permute-start | bytes 786440 | tf_op jit(solution)/shard_map/ppermute | solution.py:31
  19.2 3.6 %fusion.36 = f32[3,3,256,256]{3,2,1,0:T(8,128)} fusion(bf16[2,6,64,256]{3,2,1,0:T(8,128)(2,1)S(1)} %get-tuple-element.10, bf16[2,4,64,256]{3,2,1,0:T(8,128)(2,1)S(1)} %fusion.10), kind=kOutput, calls=%fused_computation.57 | convolution fusion | flops 597688320 | bytes 3014656 | tf_op jit(solution)/shard_map/conv_general_dilated | solution.py:125
  22.9 2.6 %concatenate.23 = f32[4,2,96,768]{3,2,1,0:T(8,128)S(1)} reshape(f32[3,3,256,256]{3,2,1,0:T(8,128)} %fusion.36) | data formatting | bytes 4718592 | tf_op jit(solution)/shard_map/concatenate | solution.py:140
  25.4 1.9 %pad_maximum_fusion = bf16[4,4,64,256]{3,2,1,0:T(8,128)(2,1)} fusion(bf16[2,4,64,256]{3,2,1,0:T(8,128)(2,1)} %bitcast.77, bf16[2,4,64,256]{3,2,1,0:T(8,128)(2,1)} %collective-permute-done.2), kind=kLoop, calls=%fused_computation.49 | loop fusion | flops 262144 | bytes 1048576 | tf_op jit(solution)/shard_map/concatenate | solution.py:102
  27.3 1.9 %rev.7 = bf16[4,4,64,256]{3,2,1,0:T(8,128)(2,1)} reverse(bf16[4,4,64,256]{3,2,1,0:T(8,128)(2,1)} %pad_maximum_fusion), dimensions={0} | reverse | bytes 1048576 | tf_op jit(solution)/shard_map/rev | solution.py:118
  29.2 1.5 %fusion.60 = f32[3,256,256]{2,1,0:T(8,128)S(1)} fusion(bf16[4,256,256]{2,1,0:T(8,128)(2,1)} %bitcast.88, bf16[2,256,256]{2,1,0:T(8,128)(2,1)} %bitcast.90), kind=kOutput, calls=%fused_computation.87 | convolution fusion | flops 201326592 | bytes 1572864 | tf_op jit(solution)/shard_map/conv_general_dilated | solution.py:117
  30.7 1.4 %fusion.1 = f32[4,96,1024]{2,1,0:T(8,128)} fusion(s32[]{:T(128)S(6)} %select_n.46, f32[4,2,96,768]{3,2,1,0:T(8,128)S(1)} %concatenate.23, f32[4,2,96,256]{3,2,1,0:T(8,128)S(1)} %bitcast.79), kind=kLoop, calls=%fused_computation.5 | loop fusion | flops 393216 | bytes 4718596 | tf_op jit(solution)/shard_map/jit(dynamic_index_in_dim)/squeeze | solution.py:64
  32.1 1.9 %collective-permute-start.4 = (f32[4,96,1024]{2,1,0:T(8,128)}, f32[4,96,1024]{2,1,0:T(8,128)}, u32[]{:S(2)}, u32[]{:S(2)}) collective-permute-start(f32[4,96,1024]{2,1,0:T(8,128)} %fusion.1), channel_id=1, source_target_pairs={{0,96},{96,0},{192,288},{288,192},{384,480},{480,384},{576,672},{6... | collective-permute-start | bytes 4718600 | tf_op jit(solution)/shard_map/ppermute | solution.py:69
  34.1 1.2 %fusion.47 = f32[2,4,64,256]{3,2,1,0:T(8,128)S(1)} fusion(bf16[3,256,256]{2,1,0:T(8,128)(2,1)} %param.7, bf16[4,2,64,256]{3,0,2,1:T(4,128)(2,1)} %copy-done.5), kind=kOutput, calls=%fused_computation.71 | convolution fusion | flops 67108864 | bytes 917504 | tf_op jit(solution)/shard_map/dot_general | solution.py:41
  35.3 2.4 %collective-permute-done.4 = f32[4,96,1024]{2,1,0:T(8,128)} collective-permute-done((f32[4,96,1024]{2,1,0:T(8,128)}, f32[4,96,1024]{2,1,0:T(8,128)}, u32[]{:S(2)}, u32[]{:S(2)}) %collective-permute-start.4) | collective-permute-done | bytes 1572896 | tf_op jit(solution)/shard_map/ppermute | solution.py:69
  37.7 1.7 %fusion.4 = f32[4,96,1024]{2,1,0:T(8,128)S(1)} fusion(f32[4,96,1024]{2,1,0:T(8,128)} %collective-permute-done.4, s32[]{:T(128)S(6)} %select_n.45, f32[4,2,96,768]{3,2,1,0:T(8,128)S(1)} %concatenate.23, f32[4,2,96,256]{3,2,1,0:T(8,128)} %bitcast.80), kind=kLoop, calls=%fused_computation.8 | loop fusion | flops 786432 | bytes 6291460 | tf_op jit(solution)/shard_map/add | solution.py:70
  39.5 3.7 %collective-permute-start.7 = (bf16[2,96,1024]{2,1,0:T(8,128)(2,1)S(1)}, bf16[2,96,1024]{2,1,0:T(8,128)(2,1)S(1)}, u32[]{:S(2)}, u32[]{:S(2)}) collective-permute-start(bf16[2,96,1024]{2,1,0:T(8,128)(2,1)S(1)} %fusion.35), channel_id=1, source_target_pairs={{0,192},{96,288},{192,0},{288,96},{384,576},{480,672},{576,384},{6... | collective-permute-start | bytes 1179656 | tf_op jit(solution)/shard_map/ppermute | solution.py:67
  44.4 1.9 %fusion.9 = bf16[2,4,64,256]{3,2,1,0:T(8,128)(2,1)} fusion(f32[2,4,64,256]{3,2,1,0:T(8,128)S(1)} %fusion.41, f32[2,4,64,256]{3,2,1,0:T(8,128)S(1)} %fusion.47, bf16[2,4,64,256]{3,2,1,0:T(8,128)(2,1)S(1)} %copy-done.2, bf16[3,256,256]{2,1,0:T(8,128)(2,1)S(1)} %copy-done.9, bf16[2,4,64,256]{3,2,1,0:T(8,128)(2,1)} %bitcast.77, ...), kind=kOutput, calls=%fused_computation.17 | convolution fusion | flops 68812800 | bytes 2228224 | tf_op jit(solution)/shard_map/dot_general | solution.py:41
  46.3 6.5 %collective-permute-done.7 = bf16[2,96,1024]{2,1,0:T(8,128)(2,1)S(1)} collective-permute-done((bf16[2,96,1024]{2,1,0:T(8,128)(2,1)S(1)}, bf16[2,96,1024]{2,1,0:T(8,128)(2,1)S(1)}, u32[]{:S(2)}, u32[]{:S(2)}) %collective-permute-start.7) | collective-permute-done | bytes 393248 | tf_op jit(solution)/shard_map/ppermute | solution.py:67
  53.0 8.9 %collective-permute-start.8 = (bf16[1,96,1024]{2,1,0:T(8,128)(2,1)S(1)}, bf16[1,96,1024]{2,1,0:T(8,128)(2,1)S(1)}, u32[]{:S(2)}, u32[]{:S(2)}) collective-permute-start(bf16[1,96,1024]{2,1,0:T(8,128)(2,1)S(1)} %dynamic-slice_convert_fusion.1), channel_id=1, source_target_pairs={{0,384},{96,480},{192,576},{288,672},{384,0},{480,96},{576,192},{6... | collective-permute-start | bytes 589832 | tf_op jit(solution)/shard_map/ppermute | solution.py:67
  61.9 4.5 %collective-permute-start.5 = (bf16[2,1,64,256]{3,2,1,0:T(8,128)(2,1)S(1)}, bf16[2,1,64,256]{3,2,1,0:T(8,128)(2,1)S(1)}, u32[]{:S(2)}, u32[]{:S(2)}) collective-permute-start(bf16[2,1,64,256]{3,2,1,0:T(8,128)(2,1)S(1)} %get-tuple-element.12), channel_id=1, source_target_pairs={{0,1},{1,2},{2,3},{3,4},{4,5},{5,6},{6,7},{7,8},{8,9},{9,10},{10,1... | collective-permute-start | bytes 196616 | tf_op jit(solution)/shard_map/ppermute | solution.py:19
  66.5 1.3 %collective-permute-start.6 = (bf16[2,1,64,256]{3,2,1,0:T(8,128)(2,1)S(1)}, bf16[2,1,64,256]{3,2,1,0:T(8,128)(2,1)S(1)}, u32[]{:S(2)}, u32[]{:S(2)}) collective-permute-start(bf16[2,1,64,256]{3,2,1,0:T(8,128)(2,1)S(1)} %get-tuple-element.13), channel_id=1, source_target_pairs={{1,0},{2,1},{3,2},{4,3},{5,4},{6,5},{7,6},{8,7},{9,8},{10,9},{11,1... | collective-permute-start | bytes 196616 | tf_op jit(solution)/shard_map/ppermute | solution.py:21
  69.0 20.3 %all-to-all-start = ((f32[96,1,1024]{2,1,0:T(1,128)}), f32[96,1,1024]{2,1,0:T(1,128)S(1)}, u32[]{:S(2)}, u32[]{:S(2)}) async-start(f32[96,1,1024]{2,1,0:T(1,128)} %copy.43), calls=%async_computation | async-start | bytes 786432 | tf_op jit(solution)/shard_map/all_to_all | solution.py:156
  93.7 18.2 %all-to-all-done = f32[96,1,1024]{2,1,0:T(1,128)S(1)} async-done(((f32[96,1,1024]{2,1,0:T(1,128)}), f32[96,1,1024]{2,1,0:T(1,128)S(1)}, u32[]{:S(2)}, u32[]{:S(2)}) %all-to-all-start) | async-done | bytes 393248 | tf_op jit(solution)/shard_map/all_to_all | solution.py:156
  (67 shorter events, 15.0 us)
Async XLA Ops:
  0.6 13.5 %copy-start = (bf16[3,3,256,256]{3,2,1,0:T(8,128)(2,1)S(1)}, bf16[3,3,256,256]{3,2,1,0:T(8,128)(2,1)}, u32[]{:S(2)}) copy-start(bf16[3,3,256,256]{3,2,1,0:T(8,128)(2,1)} %param.6) | copy-start | bytes 3538948
  0.6 10.4 %copy-start.3 = (bf16[2,4,64,256]{3,2,1,0:T(8,128)(2,1)S(1)}, bf16[2,4,64,256]{3,2,1,0:T(8,128)(2,1)}, u32[]{:S(2)}) copy-start(bf16[2,4,64,256]{3,2,1,0:T(8,128)(2,1)} %param.5) | copy-start | bytes 786436
  3.1 8.7 %collective-permute-start = (bf16[2,1,64,256]{3,2,1,0:T(8,128)(2,1)S(1)}, bf16[2,1,64,256]{3,2,1,0:T(8,128)(2,1)S(1)}, u32[]{:S(2)}, u32[]{:S(2)}) collective-permute-start(bf16[2,1,64,256]{3,2,1,0:T(8,128)(2,1)S(1)} %get-tuple-element.14), channel_id=1, source_target_pairs={{0,1},{1,2},{2,3},{3,4},{4,5},{5,6},{6,7},{7,8},{8,9},{9,10},{10,1... | collective-permute-start | bytes 196616 | tf_op jit(solution)/shard_map/ppermute | solution.py:19
  6.6 6.2 %collective-permute-start.1 = (bf16[2,1,64,256]{3,2,1,0:T(8,128)(2,1)S(1)}, bf16[2,1,64,256]{3,2,1,0:T(8,128)(2,1)S(1)}, u32[]{:S(2)}, u32[]{:S(2)}) collective-permute-start(bf16[2,1,64,256]{3,2,1,0:T(8,128)(2,1)S(1)} %get-tuple-element.15), channel_id=1, source_target_pairs={{1,0},{2,1},{3,2},{4,3},{5,4},{6,5},{7,6},{8,7},{9,8},{10,9},{11,1... | collective-permute-start | bytes 196616 | tf_op jit(solution)/shard_map/ppermute | solution.py:21
  7.9 10.1 %collective-permute-start.3 = (bf16[2,4,64,256]{3,2,1,0:T(8,128)(2,1)}, bf16[2,4,64,256]{3,2,1,0:T(8,128)(2,1)S(1)}, u32[]{:S(2)}, u32[]{:S(2)}) collective-permute-start(bf16[2,4,64,256]{3,2,1,0:T(8,128)(2,1)} %param.5), channel_id=1, source_target_pairs={{96,0},{192,96},{288,192},{384,288},{480,384},{576,480},{672,576},... | collective-permute-start | bytes 786440 | tf_op jit(solution)/shard_map/ppermute | solution.py:31
  12.8 1.3 %copy-start.11 = (pred[16,9]{0,1:T(8,128)(4,1)S(1)}, pred[16,9]{0,1:T(8,128)(4,1)}, u32[]{:S(2)}) copy-start(pred[16,9]{0,1:T(8,128)(4,1)} %constant.106) | copy-start | bytes 436
  15.0 3.0 %copy-start.8 = (bf16[3,256,256]{2,1,0:T(8,128)(2,1)S(1)}, bf16[3,256,256]{2,1,0:T(8,128)(2,1)}, u32[]{:S(2)}) copy-start(bf16[3,256,256]{2,1,0:T(8,128)(2,1)} %param.7) | copy-start | bytes 1179652
  15.2 3.3 %copy-start.5 = (bf16[4,2,64,256]{3,0,2,1:T(4,128)(2,1)}, bf16[4,2,64,256]{3,0,2,1:T(4,128)(2,1)S(1)}, u32[]{:S(2)}) copy-start(bf16[4,2,64,256]{3,0,2,1:T(4,128)(2,1)S(1)} %slice.54) | copy-start | bytes 786436
  16.0 9.4 %collective-permute-start.2 = (bf16[2,4,64,256]{3,2,1,0:T(8,128)(2,1)}, bf16[2,4,64,256]{3,2,1,0:T(8,128)(2,1)}, u32[]{:S(2)}, u32[]{:S(2)}) collective-permute-start(bf16[2,4,64,256]{3,2,1,0:T(8,128)(2,1)} %bitcast.77), channel_id=1, source_target_pairs={{0,96},{96,192},{192,288},{288,384},{384,480},{480,576},{576,672},... | collective-permute-start | bytes 786440 | tf_op jit(solution)/shard_map/ppermute | solution.py:31
  18.5 0.7 copy-start.6
  30.7 1.4 %copy-start.1 = (f32[3,256,256]{2,1,0:T(8,128)}, f32[3,256,256]{2,1,0:T(8,128)S(1)}, u32[]{:S(2)}) copy-start(f32[3,256,256]{2,1,0:T(8,128)S(1)} %fusion.60) | copy-start | bytes 2359300
  32.1 5.6 %collective-permute-start.4 = (f32[4,96,1024]{2,1,0:T(8,128)}, f32[4,96,1024]{2,1,0:T(8,128)}, u32[]{:S(2)}, u32[]{:S(2)}) collective-permute-start(f32[4,96,1024]{2,1,0:T(8,128)} %fusion.1), channel_id=1, source_target_pairs={{0,96},{96,0},{192,288},{288,192},{384,480},{480,384},{576,672},{6... | collective-permute-start | bytes 4718600 | tf_op jit(solution)/shard_map/ppermute | solution.py:69
  35.3 7.9 %copy-start.9 = (bf16[3,256,256]{2,1,0:T(8,128)(2,1)S(1)}, bf16[3,256,256]{2,1,0:T(8,128)(2,1)}, u32[]{:S(2)}) copy-start(bf16[3,256,256]{2,1,0:T(8,128)(2,1)} %param.7) | copy-start | bytes 1179652
  39.4 5.0 %copy-start.2 = (bf16[2,4,64,256]{3,2,1,0:T(8,128)(2,1)S(1)}, bf16[2,4,64,256]{3,2,1,0:T(8,128)(2,1)}, u32[]{:S(2)}) copy-start(bf16[2,4,64,256]{3,2,1,0:T(8,128)(2,1)} %param.4) | copy-start | bytes 786436
  39.5 13.3 %collective-permute-start.7 = (bf16[2,96,1024]{2,1,0:T(8,128)(2,1)S(1)}, bf16[2,96,1024]{2,1,0:T(8,128)(2,1)S(1)}, u32[]{:S(2)}, u32[]{:S(2)}) collective-permute-start(bf16[2,96,1024]{2,1,0:T(8,128)(2,1)S(1)} %fusion.35), channel_id=1, source_target_pairs={{0,192},{96,288},{192,0},{288,96},{384,576},{480,672},{576,384},{6... | collective-permute-start | bytes 1179656 | tf_op jit(solution)/shard_map/ppermute | solution.py:67
  46.3 15.6 %copy-start.7 = (bf16[2,4,64,256]{3,2,1,0:T(8,128)(2,1)S(1)}, bf16[2,4,64,256]{3,2,1,0:T(8,128)(2,1)}, u32[]{:S(2)}) copy-start(bf16[2,4,64,256]{3,2,1,0:T(8,128)(2,1)} %copy-done.6) | copy-start | bytes 786436
  53.0 14.8 %collective-permute-start.8 = (bf16[1,96,1024]{2,1,0:T(8,128)(2,1)S(1)}, bf16[1,96,1024]{2,1,0:T(8,128)(2,1)S(1)}, u32[]{:S(2)}, u32[]{:S(2)}) collective-permute-start(bf16[1,96,1024]{2,1,0:T(8,128)(2,1)S(1)} %dynamic-slice_convert_fusion.1), channel_id=1, source_target_pairs={{0,384},{96,480},{192,576},{288,672},{384,0},{480,96},{576,192},{6... | collective-permute-start | bytes 589832 | tf_op jit(solution)/shard_map/ppermute | solution.py:67
  61.9 27.4 %collective-permute-start.5 = (bf16[2,1,64,256]{3,2,1,0:T(8,128)(2,1)S(1)}, bf16[2,1,64,256]{3,2,1,0:T(8,128)(2,1)S(1)}, u32[]{:S(2)}, u32[]{:S(2)}) collective-permute-start(bf16[2,1,64,256]{3,2,1,0:T(8,128)(2,1)S(1)} %get-tuple-element.12), channel_id=1, source_target_pairs={{0,1},{1,2},{2,3},{3,4},{4,5},{5,6},{6,7},{7,8},{8,9},{9,10},{10,1... | collective-permute-start | bytes 196616 | tf_op jit(solution)/shard_map/ppermute | solution.py:19
  66.5 22.9 %collective-permute-start.6 = (bf16[2,1,64,256]{3,2,1,0:T(8,128)(2,1)S(1)}, bf16[2,1,64,256]{3,2,1,0:T(8,128)(2,1)S(1)}, u32[]{:S(2)}, u32[]{:S(2)}) collective-permute-start(bf16[2,1,64,256]{3,2,1,0:T(8,128)(2,1)S(1)} %get-tuple-element.13), channel_id=1, source_target_pairs={{1,0},{2,1},{3,2},{4,3},{5,4},{6,5},{7,6},{8,7},{9,8},{10,9},{11,1... | collective-permute-start | bytes 196616 | tf_op jit(solution)/shard_map/ppermute | solution.py:21
  69.0 42.9 %all-to-all-start = ((f32[96,1,1024]{2,1,0:T(1,128)}), f32[96,1,1024]{2,1,0:T(1,128)S(1)}, u32[]{:S(2)}, u32[]{:S(2)}) async-start(f32[96,1,1024]{2,1,0:T(1,128)} %copy.43), calls=%async_computation | async-start | bytes 786432 | tf_op jit(solution)/shard_map/all_to_all | solution.py:156
  91.6 1.0 copy-start.4
  112.2 0.6 copy-start.10
